TPU v7x, 32 devices: a whole 2x2x4 slice. The times are simulated.
32 devices in a mesh: ctx: 8 (over y, x, core), tp: 4 (over z).
Axes of the slice: x: 2, y: 2, z: 4, core: 2. Of those that a mesh axis runs over, the one named last changes fastest.
Arguments:
- q_in: bfloat16 [1024, 8192], P('ctx', 'tp'), may hold values from -6 to 6
- k_in: bfloat16 [1024, 8192], P('ctx', 'tp'), may hold values from -6 to 6
- v_in: bfloat16 [1024, 8192], P('ctx', 'tp'), may hold values from -6 to 6
- short_filter: float32 [3, 3, 8192], P(None, None, 'tp'), may hold values from -3 to 3
- rate: float32 [8192, 16], P('tp'), may hold values from 9.765625e-05 to 0.05
- residue: float32 [8192, 16], P('tp'), may hold values from -0.3125 to 0.3125
- resid: bfloat16 [1024, 8192], P('ctx', 'tp'), may hold values from -18 to 18, as said below
- gain: float32 [8192], P('tp'), may hold values from 0.5 to 1.5
Outputs:
- normed: bfloat16 [1024, 8192], P('ctx', 'tp')
Inputs may be any that keep to these rules, and one draw needn't show every extreme that they name: `resid`: residual stream entries; channel scales differ across the width.
All inputs are finite; a program needn't handle non-finite values.
Results may differ from a plain program's by a relative error of at most 0.0042.
Values may be sent and summed in bfloat16 or wider, within the bound.
No kernel may reach another device: no remote copies, remote signals or barrier semaphores. Data moves between devices by JAX's collectives and lax.ppermute only.
A program may use at most 64 MiB of HBM per device.

v0:
```python
import jax
import jax.numpy as jnp
from jax import lax
from jax.sharding import PartitionSpec as P

D = 8192


def from_behind(block, axis, distance):
    devices = range(lax.axis_size(axis))
    route = [(i - distance, i) for i in devices if i - distance in devices]
    return lax.ppermute(block, axis, route)


def entering(value, axis, join, neutral):
    count, mine = (lax.axis_size(axis), lax.axis_index(axis))
    pieces = jax.tree.map(lambda part: lax.all_gather(part, axis), value)
    running = jax.tree.map(
        lambda part, zero: jnp.full_like(part, 0) + jnp.asarray(zero, part.dtype), value, neutral
    )

    def lap(position, running):
        longer = join(running, jax.tree.map(lambda part: part[position], pieces))
        return jax.tree.map(lambda new, old: jnp.where(position < mine, new, old), longer, running)

    return lax.fori_loop(0, count - 1, lap, running)


def per_device(q_in, k_in, v_in, short_filter, rate, residue, resid, gain):
    rows, width = q_in.shape
    taps = short_filter.shape[1]
    stacked = jnp.stack([q_in, k_in, v_in])
    tail = stacked[:, rows - (taps - 1) :, :]
    before = from_behind(tail, "ctx", 1)
    padded = jnp.concatenate([before, stacked], axis=1).astype(jnp.float32)
    feats = short_filter[:, 0, None, :] * padded[:, taps - 1 :, :]
    for j in range(1, taps):
        feats = (
            feats + short_filter[:, j, None, :] * padded[:, taps - 1 - j : taps - 1 - j + rows, :]
        )
    q_feat = feats[0]
    gated = (feats[1] * feats[2]).astype(jnp.bfloat16)
    values = lax.optimization_barrier(gated).astype(jnp.float32)
    block = min(128, rows)
    blocks = values.reshape(rows // block, block, width)
    offsets = jnp.arange(block, dtype=jnp.int32).astype(jnp.float32)
    grow = jnp.exp(rate[None, :, :] * offsets[:, None, None])
    fade = jnp.exp(-rate[None, :, :] * offsets[:, None, None])
    enter = jnp.exp(-rate[None, :, :] * (offsets[:, None, None] + 1.0))
    last_fade = jnp.exp(-rate * (block - 1))
    block_decay = jnp.exp(-rate * block)

    def end_step(state, piece):
        summed = jnp.einsum("sc,scm->cm", piece, grow)
        return (state * block_decay + last_fade * summed, None)

    zeros = jnp.zeros(rate.shape, jnp.float32)
    ending, unused = lax.scan(end_step, zeros, blocks)
    power = jnp.exp(-rate * rows)

    def combine(earlier, later):
        return (earlier[0] * later[1] + later[0], earlier[1] * later[1])

    incoming, unused_power = entering(
        (ending, power), "ctx", combine, (zeros, jnp.ones(rate.shape, jnp.float32))
    )

    def main_step(state, piece):
        running = jnp.cumsum(piece[:, :, None] * grow, axis=0) * fade
        states = running + enter * state[None, :, :]
        return (states[-1], jnp.sum(states * residue[None, :, :], axis=2))

    unused_state, outputs = lax.scan(main_step, incoming, blocks)
    mixed = outputs.reshape(rows, width)
    stream = resid.astype(jnp.float32) + q_feat * mixed
    squares = lax.psum(jnp.sum(stream * stream, axis=1), "tp")
    scale = lax.rsqrt(squares / D + 1e-05)
    return (stream * scale[:, None] * gain[None, :]).astype(jnp.bfloat16)


def solution(mesh):
    in_specs = (
        P("ctx", "tp"),
        P("ctx", "tp"),
        P("ctx", "tp"),
        P(None, None, "tp"),
        P("tp", None),
        P("tp", None),
        P("ctx", "tp"),
        P("tp"),
    )
    out_specs = P("ctx", "tp")
    return jax.shard_map(
        per_device, mesh=mesh, in_specs=in_specs, out_specs=out_specs, check_vma=False
    )
```

profile of v0, /device:TPU:0, one launch (start us, length us, event | category | flops | bytes accessed | tf_op | source)
XLA Modules:
  0.0 123.1 jit_solution(8678517536987251884)
XLA Ops:
  6.5 0.0 all-gather.5.cloned.1.call-start
  6.5 0.8 pad_maximum_fusion
  7.4 2.4 %collective-permute-start = (bf16[3,2,2048]{2,1,0:T(2,128)(2,1)S(1)}, bf16[3,2,2048]{2,1,0:T(2,128)(2,1)S(1)}, u32[]{:S(2)}, u32[]{:S(2)}) collective-permute-start(bf16[3,2,2048]{2,1,0:T(2,128)(2,1)S(1)} %pad_maximum_fusion), channel_id=1, source_target_pairs={{0,4},{4,8},{8,12},{12,16},{16,20},{20,24},{24,28},{1,5},{5,9},{9,... | collective-permute-start | bytes 73736 | tf_op jit(solution)/shard_map/ppermute | solution.py:12
  9.8 1.1 fusion.15
  11.0 0.0 collective-permute-done
  11.0 1.8 %maximum_convert_fusion = f32[3,130,2048]{2,1,0:T(8,128)S(1)} fusion(bf16[1,128,2048]{2,1,0:T(8,128)(2,1)} %bitcast.53, bf16[1,128,2048]{2,1,0:T(8,128)(2,1)} %bitcast.55, bf16[1,128,2048]{2,1,0:T(8,128)(2,1)} %bitcast.57, bf16[3,2,2048]{2,1,0:T(2,128)(2,1)S(1)} %collective-permute-done), kind=kLoop, calls=%fused_computation.20 | loop fusion | flops 6389760 | bytes 4792320 | tf_op jit(solution)/shard_map/convert_element_type | solution.py:35
  12.8 0.9 fusion.8
  13.7 0.0 copy-start.2
  13.8 0.1 fusion.13
  13.9 1.1 bitcast_convert_fusion
  15.0 0.0 copy-done.2
  15.0 3.1 %multiply_reduce_fusion = f32[2048,16]{0,1:T(8,128)S(1)} fusion(f32[2048,128]{0,1:T(8,128)S(1)} %get-tuple-element.177, f32[128]{0:T(128)S(1)} %iota_convert_fusion, f32[2048,16]{0,1:T(8,128)S(1)} %copy-done.2), kind=kLoop, calls=%fused_computation.7 | loop fusion | flops 12550144 | bytes 1311232 | tf_op jit(solution)/shard_map/while/body/eval_jaxpr/sc,scm->cm/dot_general | solution.py:54
  18.1 0.8 fusion.14
  18.8 0.0 all-gather.5.cloned.1.call-update
  18.9 0.0 all-gather.7.cloned.1.call-start
  18.9 0.7 all-gather.7.cloned.1.call-update
  19.6 27.0 %all-gather.5.cloned.1.call-done = f32[16384,16]{0,1:T(8,128)} async-done(((f32[2048,16]{0,1:T(8,128)}), f32[16384,16]{0,1:T(8,128)}) %all-gather.5.cloned.1.call-update) | async-done | bytes 1048592 | tf_op jit(solution)/shard_map/all_gather | solution.py:17
  46.7 2.9 %copy.24 = f32[2,8,8,2048]{3,2,1,0:T(8,128)} copy(f32[2,8,8,2048]{3,1,2,0:T(8,128)} %bitcast.58) | data formatting | bytes 2097152
  49.5 22.5 %all-gather.7.cloned.1.call-done = f32[16384,16]{0,1:T(8,128)} async-done(((f32[2048,16]{0,1:T(8,128)}), f32[16384,16]{0,1:T(8,128)}) %all-gather.7.cloned.1.call-update) | async-done | bytes 1048592 | tf_op jit(solution)/shard_map/all_gather | solution.py:17
  72.0 2.8 %copy.25 = f32[2,8,8,2048]{3,2,1,0:T(8,128)} copy(f32[2,8,8,2048]{3,1,2,0:T(8,128)} %bitcast.59) | data formatting | bytes 2097152
  74.8 13.1 %while.9 = (s32[]{:T(128)}, f32[2048,16]{0,1:T(8,128)S(1)}, s32[]{:T(128)}, f32[8,2048,16]{1,0,2:T(8,128)}, f32[8,2048,16]{1,0,2:T(8,128)}, /*index=5*/s32[]{:T(128)}, s32[]{:T(128)}) while((s32[]{:T(128)}, f32[2048,16]{0,1:T(8,128)S(1)}, s32[]{:T(128)}, f32[8,2048,16]{1,0,2:T(8,128)}, f32[8,2048,16]{1,0,2:T(8,128)}, ...), condition=%wide.region_2.3_spmd.clone, body=%wide.region_1.2_spmd.clone.sunk | while | flops 131076 | bytes 1048677 | solution.py:26
  74.8 1.7 %constant_dynamic-slice_fusion.3 = (f32[1,2048,16]{1,0,2:T(1,128)S(1)}, f32[1,2048,16]{1,0,2:T(1,128)S(1)}) fusion(f32[8,2048,16]{1,0,2:T(8,128)} %get-tuple-element.240, s32[]{:T(128)} %get-tuple-element.229, f32[8,2048,16]{1,0,2:T(8,128)} %get-tuple-element.239), kind=kLoop, calls=%fused_computation.5.clone.1 | loop fusion | bytes 524292 | tf_op jit(solution)/shard_map/while/body/eval_jaxpr/dynamic_slice | solution.py:23
  76.6 0.1 fusion.17
  76.7 1.7 %constant_dynamic-slice_fusion.3 = (f32[1,2048,16]{1,0,2:T(1,128)S(1)}, f32[1,2048,16]{1,0,2:T(1,128)S(1)}) fusion(f32[8,2048,16]{1,0,2:T(8,128)} %get-tuple-element.240, s32[]{:T(128)} %get-tuple-element.229, f32[8,2048,16]{1,0,2:T(8,128)} %get-tuple-element.239), kind=kLoop, calls=%fused_computation.5.clone.1 | loop fusion | bytes 524292 | tf_op jit(solution)/shard_map/while/body/eval_jaxpr/dynamic_slice | solution.py:23
  78.4 0.1 fusion.17
  78.5 1.7 %constant_dynamic-slice_fusion.3 = (f32[1,2048,16]{1,0,2:T(1,128)S(1)}, f32[1,2048,16]{1,0,2:T(1,128)S(1)}) fusion(f32[8,2048,16]{1,0,2:T(8,128)} %get-tuple-element.240, s32[]{:T(128)} %get-tuple-element.229, f32[8,2048,16]{1,0,2:T(8,128)} %get-tuple-element.239), kind=kLoop, calls=%fused_computation.5.clone.1 | loop fusion | bytes 524292 | tf_op jit(solution)/shard_map/while/body/eval_jaxpr/dynamic_slice | solution.py:23
  80.3 0.1 fusion.17
  80.4 1.7 %constant_dynamic-slice_fusion.3 = (f32[1,2048,16]{1,0,2:T(1,128)S(1)}, f32[1,2048,16]{1,0,2:T(1,128)S(1)}) fusion(f32[8,2048,16]{1,0,2:T(8,128)} %get-tuple-element.240, s32[]{:T(128)} %get-tuple-element.229, f32[8,2048,16]{1,0,2:T(8,128)} %get-tuple-element.239), kind=kLoop, calls=%fused_computation.5.clone.1 | loop fusion | bytes 524292 | tf_op jit(solution)/shard_map/while/body/eval_jaxpr/dynamic_slice | solution.py:23
  82.2 0.1 fusion.17
  82.3 1.7 %constant_dynamic-slice_fusion.3 = (f32[1,2048,16]{1,0,2:T(1,128)S(1)}, f32[1,2048,16]{1,0,2:T(1,128)S(1)}) fusion(f32[8,2048,16]{1,0,2:T(8,128)} %get-tuple-element.240, s32[]{:T(128)} %get-tuple-element.229, f32[8,2048,16]{1,0,2:T(8,128)} %get-tuple-element.239), kind=kLoop, calls=%fused_computation.5.clone.1 | loop fusion | bytes 524292 | tf_op jit(solution)/shard_map/while/body/eval_jaxpr/dynamic_slice | solution.py:23
  84.0 0.1 fusion.17
  84.2 1.7 %constant_dynamic-slice_fusion.3 = (f32[1,2048,16]{1,0,2:T(1,128)S(1)}, f32[1,2048,16]{1,0,2:T(1,128)S(1)}) fusion(f32[8,2048,16]{1,0,2:T(8,128)} %get-tuple-element.240, s32[]{:T(128)} %get-tuple-element.229, f32[8,2048,16]{1,0,2:T(8,128)} %get-tuple-element.239), kind=kLoop, calls=%fused_computation.5.clone.1 | loop fusion | bytes 524292 | tf_op jit(solution)/shard_map/while/body/eval_jaxpr/dynamic_slice | solution.py:23
  85.9 0.1 fusion.17
  86.0 1.7 %constant_dynamic-slice_fusion.3 = (f32[1,2048,16]{1,0,2:T(1,128)S(1)}, f32[1,2048,16]{1,0,2:T(1,128)S(1)}) fusion(f32[8,2048,16]{1,0,2:T(8,128)} %get-tuple-element.240, s32[]{:T(128)} %get-tuple-element.229, f32[8,2048,16]{1,0,2:T(8,128)} %get-tuple-element.239), kind=kLoop, calls=%fused_computation.5.clone.1 | loop fusion | bytes 524292 | tf_op jit(solution)/shard_map/while/body/eval_jaxpr/dynamic_slice | solution.py:23
  87.8 0.1 fusion.17
  87.9 0.0 copy-start.1
  87.9 0.0 copy-start.3
  87.9 13.0 %multiply_reduce_fusion.1 = f32[128,2048]{1,0:T(8,128)S(1)} fusion(f32[2048,16]{0,1:T(8,128)} %param.15, f32[2048,16]{0,1:T(8,128)S(1)} %get-tuple-element.141, f32[128]{0:T(128)S(1)} %broadcast_add_fusion, f32[2048,16]{0,1:T(8,128)} %get-tuple-element.179, f32[128]{0:T(128)S(1)} %iota_convert_fusion, f32[2048,16]{0,1:T(8,128)} %param.14, ...), kind=kOutput, calls=%fused_computation.8 | output fusion | flops 570163200 | bytes 2622464 | tf_op jit(solution)/shard_map/while/body/eval_jaxpr/jit(cumsum)/reduce_window_sum | solution.py:69
  100.9 0.0 copy-start
  100.9 1.0 copy-done
  101.9 0.0 copy-done.1
  101.9 0.3 multiply_reduce_fusion.2
  102.2 11.7 %psum.7 = f32[128]{0:T(128)S(1)} all-reduce(f32[128]{0:T(128)S(1)} %multiply_reduce_fusion.2), channel_id=1, replica_groups=mesh['ctx'=8,'tp'=4] {'tp'}, use_global_device_ids=true, to_apply=%region_5.6 | all-reduce | flops 128 | bytes 1024 | tf_op jit(solution)/shard_map/psum | solution.py:76
  113.9 0.0 copy-done.3
  113.9 2.4 %multiply_convert_fusion = bf16[128,2048]{1,0:T(8,128)(2,1)} fusion(f32[2048]{0:T(1024)S(1)} %copy-done.3, f32[128]{0:T(128)S(1)} %add_rsqrt_fusion, f32[128,2048]{1,0:T(8,128)} %copy-done, f32[3,128,2048]{2,1,0:T(8,128)S(1)} %fusion.8, bf16[128,2048]{1,0:T(8,128)(2,1)} %param.16), kind=kLoop, calls=%fused_computation.26 | loop fusion | flops 1572864 | bytes 3154432 | tf_op jit(solution)/shard_map/convert_element_type | solution.py:78
  (6 shorter events, 0.1 us)
Async XLA Ops:
  6.5 40.1 %all-gather.5.cloned.1.call-start = ((), (), s32[]{:S(2)}) async-start(), calls=%async_computation | async-start | bytes 1179648 | tf_op jit(solution)/shard_map/all_gather | solution.py:17
  7.4 3.6 %collective-permute-start = (bf16[3,2,2048]{2,1,0:T(2,128)(2,1)S(1)}, bf16[3,2,2048]{2,1,0:T(2,128)(2,1)S(1)}, u32[]{:S(2)}, u32[]{:S(2)}) collective-permute-start(bf16[3,2,2048]{2,1,0:T(2,128)(2,1)S(1)} %pad_maximum_fusion), channel_id=1, source_target_pairs={{0,4},{4,8},{8,12},{12,16},{16,20},{20,24},{24,28},{1,5},{5,9},{9,... | collective-permute-start | bytes 73736 | tf_op jit(solution)/shard_map/ppermute | solution.py:12
  13.7 1.2 %copy-start.2 = (f32[2048,16]{0,1:T(8,128)S(1)}, f32[2048,16]{0,1:T(8,128)}, u32[]{:S(2)}) copy-start(f32[2048,16]{0,1:T(8,128)} %param.14) | copy-start | bytes 393220
  18.9 53.1 %all-gather.7.cloned.1.call-start = ((), (), s32[]{:S(2)}) async-start(), calls=%async_computation.1 | async-start | bytes 1179648 | tf_op jit(solution)/shard_map/all_gather | solution.py:17
  87.9 14.0 %copy-start.1 = (bf16[128,2048]{1,0:T(8,128)(2,1)S(1)}, bf16[128,2048]{1,0:T(8,128)(2,1)}, u32[]{:S(2)}) copy-start(bf16[128,2048]{1,0:T(8,128)(2,1)} %param.16) | copy-start | bytes 1572868
  87.9 26.0 %copy-start.3 = (f32[2048]{0:T(1024)S(1)}, f32[2048]{0:T(1024)}, u32[]{:S(2)}) copy-start(f32[2048]{0:T(1024)} %param.17) | copy-start | bytes 24580
  100.9 1.0 copy-start
Sparse Core Ops, SparseCore 0:
  19.0 27.6 all-gather.4
  48.6 23.3 all-gather.6
where the time goes:
time: 124 us; the launch traced here: 123 us
  waiting for transfers between devices  50.2 us (40%)
  other arithmetic  25 us (20%)
  local copies, waits for them, and re-layouts  20 us (16%)
  between operations  13.5 us (11%)
  blocking collectives  11.7 us (9%)
  starting transfers between devices  2.44 us (2%)
    all_gather x2, waiting for transfers between devices, entering(): pieces = jax.tree.map(lambda part: lax.all_gather(part, axis), value)  49.5 us
    another operation x1, other arithmetic, main_step(): running = jnp.cumsum(piece[:, :, None] * grow, axis=0) * fade  13 us
    dynamic_slice x7, local copies, waits for them, and re-layouts, lap(): longer = join(running, jax.tree.map(lambda part: part[position], pieces))  12.2 us
    psum x1, blocking collectives, per_device(): squares = lax.psum(jnp.sum(stream * stream, axis=1), 'tp')  11.7 us
    unnamed x12, local copies, waits for them, and re-layouts  6.72 us
    dot_general x1, other arithmetic, end_step(): summed = jnp.einsum('sc,scm->cm', piece, grow)  3.11 us
  transfers between devices with their start and end apart: 3, of which 2 were waited for; matrix products, arithmetic and copies ran while one was open for 3% of the time, Pallas kernels for 0%

commit v1 on v0

--- a/solution.py
+++ b/solution.py
@@ -12,18 +12,28 @@
     return lax.ppermute(block, axis, route)
 
 
-def entering(value, axis, join, neutral):
-    count, mine = (lax.axis_size(axis), lax.axis_index(axis))
-    pieces = jax.tree.map(lambda part: lax.all_gather(part, axis), value)
-    running = jax.tree.map(
-        lambda part, zero: jnp.full_like(part, 0) + jnp.asarray(zero, part.dtype), value, neutral
-    )
+def scan_in(ending, rate, rows, axis):
+    count = lax.axis_size(axis)
+    if count == 1:
+        return jnp.zeros_like(ending)
+    incoming = from_behind(ending, axis, 1)
+    if count > 2:
+        incoming = incoming + jnp.exp(-rate * rows) * from_behind(ending, axis, 2)
+    shift = 2
+    while shift < count:
+        incoming = incoming + jnp.exp(-rate * (rows * shift)) * from_behind(incoming, axis, shift)
+        shift *= 2
+    return incoming
 
-    def lap(position, running):
-        longer = join(running, jax.tree.map(lambda part: part[position], pieces))
-        return jax.tree.map(lambda new, old: jnp.where(position < mine, new, old), longer, running)
 
-    return lax.fori_loop(0, count - 1, lap, running)
+def butterfly_sum(value, axis):
+    count = lax.axis_size(axis)
+    assert count & (count - 1) == 0
+    step = 1
+    while step < count:
+        value = value + lax.ppermute(value, axis, [(i, i ^ step) for i in range(count)])
+        step *= 2
+    return value
 
 
 def per_device(q_in, k_in, v_in, short_filter, rate, residue, resid, gain):
@@ -56,14 +66,7 @@
 
     zeros = jnp.zeros(rate.shape, jnp.float32)
     ending, unused = lax.scan(end_step, zeros, blocks)
-    power = jnp.exp(-rate * rows)
-
-    def combine(earlier, later):
-        return (earlier[0] * later[1] + later[0], earlier[1] * later[1])
-
-    incoming, unused_power = entering(
-        (ending, power), "ctx", combine, (zeros, jnp.ones(rate.shape, jnp.float32))
-    )
+    incoming = scan_in(ending, rate, rows, "ctx")
 
     def main_step(state, piece):
         running = jnp.cumsum(piece[:, :, None] * grow, axis=0) * fade
@@ -73,7 +76,7 @@
     unused_state, outputs = lax.scan(main_step, incoming, blocks)
     mixed = outputs.reshape(rows, width)
     stream = resid.astype(jnp.float32) + q_feat * mixed
-    squares = lax.psum(jnp.sum(stream * stream, axis=1), "tp")
+    squares = butterfly_sum(jnp.sum(stream * stream, axis=1), "tp")
     scale = lax.rsqrt(squares / D + 1e-05)
     return (stream * scale[:, None] * gain[None, :]).astype(jnp.bfloat16)
 

time: 124 us -> 61.9 us (0.50)
  waiting for transfers between devices: 50.2 us -> 12 us
  starting transfers between devices: 2.44 us -> 27.1 us
  local copies, waits for them, and re-layouts: 20 us -> 1.73 us
  between operations: 13.5 us -> 0.2 us
  blocking collectives: 11.7 us -> 0 us
  other arithmetic: 25 us -> 20.5 us
    all_gather x2 -> x0, waiting for transfers between devices: 49.5 us -> none  [entering(): pieces = jax.tree.map(lambda part: lax.all_gather(part, axis), value)]
    ppermute x1 -> x5, starting transfers between devices: 2.4 us -> 22.9 us  [from_behind(): return lax.ppermute(block, axis, route)]
    dynamic_slice x7 -> x0, local copies, waits for them, and re-layouts: 12.2 us -> none  [lap(): longer = join(running, jax.tree.map(lambda part: part[position], pieces))]
    psum x1 -> x0, blocking collectives: 11.7 us -> none  [per_device(): squares = lax.psum(jnp.sum(stream * stream, axis=1), 'tp')]
    ppermute x1 -> x5, waiting for transfers between devices: 0.01 us -> 8.18 us  [from_behind(): return lax.ppermute(block, axis, route)]
    unnamed x12 -> x10, local copies, waits for them, and re-layouts: 6.72 us -> 0.61 us
    ppermute x0 -> x2, starting transfers between devices: none -> 4.23 us  [butterfly_sum(): lax.ppermute(value, axis, [(i, i ^ step) for i in range(count)])]
    ppermute x0 -> x2, waiting for transfers between devices: none -> 3.87 us  [butterfly_sum(): lax.ppermute(value, axis, [(i, i ^ step) for i in range(count)])]
  transfers between devices with their start and end apart: 3 -> 7, of which waited for: 2 -> 5; matrix products, arithmetic and copies ran while one was open for 3% -> 2% of each run, Pallas kernels for 0% -> 0%
where the time goes in v1:
time: 61.9 us; the launch traced here: 61.6 us
  starting transfers between devices  27.1 us (44%)
  other arithmetic  20.5 us (33%)
  waiting for transfers between devices  12 us (19%)
  local copies, waits for them, and re-layouts  1.73 us (3%)
    ppermute x5, starting transfers between devices, from_behind(): return lax.ppermute(block, axis, route)  22.9 us
    another operation x1, other arithmetic, main_step(): running = jnp.cumsum(piece[:, :, None] * grow, axis=0) * fade  12 us
    ppermute x5, waiting for transfers between devices, from_behind(): return lax.ppermute(block, axis, route)  8.18 us
    ppermute x2, starting transfers between devices, butterfly_sum(): lax.ppermute(value, axis, [(i, i ^ step) for i in range(count)])  4.23 us
    ppermute x2, waiting for transfers between devices, butterfly_sum(): lax.ppermute(value, axis, [(i, i ^ step) for i in range(count)])  3.87 us
    dot_general x1, other arithmetic, end_step(): summed = jnp.einsum('sc,scm->cm', piece, grow)  3.07 us
    convert_element_type x1, other arithmetic, per_device(): padded = jnp.concatenate([before, stacked], axis=1).astype(jnp.float32)  1.85 us
  transfers between devices with their start and end apart: 7, of which 5 were waited for; matrix products, arithmetic and copies ran while one was open for 2% of the time, Pallas kernels for 0%

profile of v1, /device:TPU:0, one launch (start us, length us, event | category | flops | bytes accessed | tf_op | source)
XLA Modules:
  0.0 61.6 jit_solution(8031327709203797292)
XLA Ops:
  0.0 0.8 %pad_maximum_fusion = bf16[3,2,2048]{2,1,0:T(2,128)(2,1)S(1)} fusion(bf16[1,128,2048]{2,1,0:T(8,128)(2,1)} %bitcast.26, bf16[1,128,2048]{2,1,0:T(8,128)(2,1)} %bitcast.28, bf16[1,128,2048]{2,1,0:T(8,128)(2,1)} %bitcast.30), kind=kLoop, calls=%fused_computation.31 | loop fusion | flops 73728 | bytes 1597440 | tf_op jit(solution)/shard_map/stack | solution.py:42
  0.8 2.4 %collective-permute-start = (bf16[3,2,2048]{2,1,0:T(2,128)(2,1)S(1)}, bf16[3,2,2048]{2,1,0:T(2,128)(2,1)S(1)}, u32[]{:S(2)}, u32[]{:S(2)}) collective-permute-start(bf16[3,2,2048]{2,1,0:T(2,128)(2,1)S(1)} %pad_maximum_fusion), channel_id=1, source_target_pairs={{0,4},{4,8},{8,12},{12,16},{16,20},{20,24},{24,28},{1,5},{5,9},{9,... | collective-permute-start | bytes 73736 | tf_op jit(solution)/shard_map/ppermute | solution.py:12
  3.2 1.1 %fusion.12 = (f32[3,1,2048]{2,1,0:T(1,128)S(1)}, f32[3,1,2048]{2,1,0:T(1,128)S(1)}, f32[3,1,2048]{2,1,0:T(1,128)S(1)}) fusion(f32[3,3,2048]{2,1,0:T(4,128)} %param.11), kind=kLoop, calls=%fused_computation.37 | loop fusion | bytes 147456 | tf_op jit(solution)/shard_map/slice | solution.py:46
  4.4 0.0 collective-permute-done
  4.4 1.8 %maximum_convert_fusion = f32[3,130,2048]{2,1,0:T(8,128)S(1)} fusion(bf16[1,128,2048]{2,1,0:T(8,128)(2,1)} %bitcast.27, bf16[1,128,2048]{2,1,0:T(8,128)(2,1)} %bitcast.29, bf16[1,128,2048]{2,1,0:T(8,128)(2,1)} %bitcast.31, bf16[3,2,2048]{2,1,0:T(2,128)(2,1)S(1)} %collective-permute-done), kind=kLoop, calls=%fused_computation.13 | loop fusion | flops 6389760 | bytes 4792320 | tf_op jit(solution)/shard_map/convert_element_type | solution.py:45
  6.3 0.9 %fusion.5 = f32[3,128,2048]{2,1,0:T(8,128)S(1)} fusion(f32[3,130,2048]{2,1,0:T(8,128)S(1)} %maximum_convert_fusion, f32[3,2048]{1,0:T(4,128)S(1)} %get-tuple-element.44, f32[3,2048]{1,0:T(4,128)S(1)} %get-tuple-element.45, f32[3,2048]{1,0:T(4,128)S(1)} %bitcast.32), kind=kLoop, calls=%fused_computation.9 | loop fusion | flops 3932160 | bytes 12656640 | tf_op jit(solution)/shard_map/add | solution.py:49
  7.2 0.0 copy-start
  7.2 0.1 fusion.10
  7.3 0.2 bitcast_convert_fusion
  7.6 0.5 copy-done
  8.1 0.0 copy-start.3
  8.1 3.1 %multiply_reduce_fusion = f32[2048,16]{0,1:T(8,128)S(1)} fusion(f32[2048,128]{0,1:T(8,128)S(1)} %get-tuple-element.29, f32[128]{0:T(128)S(1)} %iota_convert_fusion, f32[2048,16]{0,1:T(8,128)S(1)} %copy-done), kind=kLoop, calls=%fused_computation | loop fusion | flops 12550144 | bytes 1311232 | tf_op jit(solution)/shard_map/while/body/eval_jaxpr/sc,scm->cm/dot_general | solution.py:64
  11.2 0.1 multiply_add_fusion.3
  11.3 4.5 %collective-permute-start.1 = (f32[2048,16]{0,1:T(8,128)S(1)}, f32[2048,16]{0,1:T(8,128)S(1)}, u32[]{:S(2)}, u32[]{:S(2)}) collective-permute-start(f32[2048,16]{0,1:T(8,128)S(1)} %multiply_add_fusion.3), channel_id=1, source_target_pairs={{0,4},{4,8},{8,12},{12,16},{16,20},{20,24},{24,28},{1,5},{5,9},{9,... | collective-permute-start | bytes 393224 | tf_op jit(solution)/shard_map/ppermute | solution.py:12
  15.8 3.8 %collective-permute-start.2 = (f32[2048,16]{0,1:T(8,128)S(1)}, f32[2048,16]{0,1:T(8,128)S(1)}, u32[]{:S(2)}, u32[]{:S(2)}) collective-permute-start(f32[2048,16]{0,1:T(8,128)S(1)} %multiply_add_fusion.3), channel_id=1, source_target_pairs={{0,8},{4,12},{8,16},{12,20},{16,24},{20,28},{1,9},{5,13},{9,17},{1... | collective-permute-start | bytes 393224 | tf_op jit(solution)/shard_map/ppermute | solution.py:12
  19.6 0.0 collective-permute-done.1
  19.6 2.5 %collective-permute-done.2 = f32[2048,16]{0,1:T(8,128)S(1)} collective-permute-done((f32[2048,16]{0,1:T(8,128)S(1)}, f32[2048,16]{0,1:T(8,128)S(1)}, u32[]{:S(2)}, u32[]{:S(2)}) %collective-permute-start.2) | collective-permute-done | bytes 131104 | tf_op jit(solution)/shard_map/ppermute | solution.py:12
  22.1 5.4 %collective-permute-start.3 = (f32[2048,16]{0,1:T(8,128)S(1)}, f32[2048,16]{0,1:T(8,128)S(1)}, u32[]{:S(2)}, u32[]{:S(2)}) collective-permute-start(f32[2048,16]{0,1:T(8,128)S(1)} %get-tuple-element.40), channel_id=1, source_target_pairs={{0,8},{4,12},{8,16},{12,20},{16,24},{20,28},{1,9},{5,13},{9,17},{1... | collective-permute-start | bytes 393224 | tf_op jit(solution)/shard_map/ppermute | solution.py:12
  27.5 3.2 %collective-permute-done.3 = f32[2048,16]{0,1:T(8,128)S(1)} collective-permute-done((f32[2048,16]{0,1:T(8,128)S(1)}, f32[2048,16]{0,1:T(8,128)S(1)}, u32[]{:S(2)}, u32[]{:S(2)}) %collective-permute-start.3) | collective-permute-done | bytes 131104 | tf_op jit(solution)/shard_map/ppermute | solution.py:12
  30.8 6.7 %collective-permute-start.4 = (f32[2048,16]{0,1:T(8,128)S(1)}, f32[2048,16]{0,1:T(8,128)S(1)}, u32[]{:S(2)}, u32[]{:S(2)}) collective-permute-start(f32[2048,16]{0,1:T(8,128)S(1)} %multiply_add_fusion.1), channel_id=1, source_target_pairs={{0,16},{4,20},{8,24},{12,28},{1,17},{5,21},{9,25},{13,29},{2,18},{... | collective-permute-start | bytes 393224 | tf_op jit(solution)/shard_map/ppermute | solution.py:12
  37.5 2.5 %collective-permute-done.4 = f32[2048,16]{0,1:T(8,128)S(1)} collective-permute-done((f32[2048,16]{0,1:T(8,128)S(1)}, f32[2048,16]{0,1:T(8,128)S(1)}, u32[]{:S(2)}, u32[]{:S(2)}) %collective-permute-start.4) | collective-permute-done | bytes 131104 | tf_op jit(solution)/shard_map/ppermute | solution.py:12
  40.1 0.0 copy-done.3
  40.1 0.0 copy-start.1
  40.1 0.0 copy-start.2
  40.1 12.0 %multiply_reduce_fusion.1 = f32[128,2048]{1,0:T(8,128)S(1)} fusion(f32[2048,16]{0,1:T(8,128)S(1)} %copy-done.3, f32[2048,16]{0,1:T(8,128)S(1)} %multiply_add_fusion, f32[128]{0:T(128)S(1)} %broadcast_add_fusion, f32[2048,16]{0,1:T(8,128)S(1)} %get-tuple-element.31, f32[128]{0:T(128)S(1)} %iota_convert_fusion, f32[2048,16]{0,1:T(8,128)S(1)} %copy-done, ...), kind=kOutput, calls=%fused_computation.1 | output fusion | flops 570163200 | bytes 2622464 | tf_op jit(solution)/shard_map/while/body/eval_jaxpr/jit(cumsum)/reduce_window_sum | solution.py:72
  52.1 0.0 copy-done.1
  52.1 0.3 multiply_reduce_fusion.2
  52.4 1.6 %collective-permute-start.5 = (f32[128]{0:T(128)S(1)}, f32[128]{0:T(128)S(1)}, u32[]{:S(2)}, u32[]{:S(2)}) collective-permute-start(f32[128]{0:T(128)S(1)} %multiply_reduce_fusion.2), channel_id=1, source_target_pairs={{0,1},{1,0},{2,3},{3,2},{4,5},{5,4},{6,7},{7,6},{8,9},{9,8},{10,11... | collective-permute-start | bytes 1544 | tf_op jit(solution)/shard_map/ppermute | solution.py:34
  54.0 2.0 %collective-permute-done.5 = f32[128]{0:T(128)S(1)} collective-permute-done((f32[128]{0:T(128)S(1)}, f32[128]{0:T(128)S(1)}, u32[]{:S(2)}, u32[]{:S(2)}) %collective-permute-start.5) | collective-permute-done | bytes 544 | tf_op jit(solution)/shard_map/ppermute | solution.py:34
  56.0 2.6 %collective-permute-start.6 = (f32[128]{0:T(128)S(1)}, f32[128]{0:T(128)S(1)}, u32[]{:S(2)}, u32[]{:S(2)}) collective-permute-start(f32[128]{0:T(128)S(1)} %add.63), channel_id=1, source_target_pairs={{0,2},{1,3},{2,0},{3,1},{4,6},{5,7},{6,4},{7,5},{8,10},{9,11},{10,... | collective-permute-start | bytes 1544 | tf_op jit(solution)/shard_map/ppermute | solution.py:34
  58.6 1.9 %collective-permute-done.6 = f32[128]{0:T(128)S(1)} collective-permute-done((f32[128]{0:T(128)S(1)}, f32[128]{0:T(128)S(1)}, u32[]{:S(2)}, u32[]{:S(2)}) %collective-permute-start.6) | collective-permute-done | bytes 544 | tf_op jit(solution)/shard_map/ppermute | solution.py:34
  60.5 0.0 copy-done.2
  60.5 1.0 %multiply_convert_fusion = bf16[128,2048]{1,0:T(8,128)(2,1)} fusion(f32[2048]{0:T(1024)S(1)} %copy-done.2, f32[128]{0:T(128)S(1)} %add_rsqrt_fusion, f32[128,2048]{1,0:T(8,128)S(1)} %multiply_reduce_fusion.1, f32[3,128,2048]{2,1,0:T(8,128)S(1)} %fusion.5, bf16[128,2048]{1,0:T(8,128)(2,1)S(1)} %copy-done.1), kind=kLoop, calls=%fused_computation.19 | loop fusion | flops 1572864 | bytes 3154432 | tf_op jit(solution)/shard_map/convert_element_type | solution.py:81
  (9 shorter events, 0.2 us)
Async XLA Ops:
  0.8 3.6 %collective-permute-start = (bf16[3,2,2048]{2,1,0:T(2,128)(2,1)S(1)}, bf16[3,2,2048]{2,1,0:T(2,128)(2,1)S(1)}, u32[]{:S(2)}, u32[]{:S(2)}) collective-permute-start(bf16[3,2,2048]{2,1,0:T(2,128)(2,1)S(1)} %pad_maximum_fusion), channel_id=1, source_target_pairs={{0,4},{4,8},{8,12},{12,16},{16,20},{20,24},{24,28},{1,5},{5,9},{9,... | collective-permute-start | bytes 73736 | tf_op jit(solution)/shard_map/ppermute | solution.py:12
  7.2 0.9 %copy-start = (f32[2048,16]{0,1:T(8,128)S(1)}, f32[2048,16]{0,1:T(8,128)}, u32[]{:S(2)}) copy-start(f32[2048,16]{0,1:T(8,128)} %param.12) | copy-start | bytes 393220
  8.1 31.9 %copy-start.3 = (f32[2048,16]{0,1:T(8,128)S(1)}, f32[2048,16]{0,1:T(8,128)}, u32[]{:S(2)}) copy-start(f32[2048,16]{0,1:T(8,128)} %param.13) | copy-start | bytes 393220
  11.3 8.4 %collective-permute-start.1 = (f32[2048,16]{0,1:T(8,128)S(1)}, f32[2048,16]{0,1:T(8,128)S(1)}, u32[]{:S(2)}, u32[]{:S(2)}) collective-permute-start(f32[2048,16]{0,1:T(8,128)S(1)} %multiply_add_fusion.3), channel_id=1, source_target_pairs={{0,4},{4,8},{8,12},{12,16},{16,20},{20,24},{24,28},{1,5},{5,9},{9,... | collective-permute-start | bytes 393224 | tf_op jit(solution)/shard_map/ppermute | solution.py:12
  15.8 6.3 %collective-permute-start.2 = (f32[2048,16]{0,1:T(8,128)S(1)}, f32[2048,16]{0,1:T(8,128)S(1)}, u32[]{:S(2)}, u32[]{:S(2)}) collective-permute-start(f32[2048,16]{0,1:T(8,128)S(1)} %multiply_add_fusion.3), channel_id=1, source_target_pairs={{0,8},{4,12},{8,16},{12,20},{16,24},{20,28},{1,9},{5,13},{9,17},{1... | collective-permute-start | bytes 393224 | tf_op jit(solution)/shard_map/ppermute | solution.py:12
  22.1 8.6 %collective-permute-start.3 = (f32[2048,16]{0,1:T(8,128)S(1)}, f32[2048,16]{0,1:T(8,128)S(1)}, u32[]{:S(2)}, u32[]{:S(2)}) collective-permute-start(f32[2048,16]{0,1:T(8,128)S(1)} %get-tuple-element.40), channel_id=1, source_target_pairs={{0,8},{4,12},{8,16},{12,20},{16,24},{20,28},{1,9},{5,13},{9,17},{1... | collective-permute-start | bytes 393224 | tf_op jit(solution)/shard_map/ppermute | solution.py:12
  30.8 9.2 %collective-permute-start.4 = (f32[2048,16]{0,1:T(8,128)S(1)}, f32[2048,16]{0,1:T(8,128)S(1)}, u32[]{:S(2)}, u32[]{:S(2)}) collective-permute-start(f32[2048,16]{0,1:T(8,128)S(1)} %multiply_add_fusion.1), channel_id=1, source_target_pairs={{0,16},{4,20},{8,24},{12,28},{1,17},{5,21},{9,25},{13,29},{2,18},{... | collective-permute-start | bytes 393224 | tf_op jit(solution)/shard_map/ppermute | solution.py:12
  40.1 12.0 %copy-start.1 = (bf16[128,2048]{1,0:T(8,128)(2,1)S(1)}, bf16[128,2048]{1,0:T(8,128)(2,1)}, u32[]{:S(2)}) copy-start(bf16[128,2048]{1,0:T(8,128)(2,1)} %param.14) | copy-start | bytes 1572868
  40.1 20.4 %copy-start.2 = (f32[2048]{0:T(1024)S(1)}, f32[2048]{0:T(1024)}, u32[]{:S(2)}) copy-start(f32[2048]{0:T(1024)} %param.15) | copy-start | bytes 24580
  52.4 3.6 %collective-permute-start.5 = (f32[128]{0:T(128)S(1)}, f32[128]{0:T(128)S(1)}, u32[]{:S(2)}, u32[]{:S(2)}) collective-permute-start(f32[128]{0:T(128)S(1)} %multiply_reduce_fusion.2), channel_id=1, source_target_pairs={{0,1},{1,0},{2,3},{3,2},{4,5},{5,4},{6,7},{7,6},{8,9},{9,8},{10,11... | collective-permute-start | bytes 1544 | tf_op jit(solution)/shard_map/ppermute | solution.py:34
  56.0 4.5 %collective-permute-start.6 = (f32[128]{0:T(128)S(1)}, f32[128]{0:T(128)S(1)}, u32[]{:S(2)}, u32[]{:S(2)}) collective-permute-start(f32[128]{0:T(128)S(1)} %add.63), channel_id=1, source_target_pairs={{0,2},{1,3},{2,0},{3,1},{4,6},{5,7},{6,4},{7,5},{8,10},{9,11},{10,... | collective-permute-start | bytes 1544 | tf_op jit(solution)/shard_map/ppermute | solution.py:34

commit v2 on v1

--- a/solution.py
+++ b/solution.py
@@ -12,18 +12,19 @@
     return lax.ppermute(block, axis, route)
 
 
-def scan_in(ending, rate, rows, axis):
+def scan_in(ending, rate, rows, axis, cover):
     count = lax.axis_size(axis)
-    if count == 1:
-        return jnp.zeros_like(ending)
-    incoming = from_behind(ending, axis, 1)
-    if count > 2:
-        incoming = incoming + jnp.exp(-rate * rows) * from_behind(ending, axis, 2)
-    shift = 2
-    while shift < count:
-        incoming = incoming + jnp.exp(-rate * (rows * shift)) * from_behind(incoming, axis, shift)
-        shift *= 2
-    return incoming
+    radix = min(count, 8)
+    arrived = [from_behind(ending, axis, shift) for shift in range(1, radix)]
+    arrived, covered = lax.optimization_barrier((arrived, cover()))
+    incoming = jnp.zeros_like(ending)
+    for shift in range(1, radix):
+        incoming = incoming + jnp.exp(-rate * (rows * (shift - 1))) * arrived[shift - 1]
+    span = radix - 1
+    while span < count - 1:
+        incoming = incoming + jnp.exp(-rate * (rows * span)) * from_behind(incoming, axis, span)
+        span *= 2
+    return incoming, covered
 
 
 def butterfly_sum(value, axis):
@@ -66,15 +67,22 @@
 
     zeros = jnp.zeros(rate.shape, jnp.float32)
     ending, unused = lax.scan(end_step, zeros, blocks)
-    incoming = scan_in(ending, rate, rows, "ctx")
 
     def main_step(state, piece):
         running = jnp.cumsum(piece[:, :, None] * grow, axis=0) * fade
         states = running + enter * state[None, :, :]
         return (states[-1], jnp.sum(states * residue[None, :, :], axis=2))
 
-    unused_state, outputs = lax.scan(main_step, incoming, blocks)
-    mixed = outputs.reshape(rows, width)
+    def local():
+        if rows == block:
+            return main_step(zeros, values)[1]
+        return lax.scan(main_step, zeros, blocks)[1].reshape(rows, width)
+
+    incoming, outputs = scan_in(ending, rate, rows, "ctx", local)
+    times = jnp.arange(rows, dtype=jnp.int32).astype(jnp.float32) + 1.0
+    weights = residue * incoming
+    mixed_in = jnp.sum(jnp.exp(-rate[None, :, :] * times[:, None, None]) * weights[None, :, :], axis=2)
+    mixed = outputs + mixed_in
     stream = resid.astype(jnp.float32) + q_feat * mixed
     squares = butterfly_sum(jnp.sum(stream * stream, axis=1), "tp")
     scale = lax.rsqrt(squares / D + 1e-05)
@@ -93,6 +101,7 @@
         P("tp"),
     )
     out_specs = P("ctx", "tp")
-    return jax.shard_map(
+    step = jax.shard_map(
         per_device, mesh=mesh, in_specs=in_specs, out_specs=out_specs, check_vma=False
     )
+    return step

time: 61.9 us -> 56.4 us (0.911)
  waiting for transfers between devices: 12 us -> 3.89 us
  other arithmetic: 20.5 us -> 25.6 us
  starting transfers between devices: 27.1 us -> 24.5 us
    ppermute x5 -> x8, waiting for transfers between devices: 8.18 us -> 0.02 us  [from_behind(): return lax.ppermute(block, axis, route)]
    reduce_sum x0 -> x1, other arithmetic: none -> 5.31 us  [per_device(): jnp.sum(jnp.exp(-rate[None, :, :] * times[:, None, None]) * weights[None,...]
    ppermute x5 -> x8, starting transfers between devices: 22.9 us -> 20.2 us  [from_behind(): return lax.ppermute(block, axis, route)]
  transfers between devices with their start and end apart: 7 -> 10, of which waited for: 5 -> 2; matrix products, arithmetic and copies ran while one was open for 2% -> 23% of each run, Pallas kernels for 0% -> 0%
where the time goes in v2:
time: 56.4 us; the launch traced here: 56 us
  other arithmetic  25.6 us (45%)
  starting transfers between devices  24.5 us (43%)
  waiting for transfers between devices  3.89 us (7%)
  local copies, waits for them, and re-layouts  1.73 us (3%)
    ppermute x8, starting transfers between devices, from_behind(): return lax.ppermute(block, axis, route)  20.2 us
    another operation x1, other arithmetic, main_step(): running = jnp.cumsum(piece[:, :, None] * grow, axis=0) * fade  11.7 us
    reduce_sum x1, other arithmetic, per_device(): jnp.sum(jnp.exp(-rate[None, :, :] * times[:, None, None]) * weights[None,...  5.31 us
    ppermute x2, starting transfers between devices, butterfly_sum(): lax.ppermute(value, axis, [(i, i ^ step) for i in range(count)])  4.23 us
    ppermute x2, waiting for transfers between devices, butterfly_sum(): lax.ppermute(value, axis, [(i, i ^ step) for i in range(count)])  3.87 us
    dot_general x1, other arithmetic, end_step(): summed = jnp.einsum('sc,scm->cm', piece, grow)  3.07 us
    convert_element_type x1, other arithmetic, per_device(): padded = jnp.concatenate([before, stacked], axis=1).astype(jnp.float32)  1.85 us
  transfers between devices with their start and end apart: 10, of which 2 were waited for; matrix products, arithmetic and copies ran while one was open for 23% of the time, Pallas kernels for 0%

profile of v2, /device:TPU:0, one launch (start us, length us, event | category | flops | bytes accessed | tf_op | source)
XLA Modules:
  0.0 56.0 jit_solution(5041625061650877975)
XLA Ops:
  0.0 0.8 %pad_maximum_fusion = bf16[3,2,2048]{2,1,0:T(2,128)(2,1)S(1)} fusion(bf16[1,128,2048]{2,1,0:T(8,128)(2,1)} %bitcast.23, bf16[1,128,2048]{2,1,0:T(8,128)(2,1)} %bitcast.25, bf16[1,128,2048]{2,1,0:T(8,128)(2,1)} %bitcast.27), kind=kLoop, calls=%fused_computation.31 | loop fusion | flops 73728 | bytes 1597440 | tf_op jit(solution)/shard_map/stack | solution.py:43
  0.8 2.4 %collective-permute-start = (bf16[3,2,2048]{2,1,0:T(2,128)(2,1)S(1)}, bf16[3,2,2048]{2,1,0:T(2,128)(2,1)S(1)}, u32[]{:S(2)}, u32[]{:S(2)}) collective-permute-start(bf16[3,2,2048]{2,1,0:T(2,128)(2,1)S(1)} %pad_maximum_fusion), channel_id=1, source_target_pairs={{0,4},{4,8},{8,12},{12,16},{16,20},{20,24},{24,28},{1,5},{5,9},{9,... | collective-permute-start | bytes 73736 | tf_op jit(solution)/shard_map/ppermute | solution.py:12
  3.2 1.1 %fusion.14 = (f32[3,1,2048]{2,1,0:T(1,128)S(1)}, f32[3,1,2048]{2,1,0:T(1,128)S(1)}, f32[3,1,2048]{2,1,0:T(1,128)S(1)}) fusion(f32[3,3,2048]{2,1,0:T(4,128)} %param.11), kind=kLoop, calls=%fused_computation.38 | loop fusion | bytes 147456 | tf_op jit(solution)/shard_map/slice | solution.py:47
  4.4 0.0 collective-permute-done
  4.4 1.8 %maximum_convert_fusion = f32[3,130,2048]{2,1,0:T(8,128)S(1)} fusion(bf16[1,128,2048]{2,1,0:T(8,128)(2,1)} %bitcast.24, bf16[1,128,2048]{2,1,0:T(8,128)(2,1)} %bitcast.26, bf16[1,128,2048]{2,1,0:T(8,128)(2,1)} %bitcast.28, bf16[3,2,2048]{2,1,0:T(2,128)(2,1)S(1)} %collective-permute-done), kind=kLoop, calls=%fused_computation.15 | loop fusion | flops 6389760 | bytes 4792320 | tf_op jit(solution)/shard_map/convert_element_type | solution.py:46
  6.3 0.9 %fusion.5 = f32[3,128,2048]{2,1,0:T(8,128)S(1)} fusion(f32[3,130,2048]{2,1,0:T(8,128)S(1)} %maximum_convert_fusion, f32[3,2048]{1,0:T(4,128)S(1)} %get-tuple-element.48, f32[3,2048]{1,0:T(4,128)S(1)} %get-tuple-element.49, f32[3,2048]{1,0:T(4,128)S(1)} %bitcast.29), kind=kLoop, calls=%fused_computation.11 | loop fusion | flops 3932160 | bytes 12656640 | tf_op jit(solution)/shard_map/add | solution.py:50
  7.2 0.0 copy-start.1
  7.2 0.1 fusion.10
  7.3 0.2 fusion.12
  7.6 0.5 copy-done.1
  8.1 0.0 copy-start.2
  8.1 3.1 %multiply_reduce_fusion = f32[2048,16]{0,1:T(8,128)S(1)} fusion(f32[2048,128]{0,1:T(8,128)S(1)} %get-tuple-element.42, f32[128]{0:T(128)S(1)} %iota_convert_fusion, f32[2048,16]{0,1:T(8,128)S(1)} %copy-done.1), kind=kLoop, calls=%fused_computation | loop fusion | flops 12550144 | bytes 1311232 | tf_op jit(solution)/shard_map/while/body/eval_jaxpr/sc,scm->cm/dot_general | solution.py:65
  11.2 0.1 fusion.13
  11.3 4.5 %collective-permute-start.1 = (f32[2048,16]{0,1:T(8,128)S(1)}, f32[2048,16]{0,1:T(8,128)S(1)}, u32[]{:S(2)}, u32[]{:S(2)}) collective-permute-start(f32[2048,16]{0,1:T(8,128)S(1)} %get-tuple-element.44), channel_id=1, source_target_pairs={{0,4},{4,8},{8,12},{12,16},{16,20},{20,24},{24,28},{1,5},{5,9},{9,... | collective-permute-start | bytes 393224 | tf_op jit(solution)/shard_map/ppermute | solution.py:12
  15.8 3.8 %collective-permute-start.2 = (f32[2048,16]{0,1:T(8,128)S(1)}, f32[2048,16]{0,1:T(8,128)S(1)}, u32[]{:S(2)}, u32[]{:S(2)}) collective-permute-start(f32[2048,16]{0,1:T(8,128)S(1)} %get-tuple-element.44), channel_id=1, source_target_pairs={{0,8},{4,12},{8,16},{12,20},{16,24},{20,28},{1,9},{5,13},{9,17},{1... | collective-permute-start | bytes 393224 | tf_op jit(solution)/shard_map/ppermute | solution.py:12
  19.6 4.3 %collective-permute-start.3 = (f32[2048,16]{0,1:T(8,128)S(1)}, f32[2048,16]{0,1:T(8,128)S(1)}, u32[]{:S(2)}, u32[]{:S(2)}) collective-permute-start(f32[2048,16]{0,1:T(8,128)S(1)} %get-tuple-element.44), channel_id=1, source_target_pairs={{0,12},{4,16},{8,20},{12,24},{16,28},{1,13},{5,17},{9,21},{13,25},... | collective-permute-start | bytes 393224 | tf_op jit(solution)/shard_map/ppermute | solution.py:12
  23.9 1.3 %collective-permute-start.4 = (f32[2048,16]{0,1:T(8,128)S(1)}, f32[2048,16]{0,1:T(8,128)S(1)}, u32[]{:S(2)}, u32[]{:S(2)}) collective-permute-start(f32[2048,16]{0,1:T(8,128)S(1)} %get-tuple-element.44), channel_id=1, source_target_pairs={{0,16},{4,20},{8,24},{12,28},{1,17},{5,21},{9,25},{13,29},{2,18},{... | collective-permute-start | bytes 393224 | tf_op jit(solution)/shard_map/ppermute | solution.py:12
  25.2 1.3 %collective-permute-start.5 = (f32[2048,16]{0,1:T(8,128)S(1)}, f32[2048,16]{0,1:T(8,128)S(1)}, u32[]{:S(2)}, u32[]{:S(2)}) collective-permute-start(f32[2048,16]{0,1:T(8,128)S(1)} %get-tuple-element.44), channel_id=1, source_target_pairs={{0,20},{4,24},{8,28},{1,21},{5,25},{9,29},{2,22},{6,26},{10,30},{3... | collective-permute-start | bytes 393224 | tf_op jit(solution)/shard_map/ppermute | solution.py:12
  26.6 0.0 collective-permute-done.1
  26.6 1.3 %collective-permute-start.6 = (f32[2048,16]{0,1:T(8,128)S(1)}, f32[2048,16]{0,1:T(8,128)S(1)}, u32[]{:S(2)}, u32[]{:S(2)}) collective-permute-start(f32[2048,16]{0,1:T(8,128)S(1)} %get-tuple-element.44), channel_id=1, source_target_pairs={{0,24},{4,28},{1,25},{5,29},{2,26},{6,30},{3,27},{7,31}} | collective-permute-start | bytes 393224 | tf_op jit(solution)/shard_map/ppermute | solution.py:12
  27.9 0.0 collective-permute-done.2
  27.9 1.3 %collective-permute-start.7 = (f32[2048,16]{0,1:T(8,128)S(1)}, f32[2048,16]{0,1:T(8,128)S(1)}, u32[]{:S(2)}, u32[]{:S(2)}) collective-permute-start(f32[2048,16]{0,1:T(8,128)S(1)} %get-tuple-element.44), channel_id=1, source_target_pairs={{0,28},{1,29},{2,30},{3,31}} | collective-permute-start | bytes 393224 | tf_op jit(solution)/shard_map/ppermute | solution.py:12
  29.2 0.0 copy-done.2
  29.2 11.7 %multiply_reduce_fusion.2 = f32[128,2048]{1,0:T(8,128)S(1)} fusion(f32[2048,16]{0,1:T(8,128)S(1)} %copy-done.2, f32[128]{0:T(128)S(1)} %broadcast_add_fusion, f32[2048,16]{0,1:T(8,128)S(1)} %get-tuple-element.43, f32[128]{0:T(128)S(1)} %iota_convert_fusion, f32[128,2048]{1,0:T(8,128)S(1)} %get-tuple-element.41, f32[2048,16]{0,1:T(8,128)S(1)} %copy-done.1), kind=kOutput, calls=%fused_computation.2 | output fusion | flops 570163200 | bytes 2491392 | tf_op jit(solution)/shard_map/jit(cumsum)/reduce_window_sum | solution.py:72
  40.9 0.0 collective-permute-done.3
  40.9 0.0 collective-permute-done.4
  40.9 0.0 collective-permute-done.5
  40.9 0.0 collective-permute-done.6
  40.9 0.0 collective-permute-done.7
  41.0 0.2 add_multiply_fusion
  41.1 0.0 copy-start
  41.1 5.3 %multiply_reduce_fusion.1 = f32[128,2048]{1,0:T(8,128)S(1)} fusion(f32[2048,16]{0,1:T(8,128)S(1)} %add_multiply_fusion, f32[128]{0:T(128)S(1)} %broadcast_add_fusion, f32[2048,16]{0,1:T(8,128)S(1)} %get-tuple-element.43), kind=kLoop, calls=%fused_computation.1 | loop fusion | flops 12320768 | bytes 1311232 | tf_op jit(solution)/shard_map/reduce_sum | solution.py:84
  46.5 0.0 copy-done
  46.5 0.0 copy-start.3
  46.5 0.4 multiply_reduce_fusion.3
  46.9 1.6 %collective-permute-start.8 = (f32[128]{0:T(128)S(1)}, f32[128]{0:T(128)S(1)}, u32[]{:S(2)}, u32[]{:S(2)}) collective-permute-start(f32[128]{0:T(128)S(1)} %get-tuple-element.39), channel_id=1, source_target_pairs={{0,1},{1,0},{2,3},{3,2},{4,5},{5,4},{6,7},{7,6},{8,9},{9,8},{10,11... | collective-permute-start | bytes 1544 | tf_op jit(solution)/shard_map/ppermute | solution.py:35
  48.6 2.0 %collective-permute-done.8 = f32[128]{0:T(128)S(1)} collective-permute-done((f32[128]{0:T(128)S(1)}, f32[128]{0:T(128)S(1)}, u32[]{:S(2)}, u32[]{:S(2)}) %collective-permute-start.8) | collective-permute-done | bytes 544 | tf_op jit(solution)/shard_map/ppermute | solution.py:35
  50.5 2.6 %collective-permute-start.9 = (f32[128]{0:T(128)S(1)}, f32[128]{0:T(128)S(1)}, u32[]{:S(2)}, u32[]{:S(2)}) collective-permute-start(f32[128]{0:T(128)S(1)} %add.79), channel_id=1, source_target_pairs={{0,2},{1,3},{2,0},{3,1},{4,6},{5,7},{6,4},{7,5},{8,10},{9,11},{10,... | collective-permute-start | bytes 1544 | tf_op jit(solution)/shard_map/ppermute | solution.py:35
  53.1 1.9 %collective-permute-done.9 = f32[128]{0:T(128)S(1)} collective-permute-done((f32[128]{0:T(128)S(1)}, f32[128]{0:T(128)S(1)}, u32[]{:S(2)}, u32[]{:S(2)}) %collective-permute-start.9) | collective-permute-done | bytes 544 | tf_op jit(solution)/shard_map/ppermute | solution.py:35
  55.0 0.0 copy-done.3
  55.0 1.0 %multiply_convert_fusion = bf16[128,2048]{1,0:T(8,128)(2,1)} fusion(f32[128,2048]{1,0:T(8,128)S(1)} %get-tuple-element.40, f32[2048]{0:T(1024)S(1)} %copy-done.3, f32[128]{0:T(128)S(1)} %add_rsqrt_fusion), kind=kLoop, calls=%fused_computation.21 | loop fusion | flops 786432 | bytes 1581568 | tf_op jit(solution)/shard_map/convert_element_type | solution.py:89
  (6 shorter events, 0.1 us)
Async XLA Ops:
  0.8 3.6 %collective-permute-start = (bf16[3,2,2048]{2,1,0:T(2,128)(2,1)S(1)}, bf16[3,2,2048]{2,1,0:T(2,128)(2,1)S(1)}, u32[]{:S(2)}, u32[]{:S(2)}) collective-permute-start(bf16[3,2,2048]{2,1,0:T(2,128)(2,1)S(1)} %pad_maximum_fusion), channel_id=1, source_target_pairs={{0,4},{4,8},{8,12},{12,16},{16,20},{20,24},{24,28},{1,5},{5,9},{9,... | collective-permute-start | bytes 73736 | tf_op jit(solution)/shard_map/ppermute | solution.py:12
  7.2 0.9 %copy-start.1 = (f32[2048,16]{0,1:T(8,128)S(1)}, f32[2048,16]{0,1:T(8,128)}, u32[]{:S(2)}) copy-start(f32[2048,16]{0,1:T(8,128)} %param.12) | copy-start | bytes 393220
  8.1 21.1 %copy-start.2 = (f32[2048,16]{0,1:T(8,128)S(1)}, f32[2048,16]{0,1:T(8,128)}, u32[]{:S(2)}) copy-start(f32[2048,16]{0,1:T(8,128)} %param.13) | copy-start | bytes 393220
  11.3 15.3 %collective-permute-start.1 = (f32[2048,16]{0,1:T(8,128)S(1)}, f32[2048,16]{0,1:T(8,128)S(1)}, u32[]{:S(2)}, u32[]{:S(2)}) collective-permute-start(f32[2048,16]{0,1:T(8,128)S(1)} %get-tuple-element.44), channel_id=1, source_target_pairs={{0,4},{4,8},{8,12},{12,16},{16,20},{20,24},{24,28},{1,5},{5,9},{9,... | collective-permute-start | bytes 393224 | tf_op jit(solution)/shard_map/ppermute | solution.py:12
  15.8 12.1 %collective-permute-start.2 = (f32[2048,16]{0,1:T(8,128)S(1)}, f32[2048,16]{0,1:T(8,128)S(1)}, u32[]{:S(2)}, u32[]{:S(2)}) collective-permute-start(f32[2048,16]{0,1:T(8,128)S(1)} %get-tuple-element.44), channel_id=1, source_target_pairs={{0,8},{4,12},{8,16},{12,20},{16,24},{20,28},{1,9},{5,13},{9,17},{1... | collective-permute-start | bytes 393224 | tf_op jit(solution)/shard_map/ppermute | solution.py:12
  19.6 21.3 %collective-permute-start.3 = (f32[2048,16]{0,1:T(8,128)S(1)}, f32[2048,16]{0,1:T(8,128)S(1)}, u32[]{:S(2)}, u32[]{:S(2)}) collective-permute-start(f32[2048,16]{0,1:T(8,128)S(1)} %get-tuple-element.44), channel_id=1, source_target_pairs={{0,12},{4,16},{8,20},{12,24},{16,28},{1,13},{5,17},{9,21},{13,25},... | collective-permute-start | bytes 393224 | tf_op jit(solution)/shard_map/ppermute | solution.py:12
  23.9 17.0 %collective-permute-start.4 = (f32[2048,16]{0,1:T(8,128)S(1)}, f32[2048,16]{0,1:T(8,128)S(1)}, u32[]{:S(2)}, u32[]{:S(2)}) collective-permute-start(f32[2048,16]{0,1:T(8,128)S(1)} %get-tuple-element.44), channel_id=1, source_target_pairs={{0,16},{4,20},{8,24},{12,28},{1,17},{5,21},{9,25},{13,29},{2,18},{... | collective-permute-start | bytes 393224 | tf_op jit(solution)/shard_map/ppermute | solution.py:12
  25.2 15.7 %collective-permute-start.5 = (f32[2048,16]{0,1:T(8,128)S(1)}, f32[2048,16]{0,1:T(8,128)S(1)}, u32[]{:S(2)}, u32[]{:S(2)}) collective-permute-start(f32[2048,16]{0,1:T(8,128)S(1)} %get-tuple-element.44), channel_id=1, source_target_pairs={{0,20},{4,24},{8,28},{1,21},{5,25},{9,29},{2,22},{6,26},{10,30},{3... | collective-permute-start | bytes 393224 | tf_op jit(solution)/shard_map/ppermute | solution.py:12
  26.6 14.4 %collective-permute-start.6 = (f32[2048,16]{0,1:T(8,128)S(1)}, f32[2048,16]{0,1:T(8,128)S(1)}, u32[]{:S(2)}, u32[]{:S(2)}) collective-permute-start(f32[2048,16]{0,1:T(8,128)S(1)} %get-tuple-element.44), channel_id=1, source_target_pairs={{0,24},{4,28},{1,25},{5,29},{2,26},{6,30},{3,27},{7,31}} | collective-permute-start | bytes 393224 | tf_op jit(solution)/shard_map/ppermute | solution.py:12
  27.9 13.1 %collective-permute-start.7 = (f32[2048,16]{0,1:T(8,128)S(1)}, f32[2048,16]{0,1:T(8,128)S(1)}, u32[]{:S(2)}, u32[]{:S(2)}) collective-permute-start(f32[2048,16]{0,1:T(8,128)S(1)} %get-tuple-element.44), channel_id=1, source_target_pairs={{0,28},{1,29},{2,30},{3,31}} | collective-permute-start | bytes 393224 | tf_op jit(solution)/shard_map/ppermute | solution.py:12
  41.1 5.3 %copy-start = (bf16[128,2048]{1,0:T(8,128)(2,1)S(1)}, bf16[128,2048]{1,0:T(8,128)(2,1)}, u32[]{:S(2)}) copy-start(bf16[128,2048]{1,0:T(8,128)(2,1)} %param.14) | copy-start | bytes 1572868
  46.5 8.6 %copy-start.3 = (f32[2048]{0:T(1024)S(1)}, f32[2048]{0:T(1024)}, u32[]{:S(2)}) copy-start(f32[2048]{0:T(1024)} %param.15) | copy-start | bytes 24580
  46.9 3.6 %collective-permute-start.8 = (f32[128]{0:T(128)S(1)}, f32[128]{0:T(128)S(1)}, u32[]{:S(2)}, u32[]{:S(2)}) collective-permute-start(f32[128]{0:T(128)S(1)} %get-tuple-element.39), channel_id=1, source_target_pairs={{0,1},{1,0},{2,3},{3,2},{4,5},{5,4},{6,7},{7,6},{8,9},{9,8},{10,11... | collective-permute-start | bytes 1544 | tf_op jit(solution)/shard_map/ppermute | solution.py:35
  50.5 4.5 %collective-permute-start.9 = (f32[128]{0:T(128)S(1)}, f32[128]{0:T(128)S(1)}, u32[]{:S(2)}, u32[]{:S(2)}) collective-permute-start(f32[128]{0:T(128)S(1)} %add.79), channel_id=1, source_target_pairs={{0,2},{1,3},{2,0},{3,1},{4,6},{5,7},{6,4},{7,5},{8,10},{9,11},{10,... | collective-permute-start | bytes 1544 | tf_op jit(solution)/shard_map/ppermute | solution.py:35

commit v3 on v2

--- a/solution.py
+++ b/solution.py
@@ -66,16 +66,22 @@
         return (state * block_decay + last_fade * summed, None)
 
     zeros = jnp.zeros(rate.shape, jnp.float32)
+    lower = (offsets[:, None] >= offsets[None, :]).astype(jnp.float32)
+
+    def cumulative(terms):
+        return jnp.einsum("ts,scm->tcm", lower, terms, precision=lax.Precision.HIGHEST)
+
     ending, unused = lax.scan(end_step, zeros, blocks)
 
     def main_step(state, piece):
-        running = jnp.cumsum(piece[:, :, None] * grow, axis=0) * fade
+        running = cumulative(piece[:, :, None] * grow) * fade
         states = running + enter * state[None, :, :]
         return (states[-1], jnp.sum(states * residue[None, :, :], axis=2))
 
     def local():
         if rows == block:
-            return main_step(zeros, values)[1]
+            running = cumulative(values[:, :, None] * grow) * fade
+            return jnp.sum(running * residue[None, :, :], axis=2)
         return lax.scan(main_step, zeros, blocks)[1].reshape(rows, width)
 
     incoming, outputs = scan_in(ending, rate, rows, "ctx", local)

time: 56.4 us -> 58.3 us (1.034)
  matrix products: 0 us -> 16 us
  other arithmetic: 25.6 us -> 11.3 us
    dot_general x0 -> x1, matrix products: none -> 16 us  [cumulative(): jnp.einsum('ts,scm->tcm', lower, terms, precision=lax.Precision.HIGHEST)]
    another operation x1 -> x0, other arithmetic: 11.7 us -> none  [main_step(): running = jnp.cumsum(piece[:, :, None] * grow, axis=0) * fade]
    reduce_sum x1, other arithmetic: 5.31 us -> 2.78 us  [per_device(): jnp.sum(jnp.exp(-rate[None, :, :] * times[:, None, None]) * weights[None,...]
  transfers between devices with their start and end apart: 10 -> 10, of which waited for: 2 -> 2; matrix products, arithmetic and copies ran while one was open for 23% -> 30% of each run, Pallas kernels for 0% -> 0%
where the time goes in v3:
time: 58.3 us; the launch traced here: 57.9 us
  starting transfers between devices  24.7 us (42%)
  matrix products  16 us (27%)
  other arithmetic  11.3 us (19%)
  waiting for transfers between devices  3.89 us (7%)
  local copies, waits for them, and re-layouts  1.72 us (3%)
    ppermute x8, starting transfers between devices, from_behind(): return lax.ppermute(block, axis, route)  20.4 us
    dot_general x1, matrix products, cumulative(): jnp.einsum('ts,scm->tcm', lower, terms, precision=lax.Precision.HIGHEST)  16 us
    ppermute x2, starting transfers between devices, butterfly_sum(): lax.ppermute(value, axis, [(i, i ^ step) for i in range(count)])  4.23 us
    ppermute x2, waiting for transfers between devices, butterfly_sum(): lax.ppermute(value, axis, [(i, i ^ step) for i in range(count)])  3.87 us
    dot_general x1, other arithmetic, end_step(): summed = jnp.einsum('sc,scm->cm', piece, grow)  2.98 us
    reduce_sum x1, other arithmetic, per_device(): jnp.sum(jnp.exp(-rate[None, :, :] * times[:, None, None]) * weights[None,...  2.78 us
    convert_element_type x1, other arithmetic, per_device(): padded = jnp.concatenate([before, stacked], axis=1).astype(jnp.float32)  1.84 us
  transfers between devices with their start and end apart: 10, of which 2 were waited for; matrix products, arithmetic and copies ran while one was open for 30% of the time, Pallas kernels for 0%

profile of v3, /device:TPU:0, one launch (start us, length us, event | category | flops | bytes accessed | tf_op | source)
XLA Modules:
  0.0 57.9 jit_solution(9446937209460096275)
XLA Ops:
  0.0 0.8 %pad_maximum_fusion = bf16[3,2,2048]{2,1,0:T(2,128)(2,1)S(1)} fusion(bf16[1,128,2048]{2,1,0:T(8,128)(2,1)} %bitcast.26, bf16[1,128,2048]{2,1,0:T(8,128)(2,1)} %bitcast.28, bf16[1,128,2048]{2,1,0:T(8,128)(2,1)} %bitcast.30), kind=kLoop, calls=%fused_computation.34 | loop fusion | flops 73728 | bytes 1597440 | tf_op jit(solution)/shard_map/stack | solution.py:43
  0.8 2.4 %collective-permute-start = (bf16[3,2,2048]{2,1,0:T(2,128)(2,1)S(1)}, bf16[3,2,2048]{2,1,0:T(2,128)(2,1)S(1)}, u32[]{:S(2)}, u32[]{:S(2)}) collective-permute-start(bf16[3,2,2048]{2,1,0:T(2,128)(2,1)S(1)} %pad_maximum_fusion), channel_id=1, source_target_pairs={{0,4},{4,8},{8,12},{12,16},{16,20},{20,24},{24,28},{1,5},{5,9},{9,... | collective-permute-start | bytes 73736 | tf_op jit(solution)/shard_map/ppermute | solution.py:12
  3.2 1.1 %fusion.20 = (f32[3,1,2048]{2,1,0:T(1,128)S(1)}, f32[3,1,2048]{2,1,0:T(1,128)S(1)}, f32[3,1,2048]{2,1,0:T(1,128)S(1)}) fusion(f32[3,3,2048]{2,1,0:T(4,128)} %param.11), kind=kLoop, calls=%fused_computation.41 | loop fusion | bytes 147456 | tf_op jit(solution)/shard_map/slice | solution.py:47
  4.4 0.0 collective-permute-done
  4.4 1.8 %maximum_convert_fusion = f32[3,130,2048]{2,1,0:T(8,128)S(1)} fusion(bf16[1,128,2048]{2,1,0:T(8,128)(2,1)} %bitcast.27, bf16[1,128,2048]{2,1,0:T(8,128)(2,1)} %bitcast.29, bf16[1,128,2048]{2,1,0:T(8,128)(2,1)} %bitcast.31, bf16[3,2,2048]{2,1,0:T(2,128)(2,1)S(1)} %collective-permute-done), kind=kLoop, calls=%fused_computation.14 | loop fusion | flops 6389760 | bytes 4792320 | tf_op jit(solution)/shard_map/convert_element_type | solution.py:46
  6.3 0.9 %fusion.7 = f32[3,128,2048]{2,1,0:T(8,128)S(1)} fusion(f32[3,130,2048]{2,1,0:T(8,128)S(1)} %maximum_convert_fusion, f32[3,2048]{1,0:T(4,128)S(1)} %get-tuple-element.48, f32[3,2048]{1,0:T(4,128)S(1)} %get-tuple-element.49, f32[3,2048]{1,0:T(4,128)S(1)} %bitcast.32), kind=kLoop, calls=%fused_computation.10 | loop fusion | flops 3932160 | bytes 12656640 | tf_op jit(solution)/shard_map/add | solution.py:50
  7.2 0.0 copy-start.1
  7.2 0.1 fusion.12
  7.3 0.2 fusion.18
  7.6 0.5 copy-done.1
  8.1 0.0 copy-start.2
  8.1 3.0 %multiply_reduce_fusion = f32[2048,16]{0,1:T(8,128)S(1)} fusion(f32[2048,128]{0,1:T(8,128)S(1)} %get-tuple-element.42, f32[128]{0:T(128)S(1)} %iota_convert_fusion, f32[2048,16]{0,1:T(8,128)S(1)} %copy-done.1), kind=kLoop, calls=%fused_computation | loop fusion | flops 12550144 | bytes 1311232 | tf_op jit(solution)/shard_map/while/body/eval_jaxpr/sc,scm->cm/dot_general | solution.py:65
  11.1 0.1 fusion.19
  11.2 4.5 %collective-permute-start.1 = (f32[2048,16]{0,1:T(8,128)S(1)}, f32[2048,16]{0,1:T(8,128)S(1)}, u32[]{:S(2)}, u32[]{:S(2)}) collective-permute-start(f32[2048,16]{0,1:T(8,128)S(1)} %get-tuple-element.44), channel_id=1, source_target_pairs={{0,4},{4,8},{8,12},{12,16},{16,20},{20,24},{24,28},{1,5},{5,9},{9,... | collective-permute-start | bytes 393224 | tf_op jit(solution)/shard_map/ppermute | solution.py:12
  15.7 3.8 %collective-permute-start.2 = (f32[2048,16]{0,1:T(8,128)S(1)}, f32[2048,16]{0,1:T(8,128)S(1)}, u32[]{:S(2)}, u32[]{:S(2)}) collective-permute-start(f32[2048,16]{0,1:T(8,128)S(1)} %get-tuple-element.44), channel_id=1, source_target_pairs={{0,8},{4,12},{8,16},{12,20},{16,24},{20,28},{1,9},{5,13},{9,17},{1... | collective-permute-start | bytes 393224 | tf_op jit(solution)/shard_map/ppermute | solution.py:12
  19.5 4.3 %collective-permute-start.3 = (f32[2048,16]{0,1:T(8,128)S(1)}, f32[2048,16]{0,1:T(8,128)S(1)}, u32[]{:S(2)}, u32[]{:S(2)}) collective-permute-start(f32[2048,16]{0,1:T(8,128)S(1)} %get-tuple-element.44), channel_id=1, source_target_pairs={{0,12},{4,16},{8,20},{12,24},{16,28},{1,13},{5,17},{9,21},{13,25},... | collective-permute-start | bytes 393224 | tf_op jit(solution)/shard_map/ppermute | solution.py:12
  23.8 1.3 %collective-permute-start.4 = (f32[2048,16]{0,1:T(8,128)S(1)}, f32[2048,16]{0,1:T(8,128)S(1)}, u32[]{:S(2)}, u32[]{:S(2)}) collective-permute-start(f32[2048,16]{0,1:T(8,128)S(1)} %get-tuple-element.44), channel_id=1, source_target_pairs={{0,16},{4,20},{8,24},{12,28},{1,17},{5,21},{9,25},{13,29},{2,18},{... | collective-permute-start | bytes 393224 | tf_op jit(solution)/shard_map/ppermute | solution.py:12
  25.2 1.3 %collective-permute-start.5 = (f32[2048,16]{0,1:T(8,128)S(1)}, f32[2048,16]{0,1:T(8,128)S(1)}, u32[]{:S(2)}, u32[]{:S(2)}) collective-permute-start(f32[2048,16]{0,1:T(8,128)S(1)} %get-tuple-element.44), channel_id=1, source_target_pairs={{0,20},{4,24},{8,28},{1,21},{5,25},{9,29},{2,22},{6,26},{10,30},{3... | collective-permute-start | bytes 393224 | tf_op jit(solution)/shard_map/ppermute | solution.py:12
  26.5 0.0 collective-permute-done.1
  26.5 1.3 %collective-permute-start.6 = (f32[2048,16]{0,1:T(8,128)S(1)}, f32[2048,16]{0,1:T(8,128)S(1)}, u32[]{:S(2)}, u32[]{:S(2)}) collective-permute-start(f32[2048,16]{0,1:T(8,128)S(1)} %get-tuple-element.44), channel_id=1, source_target_pairs={{0,24},{4,28},{1,25},{5,29},{2,26},{6,30},{3,27},{7,31}} | collective-permute-start | bytes 393224 | tf_op jit(solution)/shard_map/ppermute | solution.py:12
  27.8 0.0 collective-permute-done.2
  27.8 1.5 %collective-permute-start.7 = (f32[2048,16]{0,1:T(8,128)S(1)}, f32[2048,16]{0,1:T(8,128)S(1)}, u32[]{:S(2)}, u32[]{:S(2)}) collective-permute-start(f32[2048,16]{0,1:T(8,128)S(1)} %get-tuple-element.44), channel_id=1, source_target_pairs={{0,28},{1,29},{2,30},{3,31}} | collective-permute-start | bytes 393224 | tf_op jit(solution)/shard_map/ppermute | solution.py:12
  29.3 0.0 copy-done.2
  29.3 16.0 %multiply_reduce_fusion.2 = f32[128,2048]{1,0:T(8,128)S(1)} fusion(f32[2048,16]{0,1:T(8,128)S(1)} %copy-done.2, f32[2048,16]{0,1:T(8,128)S(1)} %get-tuple-element.43, f32[128]{0:T(128)S(1)} %iota_convert_fusion, f32[128,2048]{1,0:T(8,128)S(1)} %get-tuple-element.41, f32[2048,16]{0,1:T(8,128)S(1)} %copy-done.1), kind=kOutput, calls=%fused_computation.2 | convolution fusion | flops 6467371008 | bytes 2490880 | tf_op jit(solution)/shard_map/ts,scm->tcm/dot_general | solution.py:72
  45.3 0.0 collective-permute-done.3
  45.3 0.0 collective-permute-done.4
  45.4 0.0 collective-permute-done.5
  45.4 0.0 collective-permute-done.6
  45.4 0.0 collective-permute-done.7
  45.4 0.2 add_multiply_fusion
  45.6 0.0 copy-start
  45.6 2.8 %multiply_reduce_fusion.1 = f32[128,2048]{1,0:T(8,128)S(1)} fusion(f32[2048,16]{0,1:T(8,128)S(1)} %add_multiply_fusion, f32[128]{0:T(128)S(1)} %broadcast_add_fusion, f32[2048,16]{0,1:T(8,128)S(1)} %get-tuple-element.43), kind=kLoop, calls=%fused_computation.1 | loop fusion | flops 12320768 | bytes 1311232 | tf_op jit(solution)/shard_map/reduce_sum | solution.py:90
  48.4 0.0 copy-done
  48.4 0.0 copy-start.3
  48.4 0.4 multiply_reduce_fusion.3
  48.8 1.6 %collective-permute-start.8 = (f32[128]{0:T(128)S(1)}, f32[128]{0:T(128)S(1)}, u32[]{:S(2)}, u32[]{:S(2)}) collective-permute-start(f32[128]{0:T(128)S(1)} %get-tuple-element.39), channel_id=1, source_target_pairs={{0,1},{1,0},{2,3},{3,2},{4,5},{5,4},{6,7},{7,6},{8,9},{9,8},{10,11... | collective-permute-start | bytes 1544 | tf_op jit(solution)/shard_map/ppermute | solution.py:35
  50.4 2.0 %collective-permute-done.8 = f32[128]{0:T(128)S(1)} collective-permute-done((f32[128]{0:T(128)S(1)}, f32[128]{0:T(128)S(1)}, u32[]{:S(2)}, u32[]{:S(2)}) %collective-permute-start.8) | collective-permute-done | bytes 544 | tf_op jit(solution)/shard_map/ppermute | solution.py:35
  52.4 2.6 %collective-permute-start.9 = (f32[128]{0:T(128)S(1)}, f32[128]{0:T(128)S(1)}, u32[]{:S(2)}, u32[]{:S(2)}) collective-permute-start(f32[128]{0:T(128)S(1)} %add.71), channel_id=1, source_target_pairs={{0,2},{1,3},{2,0},{3,1},{4,6},{5,7},{6,4},{7,5},{8,10},{9,11},{10,... | collective-permute-start | bytes 1544 | tf_op jit(solution)/shard_map/ppermute | solution.py:35
  55.0 1.9 %collective-permute-done.9 = f32[128]{0:T(128)S(1)} collective-permute-done((f32[128]{0:T(128)S(1)}, f32[128]{0:T(128)S(1)}, u32[]{:S(2)}, u32[]{:S(2)}) %collective-permute-start.9) | collective-permute-done | bytes 544 | tf_op jit(solution)/shard_map/ppermute | solution.py:35
  56.9 0.0 copy-done.3
  56.9 1.0 %multiply_convert_fusion = bf16[128,2048]{1,0:T(8,128)(2,1)} fusion(f32[128,2048]{1,0:T(8,128)S(1)} %get-tuple-element.40, f32[2048]{0:T(1024)S(1)} %copy-done.3, f32[128]{0:T(128)S(1)} %add_rsqrt_fusion), kind=kLoop, calls=%fused_computation.20 | loop fusion | flops 786432 | bytes 1581568 | tf_op jit(solution)/shard_map/convert_element_type | solution.py:95
  (6 shorter events, 0.1 us)
Async XLA Ops:
  0.8 3.6 %collective-permute-start = (bf16[3,2,2048]{2,1,0:T(2,128)(2,1)S(1)}, bf16[3,2,2048]{2,1,0:T(2,128)(2,1)S(1)}, u32[]{:S(2)}, u32[]{:S(2)}) collective-permute-start(bf16[3,2,2048]{2,1,0:T(2,128)(2,1)S(1)} %pad_maximum_fusion), channel_id=1, source_target_pairs={{0,4},{4,8},{8,12},{12,16},{16,20},{20,24},{24,28},{1,5},{5,9},{9,... | collective-permute-start | bytes 73736 | tf_op jit(solution)/shard_map/ppermute | solution.py:12
  7.2 0.9 %copy-start.1 = (f32[2048,16]{0,1:T(8,128)S(1)}, f32[2048,16]{0,1:T(8,128)}, u32[]{:S(2)}) copy-start(f32[2048,16]{0,1:T(8,128)} %param.12) | copy-start | bytes 393220
  8.1 21.2 %copy-start.2 = (f32[2048,16]{0,1:T(8,128)S(1)}, f32[2048,16]{0,1:T(8,128)}, u32[]{:S(2)}) copy-start(f32[2048,16]{0,1:T(8,128)} %param.13) | copy-start | bytes 393220
  11.2 15.3 %collective-permute-start.1 = (f32[2048,16]{0,1:T(8,128)S(1)}, f32[2048,16]{0,1:T(8,128)S(1)}, u32[]{:S(2)}, u32[]{:S(2)}) collective-permute-start(f32[2048,16]{0,1:T(8,128)S(1)} %get-tuple-element.44), channel_id=1, source_target_pairs={{0,4},{4,8},{8,12},{12,16},{16,20},{20,24},{24,28},{1,5},{5,9},{9,... | collective-permute-start | bytes 393224 | tf_op jit(solution)/shard_map/ppermute | solution.py:12
  15.7 12.1 %collective-permute-start.2 = (f32[2048,16]{0,1:T(8,128)S(1)}, f32[2048,16]{0,1:T(8,128)S(1)}, u32[]{:S(2)}, u32[]{:S(2)}) collective-permute-start(f32[2048,16]{0,1:T(8,128)S(1)} %get-tuple-element.44), channel_id=1, source_target_pairs={{0,8},{4,12},{8,16},{12,20},{16,24},{20,28},{1,9},{5,13},{9,17},{1... | collective-permute-start | bytes 393224 | tf_op jit(solution)/shard_map/ppermute | solution.py:12
  19.5 25.8 %collective-permute-start.3 = (f32[2048,16]{0,1:T(8,128)S(1)}, f32[2048,16]{0,1:T(8,128)S(1)}, u32[]{:S(2)}, u32[]{:S(2)}) collective-permute-start(f32[2048,16]{0,1:T(8,128)S(1)} %get-tuple-element.44), channel_id=1, source_target_pairs={{0,12},{4,16},{8,20},{12,24},{16,28},{1,13},{5,17},{9,21},{13,25},... | collective-permute-start | bytes 393224 | tf_op jit(solution)/shard_map/ppermute | solution.py:12
  23.8 21.5 %collective-permute-start.4 = (f32[2048,16]{0,1:T(8,128)S(1)}, f32[2048,16]{0,1:T(8,128)S(1)}, u32[]{:S(2)}, u32[]{:S(2)}) collective-permute-start(f32[2048,16]{0,1:T(8,128)S(1)} %get-tuple-element.44), channel_id=1, source_target_pairs={{0,16},{4,20},{8,24},{12,28},{1,17},{5,21},{9,25},{13,29},{2,18},{... | collective-permute-start | bytes 393224 | tf_op jit(solution)/shard_map/ppermute | solution.py:12
  25.2 20.2 %collective-permute-start.5 = (f32[2048,16]{0,1:T(8,128)S(1)}, f32[2048,16]{0,1:T(8,128)S(1)}, u32[]{:S(2)}, u32[]{:S(2)}) collective-permute-start(f32[2048,16]{0,1:T(8,128)S(1)} %get-tuple-element.44), channel_id=1, source_target_pairs={{0,20},{4,24},{8,28},{1,21},{5,25},{9,29},{2,22},{6,26},{10,30},{3... | collective-permute-start | bytes 393224 | tf_op jit(solution)/shard_map/ppermute | solution.py:12
  26.5 18.9 %collective-permute-start.6 = (f32[2048,16]{0,1:T(8,128)S(1)}, f32[2048,16]{0,1:T(8,128)S(1)}, u32[]{:S(2)}, u32[]{:S(2)}) collective-permute-start(f32[2048,16]{0,1:T(8,128)S(1)} %get-tuple-element.44), channel_id=1, source_target_pairs={{0,24},{4,28},{1,25},{5,29},{2,26},{6,30},{3,27},{7,31}} | collective-permute-start | bytes 393224 | tf_op jit(solution)/shard_map/ppermute | solution.py:12
  27.8 17.6 %collective-permute-start.7 = (f32[2048,16]{0,1:T(8,128)S(1)}, f32[2048,16]{0,1:T(8,128)S(1)}, u32[]{:S(2)}, u32[]{:S(2)}) collective-permute-start(f32[2048,16]{0,1:T(8,128)S(1)} %get-tuple-element.44), channel_id=1, source_target_pairs={{0,28},{1,29},{2,30},{3,31}} | collective-permute-start | bytes 393224 | tf_op jit(solution)/shard_map/ppermute | solution.py:12
  45.6 2.8 %copy-start = (bf16[128,2048]{1,0:T(8,128)(2,1)S(1)}, bf16[128,2048]{1,0:T(8,128)(2,1)}, u32[]{:S(2)}) copy-start(bf16[128,2048]{1,0:T(8,128)(2,1)} %param.14) | copy-start | bytes 1572868
  48.4 8.5 %copy-start.3 = (f32[2048]{0:T(1024)S(1)}, f32[2048]{0:T(1024)}, u32[]{:S(2)}) copy-start(f32[2048]{0:T(1024)} %param.15) | copy-start | bytes 24580
  48.8 3.6 %collective-permute-start.8 = (f32[128]{0:T(128)S(1)}, f32[128]{0:T(128)S(1)}, u32[]{:S(2)}, u32[]{:S(2)}) collective-permute-start(f32[128]{0:T(128)S(1)} %get-tuple-element.39), channel_id=1, source_target_pairs={{0,1},{1,0},{2,3},{3,2},{4,5},{5,4},{6,7},{7,6},{8,9},{9,8},{10,11... | collective-permute-start | bytes 1544 | tf_op jit(solution)/shard_map/ppermute | solution.py:35
  52.4 4.5 %collective-permute-start.9 = (f32[128]{0:T(128)S(1)}, f32[128]{0:T(128)S(1)}, u32[]{:S(2)}, u32[]{:S(2)}) collective-permute-start(f32[128]{0:T(128)S(1)} %add.71), channel_id=1, source_target_pairs={{0,2},{1,3},{2,0},{3,1},{4,6},{5,7},{6,4},{7,5},{8,10},{9,11},{10,... | collective-permute-start | bytes 1544 | tf_op jit(solution)/shard_map/ppermute | solution.py:35

commit v4 on v2

--- a/solution.py
+++ b/solution.py
@@ -75,7 +75,8 @@
 
     def local():
         if rows == block:
-            return main_step(zeros, values)[1]
+            running = jnp.cumsum(values[:, :, None] * grow, axis=0) * fade
+            return jnp.sum(running * residue[None, :, :], axis=2)
         return lax.scan(main_step, zeros, blocks)[1].reshape(rows, width)
 
     incoming, outputs = scan_in(ending, rate, rows, "ctx", local)

time: 56.4 us -> 53.5 us (0.949)
  other arithmetic: 25.6 us -> 22.6 us
    another operation x1, other arithmetic: 11.7 us -> 8.65 us  [local(): running = jnp.cumsum(values[:, :, None] * grow, axis=0) * fade]
  transfers between devices with their start and end apart: 10 -> 10, of which waited for: 2 -> 2; matrix products, arithmetic and copies ran while one was open for 23% -> 18% of each run, Pallas kernels for 0% -> 0%
where the time goes in v4:
time: 53.5 us; the launch traced here: 53.1 us
  starting transfers between devices  24.7 us (46%)
  other arithmetic  22.6 us (42%)
  waiting for transfers between devices  3.89 us (7%)
  local copies, waits for them, and re-layouts  1.73 us (3%)
    ppermute x8, starting transfers between devices, from_behind(): return lax.ppermute(block, axis, route)  20.4 us
    another operation x1, other arithmetic, local(): running = jnp.cumsum(values[:, :, None] * grow, axis=0) * fade  8.65 us
    reduce_sum x1, other arithmetic, per_device(): jnp.sum(jnp.exp(-rate[None, :, :] * times[:, None, None]) * weights[None,...  5.31 us
    ppermute x2, starting transfers between devices, butterfly_sum(): lax.ppermute(value, axis, [(i, i ^ step) for i in range(count)])  4.23 us
    ppermute x2, waiting for transfers between devices, butterfly_sum(): lax.ppermute(value, axis, [(i, i ^ step) for i in range(count)])  3.87 us
    dot_general x1, other arithmetic, end_step(): summed = jnp.einsum('sc,scm->cm', piece, grow)  3.07 us
    convert_element_type x1, other arithmetic, per_device(): padded = jnp.concatenate([before, stacked], axis=1).astype(jnp.float32)  1.85 us
    slice x1, local copies, waits for them, and re-layouts, per_device(): feats = short_filter[:, 0, None, :] * padded[:, taps - 1:, :]  1.12 us
  transfers between devices with their start and end apart: 10, of which 2 were waited for; matrix products, arithmetic and copies ran while one was open for 18% of the time, Pallas kernels for 0%

profile of v4, /device:TPU:0, one launch (start us, length us, event | category | flops | bytes accessed | tf_op | source)
XLA Modules:
  0.0 53.1 jit_solution(8022264352470101240)
XLA Ops:
  0.0 0.8 %pad_maximum_fusion = bf16[3,2,2048]{2,1,0:T(2,128)(2,1)S(1)} fusion(bf16[1,128,2048]{2,1,0:T(8,128)(2,1)} %bitcast.23, bf16[1,128,2048]{2,1,0:T(8,128)(2,1)} %bitcast.25, bf16[1,128,2048]{2,1,0:T(8,128)(2,1)} %bitcast.27), kind=kLoop, calls=%fused_computation.30 | loop fusion | flops 73728 | bytes 1597440 | tf_op jit(solution)/shard_map/stack | solution.py:43
  0.8 2.4 %collective-permute-start = (bf16[3,2,2048]{2,1,0:T(2,128)(2,1)S(1)}, bf16[3,2,2048]{2,1,0:T(2,128)(2,1)S(1)}, u32[]{:S(2)}, u32[]{:S(2)}) collective-permute-start(bf16[3,2,2048]{2,1,0:T(2,128)(2,1)S(1)} %pad_maximum_fusion), channel_id=1, source_target_pairs={{0,4},{4,8},{8,12},{12,16},{16,20},{20,24},{24,28},{1,5},{5,9},{9,... | collective-permute-start | bytes 73736 | tf_op jit(solution)/shard_map/ppermute | solution.py:12
  3.2 1.1 %fusion.14 = (f32[3,1,2048]{2,1,0:T(1,128)S(1)}, f32[3,1,2048]{2,1,0:T(1,128)S(1)}, f32[3,1,2048]{2,1,0:T(1,128)S(1)}) fusion(f32[3,3,2048]{2,1,0:T(4,128)} %param.11), kind=kLoop, calls=%fused_computation.37 | loop fusion | bytes 147456 | tf_op jit(solution)/shard_map/slice | solution.py:47
  4.4 0.0 collective-permute-done
  4.4 1.8 %maximum_convert_fusion = f32[3,130,2048]{2,1,0:T(8,128)S(1)} fusion(bf16[1,128,2048]{2,1,0:T(8,128)(2,1)} %bitcast.24, bf16[1,128,2048]{2,1,0:T(8,128)(2,1)} %bitcast.26, bf16[1,128,2048]{2,1,0:T(8,128)(2,1)} %bitcast.28, bf16[3,2,2048]{2,1,0:T(2,128)(2,1)S(1)} %collective-permute-done), kind=kLoop, calls=%fused_computation.14 | loop fusion | flops 6389760 | bytes 4792320 | tf_op jit(solution)/shard_map/convert_element_type | solution.py:46
  6.3 0.9 %fusion.5 = f32[3,128,2048]{2,1,0:T(8,128)S(1)} fusion(f32[3,130,2048]{2,1,0:T(8,128)S(1)} %maximum_convert_fusion, f32[3,2048]{1,0:T(4,128)S(1)} %get-tuple-element.48, f32[3,2048]{1,0:T(4,128)S(1)} %get-tuple-element.49, f32[3,2048]{1,0:T(4,128)S(1)} %bitcast.29), kind=kLoop, calls=%fused_computation.10 | loop fusion | flops 3932160 | bytes 12656640 | tf_op jit(solution)/shard_map/add | solution.py:50
  7.2 0.0 copy-start.1
  7.2 0.1 fusion.10
  7.3 0.2 fusion.12
  7.6 0.5 %copy-done.1 = f32[2048,16]{0,1:T(8,128)S(1)} copy-done((f32[2048,16]{0,1:T(8,128)S(1)}, f32[2048,16]{0,1:T(8,128)}, u32[]{:S(2)}) %copy-start.1) | copy-done | bytes 131096
  8.1 0.0 copy-start.2
  8.1 3.1 %multiply_reduce_fusion = f32[2048,16]{0,1:T(8,128)S(1)} fusion(f32[2048,128]{0,1:T(8,128)S(1)} %get-tuple-element.42, f32[128]{0:T(128)S(1)} %iota_convert_fusion, f32[2048,16]{0,1:T(8,128)S(1)} %copy-done.1), kind=kLoop, calls=%fused_computation | loop fusion | flops 12550144 | bytes 1311232 | tf_op jit(solution)/shard_map/while/body/eval_jaxpr/sc,scm->cm/dot_general | solution.py:65
  11.2 0.1 fusion.13
  11.3 4.5 %collective-permute-start.1 = (f32[2048,16]{0,1:T(8,128)S(1)}, f32[2048,16]{0,1:T(8,128)S(1)}, u32[]{:S(2)}, u32[]{:S(2)}) collective-permute-start(f32[2048,16]{0,1:T(8,128)S(1)} %get-tuple-element.44), channel_id=1, source_target_pairs={{0,4},{4,8},{8,12},{12,16},{16,20},{20,24},{24,28},{1,5},{5,9},{9,... | collective-permute-start | bytes 393224 | tf_op jit(solution)/shard_map/ppermute | solution.py:12
  15.8 3.8 %collective-permute-start.2 = (f32[2048,16]{0,1:T(8,128)S(1)}, f32[2048,16]{0,1:T(8,128)S(1)}, u32[]{:S(2)}, u32[]{:S(2)}) collective-permute-start(f32[2048,16]{0,1:T(8,128)S(1)} %get-tuple-element.44), channel_id=1, source_target_pairs={{0,8},{4,12},{8,16},{12,20},{16,24},{20,28},{1,9},{5,13},{9,17},{1... | collective-permute-start | bytes 393224 | tf_op jit(solution)/shard_map/ppermute | solution.py:12
  19.6 4.3 %collective-permute-start.3 = (f32[2048,16]{0,1:T(8,128)S(1)}, f32[2048,16]{0,1:T(8,128)S(1)}, u32[]{:S(2)}, u32[]{:S(2)}) collective-permute-start(f32[2048,16]{0,1:T(8,128)S(1)} %get-tuple-element.44), channel_id=1, source_target_pairs={{0,12},{4,16},{8,20},{12,24},{16,28},{1,13},{5,17},{9,21},{13,25},... | collective-permute-start | bytes 393224 | tf_op jit(solution)/shard_map/ppermute | solution.py:12
  23.9 1.3 %collective-permute-start.4 = (f32[2048,16]{0,1:T(8,128)S(1)}, f32[2048,16]{0,1:T(8,128)S(1)}, u32[]{:S(2)}, u32[]{:S(2)}) collective-permute-start(f32[2048,16]{0,1:T(8,128)S(1)} %get-tuple-element.44), channel_id=1, source_target_pairs={{0,16},{4,20},{8,24},{12,28},{1,17},{5,21},{9,25},{13,29},{2,18},{... | collective-permute-start | bytes 393224 | tf_op jit(solution)/shard_map/ppermute | solution.py:12
  25.2 1.3 %collective-permute-start.5 = (f32[2048,16]{0,1:T(8,128)S(1)}, f32[2048,16]{0,1:T(8,128)S(1)}, u32[]{:S(2)}, u32[]{:S(2)}) collective-permute-start(f32[2048,16]{0,1:T(8,128)S(1)} %get-tuple-element.44), channel_id=1, source_target_pairs={{0,20},{4,24},{8,28},{1,21},{5,25},{9,29},{2,22},{6,26},{10,30},{3... | collective-permute-start | bytes 393224 | tf_op jit(solution)/shard_map/ppermute | solution.py:12
  26.6 0.0 collective-permute-done.1
  26.6 1.3 %collective-permute-start.6 = (f32[2048,16]{0,1:T(8,128)S(1)}, f32[2048,16]{0,1:T(8,128)S(1)}, u32[]{:S(2)}, u32[]{:S(2)}) collective-permute-start(f32[2048,16]{0,1:T(8,128)S(1)} %get-tuple-element.44), channel_id=1, source_target_pairs={{0,24},{4,28},{1,25},{5,29},{2,26},{6,30},{3,27},{7,31}} | collective-permute-start | bytes 393224 | tf_op jit(solution)/shard_map/ppermute | solution.py:12
  27.9 0.0 collective-permute-done.2
  27.9 1.5 %collective-permute-start.7 = (f32[2048,16]{0,1:T(8,128)S(1)}, f32[2048,16]{0,1:T(8,128)S(1)}, u32[]{:S(2)}, u32[]{:S(2)}) collective-permute-start(f32[2048,16]{0,1:T(8,128)S(1)} %get-tuple-element.44), channel_id=1, source_target_pairs={{0,28},{1,29},{2,30},{3,31}} | collective-permute-start | bytes 393224 | tf_op jit(solution)/shard_map/ppermute | solution.py:12
  29.4 0.0 copy-done.2
  29.4 8.7 %multiply_reduce_fusion.2 = f32[128,2048]{1,0:T(8,128)S(1)} fusion(f32[2048,16]{0,1:T(8,128)S(1)} %copy-done.2, f32[2048,16]{0,1:T(8,128)S(1)} %get-tuple-element.43, f32[128]{0:T(128)S(1)} %iota_convert_fusion, f32[128,2048]{1,0:T(8,128)S(1)} %get-tuple-element.41, f32[2048,16]{0,1:T(8,128)S(1)} %copy-done.1), kind=kOutput, calls=%fused_computation.2 | output fusion | flops 557580288 | bytes 2490880 | tf_op jit(solution)/shard_map/jit(cumsum)/reduce_window_sum | solution.py:78
  38.0 0.0 collective-permute-done.3
  38.0 0.0 collective-permute-done.4
  38.1 0.0 collective-permute-done.5
  38.1 0.0 collective-permute-done.6
  38.1 0.0 collective-permute-done.7
  38.1 0.2 add_multiply_fusion
  38.3 0.0 copy-start
  38.3 5.3 %multiply_reduce_fusion.1 = f32[128,2048]{1,0:T(8,128)S(1)} fusion(f32[2048,16]{0,1:T(8,128)S(1)} %add_multiply_fusion, f32[128]{0:T(128)S(1)} %broadcast_add_fusion, f32[2048,16]{0,1:T(8,128)S(1)} %get-tuple-element.43), kind=kLoop, calls=%fused_computation.1 | loop fusion | flops 12320768 | bytes 1311232 | tf_op jit(solution)/shard_map/reduce_sum | solution.py:85
  43.6 0.0 copy-done
  43.6 0.0 copy-start.3
  43.6 0.4 multiply_reduce_fusion.3
  44.0 1.6 %collective-permute-start.8 = (f32[128]{0:T(128)S(1)}, f32[128]{0:T(128)S(1)}, u32[]{:S(2)}, u32[]{:S(2)}) collective-permute-start(f32[128]{0:T(128)S(1)} %get-tuple-element.39), channel_id=1, source_target_pairs={{0,1},{1,0},{2,3},{3,2},{4,5},{5,4},{6,7},{7,6},{8,9},{9,8},{10,11... | collective-permute-start | bytes 1544 | tf_op jit(solution)/shard_map/ppermute | solution.py:35
  45.7 2.0 %collective-permute-done.8 = f32[128]{0:T(128)S(1)} collective-permute-done((f32[128]{0:T(128)S(1)}, f32[128]{0:T(128)S(1)}, u32[]{:S(2)}, u32[]{:S(2)}) %collective-permute-start.8) | collective-permute-done | bytes 544 | tf_op jit(solution)/shard_map/ppermute | solution.py:35
  47.7 2.6 %collective-permute-start.9 = (f32[128]{0:T(128)S(1)}, f32[128]{0:T(128)S(1)}, u32[]{:S(2)}, u32[]{:S(2)}) collective-permute-start(f32[128]{0:T(128)S(1)} %add.71), channel_id=1, source_target_pairs={{0,2},{1,3},{2,0},{3,1},{4,6},{5,7},{6,4},{7,5},{8,10},{9,11},{10,... | collective-permute-start | bytes 1544 | tf_op jit(solution)/shard_map/ppermute | solution.py:35
  50.3 1.9 %collective-permute-done.9 = f32[128]{0:T(128)S(1)} collective-permute-done((f32[128]{0:T(128)S(1)}, f32[128]{0:T(128)S(1)}, u32[]{:S(2)}, u32[]{:S(2)}) %collective-permute-start.9) | collective-permute-done | bytes 544 | tf_op jit(solution)/shard_map/ppermute | solution.py:35
  52.2 0.0 copy-done.3
  52.2 1.0 %multiply_convert_fusion = bf16[128,2048]{1,0:T(8,128)(2,1)} fusion(f32[128,2048]{1,0:T(8,128)S(1)} %get-tuple-element.40, f32[2048]{0:T(1024)S(1)} %copy-done.3, f32[128]{0:T(128)S(1)} %add_rsqrt_fusion), kind=kLoop, calls=%fused_computation.20 | loop fusion | flops 786432 | bytes 1581568 | tf_op jit(solution)/shard_map/convert_element_type | solution.py:90
  (6 shorter events, 0.1 us)
Async XLA Ops:
  0.8 3.6 %collective-permute-start = (bf16[3,2,2048]{2,1,0:T(2,128)(2,1)S(1)}, bf16[3,2,2048]{2,1,0:T(2,128)(2,1)S(1)}, u32[]{:S(2)}, u32[]{:S(2)}) collective-permute-start(bf16[3,2,2048]{2,1,0:T(2,128)(2,1)S(1)} %pad_maximum_fusion), channel_id=1, source_target_pairs={{0,4},{4,8},{8,12},{12,16},{16,20},{20,24},{24,28},{1,5},{5,9},{9,... | collective-permute-start | bytes 73736 | tf_op jit(solution)/shard_map/ppermute | solution.py:12
  7.2 0.9 %copy-start.1 = (f32[2048,16]{0,1:T(8,128)S(1)}, f32[2048,16]{0,1:T(8,128)}, u32[]{:S(2)}) copy-start(f32[2048,16]{0,1:T(8,128)} %param.12) | copy-start | bytes 393220
  8.1 21.3 %copy-start.2 = (f32[2048,16]{0,1:T(8,128)S(1)}, f32[2048,16]{0,1:T(8,128)}, u32[]{:S(2)}) copy-start(f32[2048,16]{0,1:T(8,128)} %param.13) | copy-start | bytes 393220
  11.3 15.3 %collective-permute-start.1 = (f32[2048,16]{0,1:T(8,128)S(1)}, f32[2048,16]{0,1:T(8,128)S(1)}, u32[]{:S(2)}, u32[]{:S(2)}) collective-permute-start(f32[2048,16]{0,1:T(8,128)S(1)} %get-tuple-element.44), channel_id=1, source_target_pairs={{0,4},{4,8},{8,12},{12,16},{16,20},{20,24},{24,28},{1,5},{5,9},{9,... | collective-permute-start | bytes 393224 | tf_op jit(solution)/shard_map/ppermute | solution.py:12
  15.8 12.1 %collective-permute-start.2 = (f32[2048,16]{0,1:T(8,128)S(1)}, f32[2048,16]{0,1:T(8,128)S(1)}, u32[]{:S(2)}, u32[]{:S(2)}) collective-permute-start(f32[2048,16]{0,1:T(8,128)S(1)} %get-tuple-element.44), channel_id=1, source_target_pairs={{0,8},{4,12},{8,16},{12,20},{16,24},{20,28},{1,9},{5,13},{9,17},{1... | collective-permute-start | bytes 393224 | tf_op jit(solution)/shard_map/ppermute | solution.py:12
  19.6 18.4 %collective-permute-start.3 = (f32[2048,16]{0,1:T(8,128)S(1)}, f32[2048,16]{0,1:T(8,128)S(1)}, u32[]{:S(2)}, u32[]{:S(2)}) collective-permute-start(f32[2048,16]{0,1:T(8,128)S(1)} %get-tuple-element.44), channel_id=1, source_target_pairs={{0,12},{4,16},{8,20},{12,24},{16,28},{1,13},{5,17},{9,21},{13,25},... | collective-permute-start | bytes 393224 | tf_op jit(solution)/shard_map/ppermute | solution.py:12
  23.9 14.1 %collective-permute-start.4 = (f32[2048,16]{0,1:T(8,128)S(1)}, f32[2048,16]{0,1:T(8,128)S(1)}, u32[]{:S(2)}, u32[]{:S(2)}) collective-permute-start(f32[2048,16]{0,1:T(8,128)S(1)} %get-tuple-element.44), channel_id=1, source_target_pairs={{0,16},{4,20},{8,24},{12,28},{1,17},{5,21},{9,25},{13,29},{2,18},{... | collective-permute-start | bytes 393224 | tf_op jit(solution)/shard_map/ppermute | solution.py:12
  25.2 12.8 %collective-permute-start.5 = (f32[2048,16]{0,1:T(8,128)S(1)}, f32[2048,16]{0,1:T(8,128)S(1)}, u32[]{:S(2)}, u32[]{:S(2)}) collective-permute-start(f32[2048,16]{0,1:T(8,128)S(1)} %get-tuple-element.44), channel_id=1, source_target_pairs={{0,20},{4,24},{8,28},{1,21},{5,25},{9,29},{2,22},{6,26},{10,30},{3... | collective-permute-start | bytes 393224 | tf_op jit(solution)/shard_map/ppermute | solution.py:12
  26.6 11.5 %collective-permute-start.6 = (f32[2048,16]{0,1:T(8,128)S(1)}, f32[2048,16]{0,1:T(8,128)S(1)}, u32[]{:S(2)}, u32[]{:S(2)}) collective-permute-start(f32[2048,16]{0,1:T(8,128)S(1)} %get-tuple-element.44), channel_id=1, source_target_pairs={{0,24},{4,28},{1,25},{5,29},{2,26},{6,30},{3,27},{7,31}} | collective-permute-start | bytes 393224 | tf_op jit(solution)/shard_map/ppermute | solution.py:12
  27.9 10.2 %collective-permute-start.7 = (f32[2048,16]{0,1:T(8,128)S(1)}, f32[2048,16]{0,1:T(8,128)S(1)}, u32[]{:S(2)}, u32[]{:S(2)}) collective-permute-start(f32[2048,16]{0,1:T(8,128)S(1)} %get-tuple-element.44), channel_id=1, source_target_pairs={{0,28},{1,29},{2,30},{3,31}} | collective-permute-start | bytes 393224 | tf_op jit(solution)/shard_map/ppermute | solution.py:12
  38.3 5.3 %copy-start = (bf16[128,2048]{1,0:T(8,128)(2,1)S(1)}, bf16[128,2048]{1,0:T(8,128)(2,1)}, u32[]{:S(2)}) copy-start(bf16[128,2048]{1,0:T(8,128)(2,1)} %param.14) | copy-start | bytes 1572868
  43.6 8.6 %copy-start.3 = (f32[2048]{0:T(1024)S(1)}, f32[2048]{0:T(1024)}, u32[]{:S(2)}) copy-start(f32[2048]{0:T(1024)} %param.15) | copy-start | bytes 24580
  44.0 3.6 %collective-permute-start.8 = (f32[128]{0:T(128)S(1)}, f32[128]{0:T(128)S(1)}, u32[]{:S(2)}, u32[]{:S(2)}) collective-permute-start(f32[128]{0:T(128)S(1)} %get-tuple-element.39), channel_id=1, source_target_pairs={{0,1},{1,0},{2,3},{3,2},{4,5},{5,4},{6,7},{7,6},{8,9},{9,8},{10,11... | collective-permute-start | bytes 1544 | tf_op jit(solution)/shard_map/ppermute | solution.py:35
  47.7 4.5 %collective-permute-start.9 = (f32[128]{0:T(128)S(1)}, f32[128]{0:T(128)S(1)}, u32[]{:S(2)}, u32[]{:S(2)}) collective-permute-start(f32[128]{0:T(128)S(1)} %add.71), channel_id=1, source_target_pairs={{0,2},{1,3},{2,0},{3,1},{4,6},{5,7},{6,4},{7,5},{8,10},{9,11},{10,... | collective-permute-start | bytes 1544 | tf_op jit(solution)/shard_map/ppermute | solution.py:35

commit v5 on v2

--- a/solution.py
+++ b/solution.py
@@ -54,34 +54,37 @@
     values = lax.optimization_barrier(gated).astype(jnp.float32)
     block = min(128, rows)
     blocks = values.reshape(rows // block, block, width)
+    decay = rate.T
+    weight = residue.T
     offsets = jnp.arange(block, dtype=jnp.int32).astype(jnp.float32)
-    grow = jnp.exp(rate[None, :, :] * offsets[:, None, None])
-    fade = jnp.exp(-rate[None, :, :] * offsets[:, None, None])
-    enter = jnp.exp(-rate[None, :, :] * (offsets[:, None, None] + 1.0))
-    last_fade = jnp.exp(-rate * (block - 1))
-    block_decay = jnp.exp(-rate * block)
+    grow = jnp.exp(decay[:, None, :] * offsets[None, :, None])
+    fade = jnp.exp(-decay[:, None, :] * offsets[None, :, None])
+    enter = jnp.exp(-decay[:, None, :] * (offsets[None, :, None] + 1.0))
+    last_fade = jnp.exp(-decay * (block - 1))
+    block_decay = jnp.exp(-decay * block)
 
     def end_step(state, piece):
-        summed = jnp.einsum("sc,scm->cm", piece, grow)
+        summed = jnp.einsum("sc,msc->mc", piece, grow)
         return (state * block_decay + last_fade * summed, None)
 
-    zeros = jnp.zeros(rate.shape, jnp.float32)
+    zeros = jnp.zeros(decay.shape, jnp.float32)
     ending, unused = lax.scan(end_step, zeros, blocks)
 
     def main_step(state, piece):
-        running = jnp.cumsum(piece[:, :, None] * grow, axis=0) * fade
-        states = running + enter * state[None, :, :]
-        return (states[-1], jnp.sum(states * residue[None, :, :], axis=2))
+        running = jnp.cumsum(piece[None, :, :] * grow, axis=1) * fade
+        states = running + enter * state[:, None, :]
+        return (states[:, -1, :], jnp.sum(states * weight[:, None, :], axis=0))
 
     def local():
         if rows == block:
-            return main_step(zeros, values)[1]
+            running = jnp.cumsum(values[None, :, :] * grow, axis=1) * fade
+            return jnp.sum(running * weight[:, None, :], axis=0)
         return lax.scan(main_step, zeros, blocks)[1].reshape(rows, width)
 
-    incoming, outputs = scan_in(ending, rate, rows, "ctx", local)
+    incoming, outputs = scan_in(ending, decay, rows, "ctx", local)
     times = jnp.arange(rows, dtype=jnp.int32).astype(jnp.float32) + 1.0
-    weights = residue * incoming
-    mixed_in = jnp.sum(jnp.exp(-rate[None, :, :] * times[:, None, None]) * weights[None, :, :], axis=2)
+    weights = weight * incoming
+    mixed_in = jnp.sum(jnp.exp(-decay[:, None, :] * times[None, :, None]) * weights[:, None, :], axis=0)
     mixed = outputs + mixed_in
     stream = resid.astype(jnp.float32) + q_feat * mixed
     squares = butterfly_sum(jnp.sum(stream * stream, axis=1), "tp")

time: 56.4 us -> 53.5 us (0.949)
  other arithmetic: 25.6 us -> 22.6 us
    another operation x1, other arithmetic: 11.7 us -> 8.65 us  [local(): running = jnp.cumsum(values[None, :, :] * grow, axis=1) * fade]
  transfers between devices with their start and end apart: 10 -> 10, of which waited for: 2 -> 2; matrix products, arithmetic and copies ran while one was open for 23% -> 18% of each run, Pallas kernels for 0% -> 0%
where the time goes in v5:
time: 53.5 us; the launch traced here: 53.1 us
  starting transfers between devices  24.7 us (46%)
  other arithmetic  22.6 us (42%)
  waiting for transfers between devices  3.89 us (7%)
  local copies, waits for them, and re-layouts  1.73 us (3%)
    ppermute x8, starting transfers between devices, from_behind(): return lax.ppermute(block, axis, route)  20.4 us
    another operation x1, other arithmetic, local(): running = jnp.cumsum(values[None, :, :] * grow, axis=1) * fade  8.65 us
    reduce_sum x1, other arithmetic, per_device(): jnp.sum(jnp.exp(-decay[:, None, :] * times[None, :, None]) * weights[:, N...  5.31 us
    ppermute x2, starting transfers between devices, butterfly_sum(): lax.ppermute(value, axis, [(i, i ^ step) for i in range(count)])  4.23 us
    ppermute x2, waiting for transfers between devices, butterfly_sum(): lax.ppermute(value, axis, [(i, i ^ step) for i in range(count)])  3.87 us
    dot_general x1, other arithmetic, end_step(): summed = jnp.einsum('sc,msc->mc', piece, grow)  3.07 us
    convert_element_type x1, other arithmetic, per_device(): padded = jnp.concatenate([before, stacked], axis=1).astype(jnp.float32)  1.85 us
    slice x1, local copies, waits for them, and re-layouts, per_device(): feats = short_filter[:, 0, None, :] * padded[:, taps - 1:, :]  1.12 us
  transfers between devices with their start and end apart: 10, of which 2 were waited for; matrix products, arithmetic and copies ran while one was open for 18% of the time, Pallas kernels for 0%

profile of v5, /device:TPU:0, one launch (start us, length us, event | category | flops | bytes accessed | tf_op | source)
XLA Modules:
  0.0 53.1 jit_solution(1241140089930268847)
XLA Ops:
  0.0 0.8 %pad_maximum_fusion = bf16[3,2,2048]{2,1,0:T(2,128)(2,1)S(1)} fusion(bf16[1,128,2048]{2,1,0:T(8,128)(2,1)} %bitcast.35, bf16[1,128,2048]{2,1,0:T(8,128)(2,1)} %bitcast.37, bf16[1,128,2048]{2,1,0:T(8,128)(2,1)} %bitcast.39), kind=kLoop, calls=%fused_computation.31 | loop fusion | flops 73728 | bytes 1597440 | tf_op jit(solution)/shard_map/stack | solution.py:43
  0.8 2.4 %collective-permute-start = (bf16[3,2,2048]{2,1,0:T(2,128)(2,1)S(1)}, bf16[3,2,2048]{2,1,0:T(2,128)(2,1)S(1)}, u32[]{:S(2)}, u32[]{:S(2)}) collective-permute-start(bf16[3,2,2048]{2,1,0:T(2,128)(2,1)S(1)} %pad_maximum_fusion), channel_id=1, source_target_pairs={{0,4},{4,8},{8,12},{12,16},{16,20},{20,24},{24,28},{1,5},{5,9},{9,... | collective-permute-start | bytes 73736 | tf_op jit(solution)/shard_map/ppermute | solution.py:12
  3.2 1.1 %fusion.14 = (f32[3,1,2048]{2,1,0:T(1,128)S(1)}, f32[3,1,2048]{2,1,0:T(1,128)S(1)}, f32[3,1,2048]{2,1,0:T(1,128)S(1)}) fusion(f32[3,3,2048]{2,1,0:T(4,128)} %param.11), kind=kLoop, calls=%fused_computation.38 | loop fusion | bytes 147456 | tf_op jit(solution)/shard_map/slice | solution.py:47
  4.4 0.0 collective-permute-done
  4.4 1.8 %maximum_convert_fusion = f32[3,130,2048]{2,1,0:T(8,128)S(1)} fusion(bf16[1,128,2048]{2,1,0:T(8,128)(2,1)} %bitcast.36, bf16[1,128,2048]{2,1,0:T(8,128)(2,1)} %bitcast.38, bf16[1,128,2048]{2,1,0:T(8,128)(2,1)} %bitcast.40, bf16[3,2,2048]{2,1,0:T(2,128)(2,1)S(1)} %collective-permute-done), kind=kLoop, calls=%fused_computation.14 | loop fusion | flops 6389760 | bytes 4792320 | tf_op jit(solution)/shard_map/convert_element_type | solution.py:46
  6.3 0.9 %fusion.5 = f32[3,128,2048]{2,1,0:T(8,128)S(1)} fusion(f32[3,130,2048]{2,1,0:T(8,128)S(1)} %maximum_convert_fusion, f32[3,2048]{1,0:T(4,128)S(1)} %get-tuple-element.48, f32[3,2048]{1,0:T(4,128)S(1)} %get-tuple-element.49, f32[3,2048]{1,0:T(4,128)S(1)} %bitcast.43), kind=kLoop, calls=%fused_computation.10 | loop fusion | flops 3932160 | bytes 12656640 | tf_op jit(solution)/shard_map/add | solution.py:50
  7.2 0.0 copy-start.1
  7.2 0.1 fusion.10
  7.3 0.2 fusion.13
  7.6 0.5 %copy-done.1 = f32[2048,16]{0,1:T(8,128)S(1)} copy-done((f32[2048,16]{0,1:T(8,128)S(1)}, f32[2048,16]{0,1:T(8,128)}, u32[]{:S(2)}) %copy-start.1) | copy-done | bytes 131096
  8.1 0.0 copy-start.2
  8.1 3.1 %multiply_reduce_fusion = f32[2048,16]{0,1:T(8,128)S(1)} fusion(f32[2048,128]{0,1:T(8,128)S(1)} %get-tuple-element.42, f32[128]{0:T(128)S(1)} %iota_convert_fusion, f32[16,2048]{1,0:T(8,128)S(1)} %bitcast.41), kind=kLoop, calls=%fused_computation | loop fusion | flops 12550144 | bytes 1311232 | tf_op jit(solution)/shard_map/while/body/eval_jaxpr/sc,msc->mc/dot_general | solution.py:67
  11.2 0.1 bitcast_negate_fusion
  11.3 4.5 %collective-permute-start.1 = (f32[16,2048]{1,0:T(8,128)S(1)}, f32[16,2048]{1,0:T(8,128)S(1)}, u32[]{:S(2)}, u32[]{:S(2)}) collective-permute-start(f32[16,2048]{1,0:T(8,128)S(1)} %get-tuple-element.44), channel_id=1, source_target_pairs={{0,4},{4,8},{8,12},{12,16},{16,20},{20,24},{24,28},{1,5},{5,9},{9,... | collective-permute-start | bytes 393224 | tf_op jit(solution)/shard_map/ppermute | solution.py:12
  15.8 3.8 %collective-permute-start.2 = (f32[16,2048]{1,0:T(8,128)S(1)}, f32[16,2048]{1,0:T(8,128)S(1)}, u32[]{:S(2)}, u32[]{:S(2)}) collective-permute-start(f32[16,2048]{1,0:T(8,128)S(1)} %get-tuple-element.44), channel_id=1, source_target_pairs={{0,8},{4,12},{8,16},{12,20},{16,24},{20,28},{1,9},{5,13},{9,17},{1... | collective-permute-start | bytes 393224 | tf_op jit(solution)/shard_map/ppermute | solution.py:12
  19.6 4.3 %collective-permute-start.3 = (f32[16,2048]{1,0:T(8,128)S(1)}, f32[16,2048]{1,0:T(8,128)S(1)}, u32[]{:S(2)}, u32[]{:S(2)}) collective-permute-start(f32[16,2048]{1,0:T(8,128)S(1)} %get-tuple-element.44), channel_id=1, source_target_pairs={{0,12},{4,16},{8,20},{12,24},{16,28},{1,13},{5,17},{9,21},{13,25},... | collective-permute-start | bytes 393224 | tf_op jit(solution)/shard_map/ppermute | solution.py:12
  23.9 1.3 %collective-permute-start.4 = (f32[16,2048]{1,0:T(8,128)S(1)}, f32[16,2048]{1,0:T(8,128)S(1)}, u32[]{:S(2)}, u32[]{:S(2)}) collective-permute-start(f32[16,2048]{1,0:T(8,128)S(1)} %get-tuple-element.44), channel_id=1, source_target_pairs={{0,16},{4,20},{8,24},{12,28},{1,17},{5,21},{9,25},{13,29},{2,18},{... | collective-permute-start | bytes 393224 | tf_op jit(solution)/shard_map/ppermute | solution.py:12
  25.2 1.3 %collective-permute-start.5 = (f32[16,2048]{1,0:T(8,128)S(1)}, f32[16,2048]{1,0:T(8,128)S(1)}, u32[]{:S(2)}, u32[]{:S(2)}) collective-permute-start(f32[16,2048]{1,0:T(8,128)S(1)} %get-tuple-element.44), channel_id=1, source_target_pairs={{0,20},{4,24},{8,28},{1,21},{5,25},{9,29},{2,22},{6,26},{10,30},{3... | collective-permute-start | bytes 393224 | tf_op jit(solution)/shard_map/ppermute | solution.py:12
  26.6 0.0 collective-permute-done.1
  26.6 1.3 %collective-permute-start.6 = (f32[16,2048]{1,0:T(8,128)S(1)}, f32[16,2048]{1,0:T(8,128)S(1)}, u32[]{:S(2)}, u32[]{:S(2)}) collective-permute-start(f32[16,2048]{1,0:T(8,128)S(1)} %get-tuple-element.44), channel_id=1, source_target_pairs={{0,24},{4,28},{1,25},{5,29},{2,26},{6,30},{3,27},{7,31}} | collective-permute-start | bytes 393224 | tf_op jit(solution)/shard_map/ppermute | solution.py:12
  27.9 0.0 collective-permute-done.2
  27.9 1.5 %collective-permute-start.7 = (f32[16,2048]{1,0:T(8,128)S(1)}, f32[16,2048]{1,0:T(8,128)S(1)}, u32[]{:S(2)}, u32[]{:S(2)}) collective-permute-start(f32[16,2048]{1,0:T(8,128)S(1)} %get-tuple-element.44), channel_id=1, source_target_pairs={{0,28},{1,29},{2,30},{3,31}} | collective-permute-start | bytes 393224 | tf_op jit(solution)/shard_map/ppermute | solution.py:12
  29.4 0.0 copy-done.2
  29.4 8.7 %multiply_reduce_fusion.2 = f32[128,2048]{1,0:T(8,128)S(1)} fusion(f32[16,2048]{1,0:T(8,128)S(1)} %bitcast.44, f32[16,2048]{1,0:T(8,128)S(1)} %get-tuple-element.43, f32[128]{0:T(128)S(1)} %iota_convert_fusion, f32[128,2048]{1,0:T(8,128)S(1)} %get-tuple-element.41, f32[16,2048]{1,0:T(8,128)S(1)} %bitcast.42), kind=kOutput, calls=%fused_computation.2 | output fusion | flops 557580288 | bytes 2490880 | tf_op jit(solution)/shard_map/jit(cumsum)/reduce_window_sum | solution.py:80
  38.0 0.0 collective-permute-done.3
  38.0 0.0 collective-permute-done.4
  38.1 0.0 collective-permute-done.5
  38.1 0.0 collective-permute-done.6
  38.1 0.0 collective-permute-done.7
  38.1 0.2 add_multiply_fusion
  38.3 0.0 copy-start
  38.3 5.3 %multiply_reduce_fusion.1 = f32[128,2048]{1,0:T(8,128)S(1)} fusion(f32[16,2048]{1,0:T(8,128)S(1)} %add_multiply_fusion, f32[128]{0:T(128)S(1)} %broadcast_add_fusion, f32[16,2048]{1,0:T(8,128)S(1)} %get-tuple-element.43), kind=kLoop, calls=%fused_computation.1 | loop fusion | flops 12320768 | bytes 1311232 | tf_op jit(solution)/shard_map/reduce_sum | solution.py:87
  43.6 0.0 copy-done
  43.6 0.0 copy-start.3
  43.6 0.4 multiply_reduce_fusion.3
  44.0 1.6 %collective-permute-start.8 = (f32[128]{0:T(128)S(1)}, f32[128]{0:T(128)S(1)}, u32[]{:S(2)}, u32[]{:S(2)}) collective-permute-start(f32[128]{0:T(128)S(1)} %get-tuple-element.39), channel_id=1, source_target_pairs={{0,1},{1,0},{2,3},{3,2},{4,5},{5,4},{6,7},{7,6},{8,9},{9,8},{10,11... | collective-permute-start | bytes 1544 | tf_op jit(solution)/shard_map/ppermute | solution.py:35
  45.7 2.0 %collective-permute-done.8 = f32[128]{0:T(128)S(1)} collective-permute-done((f32[128]{0:T(128)S(1)}, f32[128]{0:T(128)S(1)}, u32[]{:S(2)}, u32[]{:S(2)}) %collective-permute-start.8) | collective-permute-done | bytes 544 | tf_op jit(solution)/shard_map/ppermute | solution.py:35
  47.7 2.6 %collective-permute-start.9 = (f32[128]{0:T(128)S(1)}, f32[128]{0:T(128)S(1)}, u32[]{:S(2)}, u32[]{:S(2)}) collective-permute-start(f32[128]{0:T(128)S(1)} %add.71), channel_id=1, source_target_pairs={{0,2},{1,3},{2,0},{3,1},{4,6},{5,7},{6,4},{7,5},{8,10},{9,11},{10,... | collective-permute-start | bytes 1544 | tf_op jit(solution)/shard_map/ppermute | solution.py:35
  50.3 1.9 %collective-permute-done.9 = f32[128]{0:T(128)S(1)} collective-permute-done((f32[128]{0:T(128)S(1)}, f32[128]{0:T(128)S(1)}, u32[]{:S(2)}, u32[]{:S(2)}) %collective-permute-start.9) | collective-permute-done | bytes 544 | tf_op jit(solution)/shard_map/ppermute | solution.py:35
  52.2 0.0 copy-done.3
  52.2 1.0 %multiply_convert_fusion = bf16[128,2048]{1,0:T(8,128)(2,1)} fusion(f32[128,2048]{1,0:T(8,128)S(1)} %get-tuple-element.40, f32[2048]{0:T(1024)S(1)} %copy-done.3, f32[128]{0:T(128)S(1)} %add_rsqrt_fusion), kind=kLoop, calls=%fused_computation.20 | loop fusion | flops 786432 | bytes 1581568 | tf_op jit(solution)/shard_map/convert_element_type | solution.py:92
  (6 shorter events, 0.1 us)
Async XLA Ops:
  0.8 3.6 %collective-permute-start = (bf16[3,2,2048]{2,1,0:T(2,128)(2,1)S(1)}, bf16[3,2,2048]{2,1,0:T(2,128)(2,1)S(1)}, u32[]{:S(2)}, u32[]{:S(2)}) collective-permute-start(bf16[3,2,2048]{2,1,0:T(2,128)(2,1)S(1)} %pad_maximum_fusion), channel_id=1, source_target_pairs={{0,4},{4,8},{8,12},{12,16},{16,20},{20,24},{24,28},{1,5},{5,9},{9,... | collective-permute-start | bytes 73736 | tf_op jit(solution)/shard_map/ppermute | solution.py:12
  7.2 0.9 %copy-start.1 = (f32[2048,16]{0,1:T(8,128)S(1)}, f32[2048,16]{0,1:T(8,128)}, u32[]{:S(2)}) copy-start(f32[2048,16]{0,1:T(8,128)} %param.12) | copy-start | bytes 393220
  8.1 21.3 %copy-start.2 = (f32[2048,16]{0,1:T(8,128)S(1)}, f32[2048,16]{0,1:T(8,128)}, u32[]{:S(2)}) copy-start(f32[2048,16]{0,1:T(8,128)} %param.13) | copy-start | bytes 393220
  11.3 15.3 %collective-permute-start.1 = (f32[16,2048]{1,0:T(8,128)S(1)}, f32[16,2048]{1,0:T(8,128)S(1)}, u32[]{:S(2)}, u32[]{:S(2)}) collective-permute-start(f32[16,2048]{1,0:T(8,128)S(1)} %get-tuple-element.44), channel_id=1, source_target_pairs={{0,4},{4,8},{8,12},{12,16},{16,20},{20,24},{24,28},{1,5},{5,9},{9,... | collective-permute-start | bytes 393224 | tf_op jit(solution)/shard_map/ppermute | solution.py:12
  15.8 12.1 %collective-permute-start.2 = (f32[16,2048]{1,0:T(8,128)S(1)}, f32[16,2048]{1,0:T(8,128)S(1)}, u32[]{:S(2)}, u32[]{:S(2)}) collective-permute-start(f32[16,2048]{1,0:T(8,128)S(1)} %get-tuple-element.44), channel_id=1, source_target_pairs={{0,8},{4,12},{8,16},{12,20},{16,24},{20,28},{1,9},{5,13},{9,17},{1... | collective-permute-start | bytes 393224 | tf_op jit(solution)/shard_map/ppermute | solution.py:12
  19.6 18.4 %collective-permute-start.3 = (f32[16,2048]{1,0:T(8,128)S(1)}, f32[16,2048]{1,0:T(8,128)S(1)}, u32[]{:S(2)}, u32[]{:S(2)}) collective-permute-start(f32[16,2048]{1,0:T(8,128)S(1)} %get-tuple-element.44), channel_id=1, source_target_pairs={{0,12},{4,16},{8,20},{12,24},{16,28},{1,13},{5,17},{9,21},{13,25},... | collective-permute-start | bytes 393224 | tf_op jit(solution)/shard_map/ppermute | solution.py:12
  23.9 14.1 %collective-permute-start.4 = (f32[16,2048]{1,0:T(8,128)S(1)}, f32[16,2048]{1,0:T(8,128)S(1)}, u32[]{:S(2)}, u32[]{:S(2)}) collective-permute-start(f32[16,2048]{1,0:T(8,128)S(1)} %get-tuple-element.44), channel_id=1, source_target_pairs={{0,16},{4,20},{8,24},{12,28},{1,17},{5,21},{9,25},{13,29},{2,18},{... | collective-permute-start | bytes 393224 | tf_op jit(solution)/shard_map/ppermute | solution.py:12
  25.2 12.8 %collective-permute-start.5 = (f32[16,2048]{1,0:T(8,128)S(1)}, f32[16,2048]{1,0:T(8,128)S(1)}, u32[]{:S(2)}, u32[]{:S(2)}) collective-permute-start(f32[16,2048]{1,0:T(8,128)S(1)} %get-tuple-element.44), channel_id=1, source_target_pairs={{0,20},{4,24},{8,28},{1,21},{5,25},{9,29},{2,22},{6,26},{10,30},{3... | collective-permute-start | bytes 393224 | tf_op jit(solution)/shard_map/ppermute | solution.py:12
  26.6 11.5 %collective-permute-start.6 = (f32[16,2048]{1,0:T(8,128)S(1)}, f32[16,2048]{1,0:T(8,128)S(1)}, u32[]{:S(2)}, u32[]{:S(2)}) collective-permute-start(f32[16,2048]{1,0:T(8,128)S(1)} %get-tuple-element.44), channel_id=1, source_target_pairs={{0,24},{4,28},{1,25},{5,29},{2,26},{6,30},{3,27},{7,31}} | collective-permute-start | bytes 393224 | tf_op jit(solution)/shard_map/ppermute | solution.py:12
  27.9 10.2 %collective-permute-start.7 = (f32[16,2048]{1,0:T(8,128)S(1)}, f32[16,2048]{1,0:T(8,128)S(1)}, u32[]{:S(2)}, u32[]{:S(2)}) collective-permute-start(f32[16,2048]{1,0:T(8,128)S(1)} %get-tuple-element.44), channel_id=1, source_target_pairs={{0,28},{1,29},{2,30},{3,31}} | collective-permute-start | bytes 393224 | tf_op jit(solution)/shard_map/ppermute | solution.py:12
  38.3 5.3 %copy-start = (bf16[128,2048]{1,0:T(8,128)(2,1)S(1)}, bf16[128,2048]{1,0:T(8,128)(2,1)}, u32[]{:S(2)}) copy-start(bf16[128,2048]{1,0:T(8,128)(2,1)} %param.14) | copy-start | bytes 1572868
  43.6 8.6 %copy-start.3 = (f32[2048]{0:T(1024)S(1)}, f32[2048]{0:T(1024)}, u32[]{:S(2)}) copy-start(f32[2048]{0:T(1024)} %param.15) | copy-start | bytes 24580
  44.0 3.6 %collective-permute-start.8 = (f32[128]{0:T(128)S(1)}, f32[128]{0:T(128)S(1)}, u32[]{:S(2)}, u32[]{:S(2)}) collective-permute-start(f32[128]{0:T(128)S(1)} %get-tuple-element.39), channel_id=1, source_target_pairs={{0,1},{1,0},{2,3},{3,2},{4,5},{5,4},{6,7},{7,6},{8,9},{9,8},{10,11... | collective-permute-start | bytes 1544 | tf_op jit(solution)/shard_map/ppermute | solution.py:35
  47.7 4.5 %collective-permute-start.9 = (f32[128]{0:T(128)S(1)}, f32[128]{0:T(128)S(1)}, u32[]{:S(2)}, u32[]{:S(2)}) collective-permute-start(f32[128]{0:T(128)S(1)} %add.71), channel_id=1, source_target_pairs={{0,2},{1,3},{2,0},{3,1},{4,6},{5,7},{6,4},{7,5},{8,10},{9,11},{10,... | collective-permute-start | bytes 1544 | tf_op jit(solution)/shard_map/ppermute | solution.py:35

commit v6 on v5

--- a/solution.py
+++ b/solution.py
@@ -2,6 +2,8 @@
 import jax.numpy as jnp
 from jax import lax
 from jax.sharding import PartitionSpec as P
+from jax.experimental import pallas as pl
+from jax.experimental.pallas import tpu as pltpu
 
 D = 8192
 
@@ -37,38 +39,73 @@
     return value
 
 
+def front_kernel(q_ref, k_ref, v_ref, halo_ref, taps_ref, coarse_ref, fine_ref, qf_ref, g_ref, end_ref, pad_ref):
+    rows = q_ref.shape[0]
+    lead = pad_ref.shape[1] - rows
+    feats = []
+    for i, ref in enumerate((q_ref, k_ref, v_ref)):
+        pad_ref[i, lead:, :] = ref[...].astype(jnp.float32)
+        pad_ref[i, lead - 2 : lead, :] = halo_ref[i].astype(jnp.float32)
+        acc = taps_ref[i, 0:1, :] * pad_ref[i, lead:, :]
+        for j in (1, 2):
+            acc = acc + taps_ref[i, j : j + 1, :] * pad_ref[i, lead - j : lead - j + rows, :]
+        feats.append(acc)
+    qf_ref[...] = feats[0]
+    gated = (feats[1] * feats[2]).astype(jnp.bfloat16).astype(jnp.float32)
+    g_ref[...] = gated
+    chunks = rows // 8
+
+    def mode(m, carry):
+        weights = coarse_ref[m]
+        inner = weights[0:1, :] * gated[0:8, :]
+        for u in range(1, chunks):
+            inner = inner + weights[u : u + 1, :] * gated[8 * u : 8 * u + 8, :]
+        end_ref[pl.ds(m, 1), :] = jnp.sum(inner * fine_ref[m], axis=0, keepdims=True)
+        return carry
+
+    lax.fori_loop(0, coarse_ref.shape[0], mode, 0)
+
+
+def front(q_in, k_in, v_in, before, short_filter, decay):
+    rows, width = q_in.shape
+    modes = decay.shape[0]
+    chunks = rows // 8
+    coarse = jnp.exp(-decay[:, None, :] * (8.0 * (chunks - 1 - jnp.arange(chunks, dtype=jnp.float32)))[None, :, None])
+    fine = jnp.exp(-decay[:, None, :] * (7.0 - jnp.arange(8, dtype=jnp.float32))[None, :, None])
+    vmem = pl.BlockSpec(memory_space=pltpu.VMEM)
+    return pl.pallas_call(
+        front_kernel,
+        out_shape=(
+            jax.ShapeDtypeStruct((rows, width), jnp.float32),
+            jax.ShapeDtypeStruct((rows, width), jnp.float32),
+            jax.ShapeDtypeStruct((modes, width), jnp.float32),
+        ),
+        in_specs=[vmem] * 7,
+        out_specs=(vmem, vmem, vmem),
+        scratch_shapes=[pltpu.VMEM((3, rows + 8, width), jnp.float32)],
+        compiler_params=pltpu.CompilerParams(vmem_limit_bytes=48 * 1024 * 1024),
+        cost_estimate=pl.CostEstimate(
+            flops=2 * rows * width * (9 + 2 * modes), transcendentals=0, bytes_accessed=rows * width * 14
+        ),
+    )(q_in, k_in, v_in, before, short_filter, coarse, fine)
+
+
 def per_device(q_in, k_in, v_in, short_filter, rate, residue, resid, gain):
     rows, width = q_in.shape
     taps = short_filter.shape[1]
     stacked = jnp.stack([q_in, k_in, v_in])
     tail = stacked[:, rows - (taps - 1) :, :]
     before = from_behind(tail, "ctx", 1)
-    padded = jnp.concatenate([before, stacked], axis=1).astype(jnp.float32)
-    feats = short_filter[:, 0, None, :] * padded[:, taps - 1 :, :]
-    for j in range(1, taps):
-        feats = (
-            feats + short_filter[:, j, None, :] * padded[:, taps - 1 - j : taps - 1 - j + rows, :]
-        )
-    q_feat = feats[0]
-    gated = (feats[1] * feats[2]).astype(jnp.bfloat16)
-    values = lax.optimization_barrier(gated).astype(jnp.float32)
+    decay = rate.T
+    weight = residue.T
+    q_feat, values, ending = front(q_in, k_in, v_in, before, short_filter, decay)
     block = min(128, rows)
     blocks = values.reshape(rows // block, block, width)
-    decay = rate.T
-    weight = residue.T
     offsets = jnp.arange(block, dtype=jnp.int32).astype(jnp.float32)
     grow = jnp.exp(decay[:, None, :] * offsets[None, :, None])
     fade = jnp.exp(-decay[:, None, :] * offsets[None, :, None])
     enter = jnp.exp(-decay[:, None, :] * (offsets[None, :, None] + 1.0))
-    last_fade = jnp.exp(-decay * (block - 1))
-    block_decay = jnp.exp(-decay * block)
-
-    def end_step(state, piece):
-        summed = jnp.einsum("sc,msc->mc", piece, grow)
-        return (state * block_decay + last_fade * summed, None)
-
     zeros = jnp.zeros(decay.shape, jnp.float32)
-    ending, unused = lax.scan(end_step, zeros, blocks)
 
     def main_step(state, piece):
         running = jnp.cumsum(piece[None, :, :] * grow, axis=1) * fade

time: 53.5 us -> 53 us (level)
  Pallas kernels: 0 us -> 5.78 us
  other arithmetic: 22.6 us -> 19.5 us
  starting transfers between devices: 24.7 us -> 23 us
  local copies, waits for them, and re-layouts: 1.73 us -> 0.05 us
    pallas_call x0 -> x1, Pallas kernels: none -> 5.78 us  [front(): pl.pallas_call(front_kernel, out_shape=(jax.ShapeDtypeStruct((rows, width...]
    dot_general x1 -> x0, other arithmetic: 3.07 us -> none  [end_step(): summed = jnp.einsum('sc,msc->mc', piece, grow)]
    convert_element_type x3 -> x0, other arithmetic: 2.18 us -> none  [the longest x1 1.85 us: per_device(): padded = jnp.concatenate([before, stacked], axis=1).astype(jnp.float32)]
    exp x0 -> x2, other arithmetic: none -> 1.91 us  [the longest x1 1.69 us: front(): jnp.exp(-decay[:, None, :] * (8.0 * (chunks - 1 - jnp.arange(chunks, dtyp...]
    ppermute x8, starting transfers between devices: 20.4 us -> 18.8 us  [from_behind(): return lax.ppermute(block, axis, route)]
    slice x1 -> x0, local copies, waits for them, and re-layouts: 1.12 us -> none  [per_device(): feats = short_filter[:, 0, None, :] * padded[:, taps - 1:, :]]
    add x1 -> x0, other arithmetic: 0.92 us -> none  [per_device(): feats + short_filter[:, j, None, :] * padded[:, taps - 1 - j:taps - 1 - j...]
    neg x1, other arithmetic: 0.05 us -> 0.92 us  [front(): -decay[:, None, :]]
  transfers between devices with their start and end apart: 10 -> 10, of which waited for: 2 -> 2; matrix products, arithmetic and copies ran while one was open for 18% -> 23% of each run, Pallas kernels for 0% -> 0%
where the time goes in v6:
time: 53 us; the launch traced here: 52.6 us
  starting transfers between devices  23 us (43%)
  other arithmetic  19.5 us (37%)
  Pallas kernels  5.78 us (11%)
  waiting for transfers between devices  3.89 us (7%)
    ppermute x8, starting transfers between devices, from_behind(): return lax.ppermute(block, axis, route)  18.8 us
    another operation x1, other arithmetic, local(): running = jnp.cumsum(values[None, :, :] * grow, axis=1) * fade  9.02 us
    pallas_call x1, Pallas kernels, front(): pl.pallas_call(front_kernel, out_shape=(jax.ShapeDtypeStruct((rows, width...  5.78 us
    reduce_sum x1, other arithmetic, per_device(): jnp.sum(jnp.exp(-decay[:, None, :] * times[None, :, None]) * weights[:, N...  5.31 us
    ppermute x2, starting transfers between devices, butterfly_sum(): lax.ppermute(value, axis, [(i, i ^ step) for i in range(count)])  4.23 us
    ppermute x2, waiting for transfers between devices, butterfly_sum(): lax.ppermute(value, axis, [(i, i ^ step) for i in range(count)])  3.87 us
    exp x1, other arithmetic, front(): jnp.exp(-decay[:, None, :] * (8.0 * (chunks - 1 - jnp.arange(chunks, dtyp...  1.69 us
  transfers between devices with their start and end apart: 10, of which 2 were waited for; matrix products, arithmetic and copies ran while one was open for 23% of the time, Pallas kernels for 0%

profile of v6, /device:TPU:0, one launch (start us, length us, event | category | flops | bytes accessed | tf_op | source)
XLA Modules:
  0.0 52.6 jit_solution(16771149542934582411)
XLA Ops:
  0.0 0.8 %pad_maximum_fusion = bf16[3,2,2048]{2,1,0:T(2,128)(2,1)S(1)} fusion(bf16[1,128,2048]{2,1,0:T(8,128)(2,1)} %bitcast.11, bf16[1,128,2048]{2,1,0:T(8,128)(2,1)} %bitcast.10, bf16[1,128,2048]{2,1,0:T(8,128)(2,1)} %bitcast.9), kind=kLoop, calls=%fused_computation.15 | loop fusion | flops 73728 | bytes 1597440 | tf_op jit(solution)/shard_map/stack | solution.py:96
  0.8 0.0 copy-start
  0.8 0.0 copy-start.1
  0.8 0.0 copy-start.2
  0.9 0.0 copy-start.3
  0.9 2.5 %collective-permute-start = (bf16[3,2,2048]{2,1,0:T(2,128)(2,1)S(1)}, bf16[3,2,2048]{2,1,0:T(2,128)(2,1)S(1)}, u32[]{:S(2)}, u32[]{:S(2)}) collective-permute-start(bf16[3,2,2048]{2,1,0:T(2,128)(2,1)S(1)} %pad_maximum_fusion), channel_id=1, source_target_pairs={{0,4},{4,8},{8,12},{12,16},{16,20},{20,24},{24,28},{1,5},{5,9},{9,... | collective-permute-start | bytes 73736 | tf_op jit(solution)/shard_map/ppermute | solution.py:14
  3.4 0.9 %bitcast_negate_fusion = f32[16,2048]{1,0:T(8,128)S(1)} fusion(f32[2048,16]{0,1:T(8,128)} %param.12), kind=kLoop, calls=%fused_computation.22 | loop fusion | flops 32768 | bytes 262144 | tf_op jit(solution)/shard_map/neg | solution.py:73
  4.4 1.7 %multiply_exponential_fusion.coarse_ref = f32[16,16,2048]{2,1,0:T(8,128)} fusion(f32[16]{0:T(128)S(1)} %subtract_multiply_fusion, f32[16,2048]{1,0:T(8,128)S(1)} %bitcast_negate_fusion), kind=kLoop, calls=%fused_computation.9 | loop fusion | flops 524288 | bytes 2228288 | tf_op jit(solution)/shard_map/exp | solution.py:73
  6.0 0.2 multiply_exponential_fusion.1.fine_ref
  6.3 0.0 copy-start.5
  6.3 0.0 copy-start.6
  6.3 0.0 collective-permute-done.halo_ref
  6.3 0.0 copy-done
  6.3 0.0 copy-done.1
  6.3 0.0 copy-done.2
  6.3 0.0 copy-done.3
  6.3 5.8 %shard_map.82 = (f32[128,2048]{1,0:T(8,128)S(1)}, f32[128,2048]{1,0:T(8,128)S(1)}, f32[16,2048]{1,0:T(8,128)S(1)}) custom-call(bf16[128,2048]{1,0:T(8,128)(2,1)S(1)} %copy-done, bf16[128,2048]{1,0:T(8,128)(2,1)S(1)} %copy-done.1, bf16[128,2048]{1,0:T(8,128)(2,1)S(1)} %copy-done.2, bf16[3,2,2048]{2,1,0:T(2,128)(2,1)S(1)} %collective-permute-done.halo_ref, ...), custom_call_target="tpu_custom_call" | custom-call | flops 21495808 | bytes 3670016 | tf_op jit(solution)/shard_map/pallas_call | solution.py:76
  12.1 4.5 %collective-permute-start.1 = (f32[16,2048]{1,0:T(8,128)S(1)}, f32[16,2048]{1,0:T(8,128)S(1)}, u32[]{:S(2)}, u32[]{:S(2)}) collective-permute-start(f32[16,2048]{1,0:T(8,128)S(1)} %get-tuple-element.17), channel_id=1, source_target_pairs={{0,4},{4,8},{8,12},{12,16},{16,20},{20,24},{24,28},{1,5},{5,9},{9,... | collective-permute-start | bytes 393224 | tf_op jit(solution)/shard_map/ppermute | solution.py:14
  16.6 3.4 %collective-permute-start.2 = (f32[16,2048]{1,0:T(8,128)S(1)}, f32[16,2048]{1,0:T(8,128)S(1)}, u32[]{:S(2)}, u32[]{:S(2)}) collective-permute-start(f32[16,2048]{1,0:T(8,128)S(1)} %get-tuple-element.17), channel_id=1, source_target_pairs={{0,8},{4,12},{8,16},{12,20},{16,24},{20,28},{1,9},{5,13},{9,17},{1... | collective-permute-start | bytes 393224 | tf_op jit(solution)/shard_map/ppermute | solution.py:14
  20.1 3.0 %collective-permute-start.3 = (f32[16,2048]{1,0:T(8,128)S(1)}, f32[16,2048]{1,0:T(8,128)S(1)}, u32[]{:S(2)}, u32[]{:S(2)}) collective-permute-start(f32[16,2048]{1,0:T(8,128)S(1)} %get-tuple-element.17), channel_id=1, source_target_pairs={{0,12},{4,16},{8,20},{12,24},{16,28},{1,13},{5,17},{9,21},{13,25},... | collective-permute-start | bytes 393224 | tf_op jit(solution)/shard_map/ppermute | solution.py:14
  23.1 1.3 %collective-permute-start.4 = (f32[16,2048]{1,0:T(8,128)S(1)}, f32[16,2048]{1,0:T(8,128)S(1)}, u32[]{:S(2)}, u32[]{:S(2)}) collective-permute-start(f32[16,2048]{1,0:T(8,128)S(1)} %get-tuple-element.17), channel_id=1, source_target_pairs={{0,16},{4,20},{8,24},{12,28},{1,17},{5,21},{9,25},{13,29},{2,18},{... | collective-permute-start | bytes 393224 | tf_op jit(solution)/shard_map/ppermute | solution.py:14
  24.4 1.3 %collective-permute-start.5 = (f32[16,2048]{1,0:T(8,128)S(1)}, f32[16,2048]{1,0:T(8,128)S(1)}, u32[]{:S(2)}, u32[]{:S(2)}) collective-permute-start(f32[16,2048]{1,0:T(8,128)S(1)} %get-tuple-element.17), channel_id=1, source_target_pairs={{0,20},{4,24},{8,28},{1,21},{5,25},{9,29},{2,22},{6,26},{10,30},{3... | collective-permute-start | bytes 393224 | tf_op jit(solution)/shard_map/ppermute | solution.py:14
  25.7 0.0 collective-permute-done.1
  25.7 1.3 %collective-permute-start.6 = (f32[16,2048]{1,0:T(8,128)S(1)}, f32[16,2048]{1,0:T(8,128)S(1)}, u32[]{:S(2)}, u32[]{:S(2)}) collective-permute-start(f32[16,2048]{1,0:T(8,128)S(1)} %get-tuple-element.17), channel_id=1, source_target_pairs={{0,24},{4,28},{1,25},{5,29},{2,26},{6,30},{3,27},{7,31}} | collective-permute-start | bytes 393224 | tf_op jit(solution)/shard_map/ppermute | solution.py:14
  27.0 0.0 collective-permute-done.2
  27.0 1.5 %collective-permute-start.7 = (f32[16,2048]{1,0:T(8,128)S(1)}, f32[16,2048]{1,0:T(8,128)S(1)}, u32[]{:S(2)}, u32[]{:S(2)}) collective-permute-start(f32[16,2048]{1,0:T(8,128)S(1)} %get-tuple-element.17), channel_id=1, source_target_pairs={{0,28},{1,29},{2,30},{3,31}} | collective-permute-start | bytes 393224 | tf_op jit(solution)/shard_map/ppermute | solution.py:14
  28.5 0.0 copy-done.5
  28.5 0.0 copy-done.6
  28.5 9.0 %multiply_reduce_fusion.1 = f32[128,2048]{1,0:T(8,128)S(1)} fusion(f32[16,2048]{1,0:T(8,128)S(1)} %bitcast.13, f32[16,2048]{1,0:T(8,128)S(1)} %bitcast_negate_fusion, f32[128]{0:T(128)S(1)} %iota_convert_fusion, f32[16,2048]{1,0:T(8,128)S(1)} %bitcast.12, f32[128,2048]{1,0:T(8,128)S(1)} %get-tuple-element.18), kind=kOutput, calls=%fused_computation.1 | output fusion | flops 557580288 | bytes 2490880 | tf_op jit(solution)/shard_map/jit(cumsum)/reduce_window_sum | solution.py:117
  37.5 0.0 collective-permute-done.3
  37.5 0.0 collective-permute-done.4
  37.6 0.0 collective-permute-done.5
  37.6 0.0 collective-permute-done.6
  37.6 0.0 collective-permute-done.7
  37.6 0.2 add_multiply_fusion
  37.8 0.0 copy-start.4
  37.8 5.3 %multiply_reduce_fusion = f32[128,2048]{1,0:T(8,128)S(1)} fusion(f32[16,2048]{1,0:T(8,128)S(1)} %add_multiply_fusion, f32[128]{0:T(128)S(1)} %broadcast_add_fusion, f32[16,2048]{1,0:T(8,128)S(1)} %bitcast_negate_fusion), kind=kLoop, calls=%fused_computation | loop fusion | flops 12320768 | bytes 1311232 | tf_op jit(solution)/shard_map/reduce_sum | solution.py:124
  43.1 0.0 copy-done.4
  43.1 0.0 copy-start.7
  43.1 0.4 multiply_reduce_fusion.2
  43.5 1.6 %collective-permute-start.8 = (f32[128]{0:T(128)S(1)}, f32[128]{0:T(128)S(1)}, u32[]{:S(2)}, u32[]{:S(2)}) collective-permute-start(f32[128]{0:T(128)S(1)} %get-tuple-element.27), channel_id=1, source_target_pairs={{0,1},{1,0},{2,3},{3,2},{4,5},{5,4},{6,7},{7,6},{8,9},{9,8},{10,11... | collective-permute-start | bytes 1544 | tf_op jit(solution)/shard_map/ppermute | solution.py:37
  45.2 2.0 %collective-permute-done.8 = f32[128]{0:T(128)S(1)} collective-permute-done((f32[128]{0:T(128)S(1)}, f32[128]{0:T(128)S(1)}, u32[]{:S(2)}, u32[]{:S(2)}) %collective-permute-start.8) | collective-permute-done | bytes 544 | tf_op jit(solution)/shard_map/ppermute | solution.py:37
  47.2 2.6 %collective-permute-start.9 = (f32[128]{0:T(128)S(1)}, f32[128]{0:T(128)S(1)}, u32[]{:S(2)}, u32[]{:S(2)}) collective-permute-start(f32[128]{0:T(128)S(1)} %add.56), channel_id=1, source_target_pairs={{0,2},{1,3},{2,0},{3,1},{4,6},{5,7},{6,4},{7,5},{8,10},{9,11},{10,... | collective-permute-start | bytes 1544 | tf_op jit(solution)/shard_map/ppermute | solution.py:37
  49.8 1.9 %collective-permute-done.9 = f32[128]{0:T(128)S(1)} collective-permute-done((f32[128]{0:T(128)S(1)}, f32[128]{0:T(128)S(1)}, u32[]{:S(2)}, u32[]{:S(2)}) %collective-permute-start.9) | collective-permute-done | bytes 544 | tf_op jit(solution)/shard_map/ppermute | solution.py:37
  51.6 0.0 copy-done.7
  51.6 1.0 %multiply_convert_fusion = bf16[128,2048]{1,0:T(8,128)(2,1)} fusion(f32[128,2048]{1,0:T(8,128)S(1)} %get-tuple-element.28, f32[2048]{0:T(1024)S(1)} %copy-done.7, f32[128]{0:T(128)S(1)} %add_rsqrt_fusion), kind=kLoop, calls=%fused_computation.10 | loop fusion | flops 786432 | bytes 1581568 | tf_op jit(solution)/shard_map/convert_element_type | solution.py:129
  (6 shorter events, 0.0 us)
Async XLA Ops:
  0.8 5.5 %copy-start = (bf16[128,2048]{1,0:T(8,128)(2,1)S(1)}, bf16[128,2048]{1,0:T(8,128)(2,1)}, u32[]{:S(2)}) copy-start(bf16[128,2048]{1,0:T(8,128)(2,1)} %q_ref.1) | copy-start | bytes 1572868
  0.8 5.5 %copy-start.1 = (bf16[128,2048]{1,0:T(8,128)(2,1)S(1)}, bf16[128,2048]{1,0:T(8,128)(2,1)}, u32[]{:S(2)}) copy-start(bf16[128,2048]{1,0:T(8,128)(2,1)} %k_ref.1) | copy-start | bytes 1572868
  0.8 5.5 %copy-start.2 = (bf16[128,2048]{1,0:T(8,128)(2,1)S(1)}, bf16[128,2048]{1,0:T(8,128)(2,1)}, u32[]{:S(2)}) copy-start(bf16[128,2048]{1,0:T(8,128)(2,1)} %v_ref.1) | copy-start | bytes 1572868
  0.9 5.5 %copy-start.3 = (f32[3,3,2048]{2,1,0:T(4,128)S(1)}, f32[3,3,2048]{2,1,0:T(4,128)}, u32[]{:S(2)}) copy-start(f32[3,3,2048]{2,1,0:T(4,128)} %taps_ref.1) | copy-start | bytes 221188
  0.9 5.4 %collective-permute-start = (bf16[3,2,2048]{2,1,0:T(2,128)(2,1)S(1)}, bf16[3,2,2048]{2,1,0:T(2,128)(2,1)S(1)}, u32[]{:S(2)}, u32[]{:S(2)}) collective-permute-start(bf16[3,2,2048]{2,1,0:T(2,128)(2,1)S(1)} %pad_maximum_fusion), channel_id=1, source_target_pairs={{0,4},{4,8},{8,12},{12,16},{16,20},{20,24},{24,28},{1,5},{5,9},{9,... | collective-permute-start | bytes 73736 | tf_op jit(solution)/shard_map/ppermute | solution.py:14
  6.3 22.2 %copy-start.5 = (f32[2048,16]{0,1:T(8,128)S(1)}, f32[2048,16]{0,1:T(8,128)}, u32[]{:S(2)}) copy-start(f32[2048,16]{0,1:T(8,128)} %param.12) | copy-start | bytes 393220
  6.3 22.2 %copy-start.6 = (f32[2048,16]{0,1:T(8,128)S(1)}, f32[2048,16]{0,1:T(8,128)}, u32[]{:S(2)}) copy-start(f32[2048,16]{0,1:T(8,128)} %param.13) | copy-start | bytes 393220
  12.1 13.5 %collective-permute-start.1 = (f32[16,2048]{1,0:T(8,128)S(1)}, f32[16,2048]{1,0:T(8,128)S(1)}, u32[]{:S(2)}, u32[]{:S(2)}) collective-permute-start(f32[16,2048]{1,0:T(8,128)S(1)} %get-tuple-element.17), channel_id=1, source_target_pairs={{0,4},{4,8},{8,12},{12,16},{16,20},{20,24},{24,28},{1,5},{5,9},{9,... | collective-permute-start | bytes 393224 | tf_op jit(solution)/shard_map/ppermute | solution.py:14
  16.6 10.4 %collective-permute-start.2 = (f32[16,2048]{1,0:T(8,128)S(1)}, f32[16,2048]{1,0:T(8,128)S(1)}, u32[]{:S(2)}, u32[]{:S(2)}) collective-permute-start(f32[16,2048]{1,0:T(8,128)S(1)} %get-tuple-element.17), channel_id=1, source_target_pairs={{0,8},{4,12},{8,16},{12,20},{16,24},{20,28},{1,9},{5,13},{9,17},{1... | collective-permute-start | bytes 393224 | tf_op jit(solution)/shard_map/ppermute | solution.py:14
  20.1 17.5 %collective-permute-start.3 = (f32[16,2048]{1,0:T(8,128)S(1)}, f32[16,2048]{1,0:T(8,128)S(1)}, u32[]{:S(2)}, u32[]{:S(2)}) collective-permute-start(f32[16,2048]{1,0:T(8,128)S(1)} %get-tuple-element.17), channel_id=1, source_target_pairs={{0,12},{4,16},{8,20},{12,24},{16,28},{1,13},{5,17},{9,21},{13,25},... | collective-permute-start | bytes 393224 | tf_op jit(solution)/shard_map/ppermute | solution.py:14
  23.1 14.5 %collective-permute-start.4 = (f32[16,2048]{1,0:T(8,128)S(1)}, f32[16,2048]{1,0:T(8,128)S(1)}, u32[]{:S(2)}, u32[]{:S(2)}) collective-permute-start(f32[16,2048]{1,0:T(8,128)S(1)} %get-tuple-element.17), channel_id=1, source_target_pairs={{0,16},{4,20},{8,24},{12,28},{1,17},{5,21},{9,25},{13,29},{2,18},{... | collective-permute-start | bytes 393224 | tf_op jit(solution)/shard_map/ppermute | solution.py:14
  24.4 13.2 %collective-permute-start.5 = (f32[16,2048]{1,0:T(8,128)S(1)}, f32[16,2048]{1,0:T(8,128)S(1)}, u32[]{:S(2)}, u32[]{:S(2)}) collective-permute-start(f32[16,2048]{1,0:T(8,128)S(1)} %get-tuple-element.17), channel_id=1, source_target_pairs={{0,20},{4,24},{8,28},{1,21},{5,25},{9,29},{2,22},{6,26},{10,30},{3... | collective-permute-start | bytes 393224 | tf_op jit(solution)/shard_map/ppermute | solution.py:14
  25.7 11.9 %collective-permute-start.6 = (f32[16,2048]{1,0:T(8,128)S(1)}, f32[16,2048]{1,0:T(8,128)S(1)}, u32[]{:S(2)}, u32[]{:S(2)}) collective-permute-start(f32[16,2048]{1,0:T(8,128)S(1)} %get-tuple-element.17), channel_id=1, source_target_pairs={{0,24},{4,28},{1,25},{5,29},{2,26},{6,30},{3,27},{7,31}} | collective-permute-start | bytes 393224 | tf_op jit(solution)/shard_map/ppermute | solution.py:14
  27.0 10.6 %collective-permute-start.7 = (f32[16,2048]{1,0:T(8,128)S(1)}, f32[16,2048]{1,0:T(8,128)S(1)}, u32[]{:S(2)}, u32[]{:S(2)}) collective-permute-start(f32[16,2048]{1,0:T(8,128)S(1)} %get-tuple-element.17), channel_id=1, source_target_pairs={{0,28},{1,29},{2,30},{3,31}} | collective-permute-start | bytes 393224 | tf_op jit(solution)/shard_map/ppermute | solution.py:14
  37.8 5.3 %copy-start.4 = (bf16[128,2048]{1,0:T(8,128)(2,1)S(1)}, bf16[128,2048]{1,0:T(8,128)(2,1)}, u32[]{:S(2)}) copy-start(bf16[128,2048]{1,0:T(8,128)(2,1)} %param.14) | copy-start | bytes 1572868
  43.1 8.5 %copy-start.7 = (f32[2048]{0:T(1024)S(1)}, f32[2048]{0:T(1024)}, u32[]{:S(2)}) copy-start(f32[2048]{0:T(1024)} %param.15) | copy-start | bytes 24580
  43.5 3.6 %collective-permute-start.8 = (f32[128]{0:T(128)S(1)}, f32[128]{0:T(128)S(1)}, u32[]{:S(2)}, u32[]{:S(2)}) collective-permute-start(f32[128]{0:T(128)S(1)} %get-tuple-element.27), channel_id=1, source_target_pairs={{0,1},{1,0},{2,3},{3,2},{4,5},{5,4},{6,7},{7,6},{8,9},{9,8},{10,11... | collective-permute-start | bytes 1544 | tf_op jit(solution)/shard_map/ppermute | solution.py:37
  47.2 4.5 %collective-permute-start.9 = (f32[128]{0:T(128)S(1)}, f32[128]{0:T(128)S(1)}, u32[]{:S(2)}, u32[]{:S(2)}) collective-permute-start(f32[128]{0:T(128)S(1)} %add.56), channel_id=1, source_target_pairs={{0,2},{1,3},{2,0},{3,1},{4,6},{5,7},{6,4},{7,5},{8,10},{9,11},{10,... | collective-permute-start | bytes 1544 | tf_op jit(solution)/shard_map/ppermute | solution.py:37

commit v7 on v6

--- a/solution.py
+++ b/solution.py
@@ -17,8 +17,8 @@
 def scan_in(ending, rate, rows, axis, cover):
     count = lax.axis_size(axis)
     radix = min(count, 8)
+    ending, covered = lax.optimization_barrier((ending, cover()))
     arrived = [from_behind(ending, axis, shift) for shift in range(1, radix)]
-    arrived, covered = lax.optimization_barrier((arrived, cover()))
     incoming = jnp.zeros_like(ending)
     for shift in range(1, radix):
         incoming = incoming + jnp.exp(-rate * (rows * (shift - 1))) * arrived[shift - 1]

time: 53 us -> 56.5 us (1.066)
  the two profiles are of different devices: /device:TPU:0 before, /device:TPU:2 now
where the time goes in v7:
time: 56.5 us; the launch traced here: 56.1 us
  other arithmetic  19.5 us (35%)
  starting transfers between devices  18.8 us (33%)
  waiting for transfers between devices  11.7 us (21%)
  Pallas kernels  5.73 us (10%)
    ppermute x8, starting transfers between devices, from_behind(): return lax.ppermute(block, axis, route)  14.6 us
    another operation x1, other arithmetic, local(): running = jnp.cumsum(values[None, :, :] * grow, axis=1) * fade  9.01 us
    ppermute x8, waiting for transfers between devices, from_behind(): return lax.ppermute(block, axis, route)  7.86 us
    pallas_call x1, Pallas kernels, front(): pl.pallas_call(front_kernel, out_shape=(jax.ShapeDtypeStruct((rows, width...  5.73 us
    reduce_sum x1, other arithmetic, per_device(): jnp.sum(jnp.exp(-decay[:, None, :] * times[None, :, None]) * weights[:, N...  5.31 us
    ppermute x2, starting transfers between devices, butterfly_sum(): lax.ppermute(value, axis, [(i, i ^ step) for i in range(count)])  4.23 us
    ppermute x2, waiting for transfers between devices, butterfly_sum(): lax.ppermute(value, axis, [(i, i ^ step) for i in range(count)])  3.87 us
    exp x1, other arithmetic, front(): jnp.exp(-decay[:, None, :] * (8.0 * (chunks - 1 - jnp.arange(chunks, dtyp...  1.69 us
  transfers between devices with their start and end apart: 10, of which 5 were waited for; matrix products, arithmetic and copies ran while one was open for 5% of the time, Pallas kernels for 0%

profile of v7, /device:TPU:2, one launch (start us, length us, event | category | flops | bytes accessed | tf_op | source)
XLA Modules:
  0.0 56.1 jit_solution(2000979127931801999)
XLA Ops:
  0.0 0.8 %pad_maximum_fusion = bf16[3,2,2048]{2,1,0:T(2,128)(2,1)S(1)} fusion(bf16[1,128,2048]{2,1,0:T(8,128)(2,1)} %bitcast.11, bf16[1,128,2048]{2,1,0:T(8,128)(2,1)} %bitcast.10, bf16[1,128,2048]{2,1,0:T(8,128)(2,1)} %bitcast.9), kind=kLoop, calls=%fused_computation.15 | loop fusion | flops 73728 | bytes 1597440 | tf_op jit(solution)/shard_map/stack | solution.py:96
  0.8 0.0 copy-start
  0.8 0.0 copy-start.1
  0.8 0.0 copy-start.2
  0.9 0.0 copy-start.3
  0.9 2.1 %collective-permute-start = (bf16[3,2,2048]{2,1,0:T(2,128)(2,1)S(1)}, bf16[3,2,2048]{2,1,0:T(2,128)(2,1)S(1)}, u32[]{:S(2)}, u32[]{:S(2)}) collective-permute-start(bf16[3,2,2048]{2,1,0:T(2,128)(2,1)S(1)} %pad_maximum_fusion), channel_id=1, source_target_pairs={{0,4},{4,8},{8,12},{12,16},{16,20},{20,24},{24,28},{1,5},{5,9},{9,... | collective-permute-start | bytes 73736 | tf_op jit(solution)/shard_map/ppermute | solution.py:14
  3.0 0.9 %bitcast_negate_fusion = f32[16,2048]{1,0:T(8,128)S(1)} fusion(f32[2048,16]{0,1:T(8,128)} %param.12), kind=kLoop, calls=%fused_computation.22 | loop fusion | flops 32768 | bytes 262144 | tf_op jit(solution)/shard_map/neg | solution.py:73
  3.9 1.7 %multiply_exponential_fusion.coarse_ref = f32[16,16,2048]{2,1,0:T(8,128)} fusion(f32[16]{0:T(128)S(1)} %subtract_multiply_fusion, f32[16,2048]{1,0:T(8,128)S(1)} %bitcast_negate_fusion), kind=kLoop, calls=%fused_computation.9 | loop fusion | flops 524288 | bytes 2228288 | tf_op jit(solution)/shard_map/exp | solution.py:73
  5.6 0.2 multiply_exponential_fusion.1.fine_ref
  5.8 0.0 copy-start.5
  5.8 0.0 copy-start.6
  5.8 0.3 collective-permute-done.halo_ref
  6.1 0.0 copy-done
  6.2 0.0 copy-done.1
  6.2 0.0 copy-done.2
  6.2 0.0 copy-done.3
  6.2 5.7 %shard_map.82 = (f32[128,2048]{1,0:T(8,128)S(1)}, f32[128,2048]{1,0:T(8,128)S(1)}, f32[16,2048]{1,0:T(8,128)S(1)}) custom-call(bf16[128,2048]{1,0:T(8,128)(2,1)S(1)} %copy-done, bf16[128,2048]{1,0:T(8,128)(2,1)S(1)} %copy-done.1, bf16[128,2048]{1,0:T(8,128)(2,1)S(1)} %copy-done.2, bf16[3,2,2048]{2,1,0:T(2,128)(2,1)S(1)} %collective-permute-done.halo_ref, ...), custom_call_target="tpu_custom_call" | custom-call | flops 21495808 | bytes 3670016 | tf_op jit(solution)/shard_map/pallas_call | solution.py:76
  11.9 0.0 copy-done.5
  11.9 0.0 copy-done.6
  11.9 9.0 %multiply_reduce_fusion.1 = f32[128,2048]{1,0:T(8,128)S(1)} fusion(f32[16,2048]{1,0:T(8,128)S(1)} %bitcast.13, f32[16,2048]{1,0:T(8,128)S(1)} %bitcast_negate_fusion, f32[128]{0:T(128)S(1)} %iota_convert_fusion, f32[16,2048]{1,0:T(8,128)S(1)} %bitcast.12, f32[128,2048]{1,0:T(8,128)S(1)} %get-tuple-element.12), kind=kOutput, calls=%fused_computation.1 | output fusion | flops 557580288 | bytes 2490880 | tf_op jit(solution)/shard_map/jit(cumsum)/reduce_window_sum | solution.py:117
  20.9 3.3 %collective-permute-start.1 = (f32[16,2048]{1,0:T(8,128)S(1)}, f32[16,2048]{1,0:T(8,128)S(1)}, u32[]{:S(2)}, u32[]{:S(2)}) collective-permute-start(f32[16,2048]{1,0:T(8,128)S(1)} %get-tuple-element.14), channel_id=1, source_target_pairs={{0,4},{4,8},{8,12},{12,16},{16,20},{20,24},{24,28},{1,5},{5,9},{9,... | collective-permute-start | bytes 393224 | tf_op jit(solution)/shard_map/ppermute | solution.py:14
  24.2 3.4 %collective-permute-start.2 = (f32[16,2048]{1,0:T(8,128)S(1)}, f32[16,2048]{1,0:T(8,128)S(1)}, u32[]{:S(2)}, u32[]{:S(2)}) collective-permute-start(f32[16,2048]{1,0:T(8,128)S(1)} %get-tuple-element.14), channel_id=1, source_target_pairs={{0,8},{4,12},{8,16},{12,20},{16,24},{20,28},{1,9},{5,13},{9,17},{1... | collective-permute-start | bytes 393224 | tf_op jit(solution)/shard_map/ppermute | solution.py:14
  27.6 1.8 %collective-permute-start.3 = (f32[16,2048]{1,0:T(8,128)S(1)}, f32[16,2048]{1,0:T(8,128)S(1)}, u32[]{:S(2)}, u32[]{:S(2)}) collective-permute-start(f32[16,2048]{1,0:T(8,128)S(1)} %get-tuple-element.14), channel_id=1, source_target_pairs={{0,12},{4,16},{8,20},{12,24},{16,28},{1,13},{5,17},{9,21},{13,25},... | collective-permute-start | bytes 393224 | tf_op jit(solution)/shard_map/ppermute | solution.py:14
  29.4 1.3 %collective-permute-start.4 = (f32[16,2048]{1,0:T(8,128)S(1)}, f32[16,2048]{1,0:T(8,128)S(1)}, u32[]{:S(2)}, u32[]{:S(2)}) collective-permute-start(f32[16,2048]{1,0:T(8,128)S(1)} %get-tuple-element.14), channel_id=1, source_target_pairs={{0,16},{4,20},{8,24},{12,28},{1,17},{5,21},{9,25},{13,29},{2,18},{... | collective-permute-start | bytes 393224 | tf_op jit(solution)/shard_map/ppermute | solution.py:14
  30.7 1.3 %collective-permute-start.5 = (f32[16,2048]{1,0:T(8,128)S(1)}, f32[16,2048]{1,0:T(8,128)S(1)}, u32[]{:S(2)}, u32[]{:S(2)}) collective-permute-start(f32[16,2048]{1,0:T(8,128)S(1)} %get-tuple-element.14), channel_id=1, source_target_pairs={{0,20},{4,24},{8,28},{1,21},{5,25},{9,29},{2,22},{6,26},{10,30},{3... | collective-permute-start | bytes 393224 | tf_op jit(solution)/shard_map/ppermute | solution.py:14
  32.0 0.0 collective-permute-done.1
  32.0 0.7 %collective-permute-start.6 = (f32[16,2048]{1,0:T(8,128)S(1)}, f32[16,2048]{1,0:T(8,128)S(1)}, u32[]{:S(2)}, u32[]{:S(2)}) collective-permute-start(f32[16,2048]{1,0:T(8,128)S(1)} %get-tuple-element.14), channel_id=1, source_target_pairs={{0,24},{4,28},{1,25},{5,29},{2,26},{6,30},{3,27},{7,31}} | collective-permute-start | bytes 393224 | tf_op jit(solution)/shard_map/ppermute | solution.py:14
  32.7 0.0 collective-permute-done.2
  32.7 0.8 %collective-permute-start.7 = (f32[16,2048]{1,0:T(8,128)S(1)}, f32[16,2048]{1,0:T(8,128)S(1)}, u32[]{:S(2)}, u32[]{:S(2)}) collective-permute-start(f32[16,2048]{1,0:T(8,128)S(1)} %get-tuple-element.14), channel_id=1, source_target_pairs={{0,28},{1,29},{2,30},{3,31}} | collective-permute-start | bytes 393224 | tf_op jit(solution)/shard_map/ppermute | solution.py:14
  33.6 0.0 collective-permute-done.3
  33.6 6.1 %collective-permute-done.4 = f32[16,2048]{1,0:T(8,128)S(1)} collective-permute-done((f32[16,2048]{1,0:T(8,128)S(1)}, f32[16,2048]{1,0:T(8,128)S(1)}, u32[]{:S(2)}, u32[]{:S(2)}) %collective-permute-start.4) | collective-permute-done | bytes 131104 | tf_op jit(solution)/shard_map/ppermute | solution.py:14
  39.7 1.4 %collective-permute-done.5 = f32[16,2048]{1,0:T(8,128)S(1)} collective-permute-done((f32[16,2048]{1,0:T(8,128)S(1)}, f32[16,2048]{1,0:T(8,128)S(1)}, u32[]{:S(2)}, u32[]{:S(2)}) %collective-permute-start.5) | collective-permute-done | bytes 131104 | tf_op jit(solution)/shard_map/ppermute | solution.py:14
  41.1 0.0 collective-permute-done.6
  41.1 0.0 collective-permute-done.7
  41.1 0.2 add_multiply_fusion
  41.3 0.0 copy-start.4
  41.3 5.3 %multiply_reduce_fusion = f32[128,2048]{1,0:T(8,128)S(1)} fusion(f32[16,2048]{1,0:T(8,128)S(1)} %add_multiply_fusion, f32[128]{0:T(128)S(1)} %broadcast_add_fusion, f32[16,2048]{1,0:T(8,128)S(1)} %bitcast_negate_fusion), kind=kLoop, calls=%fused_computation | loop fusion | flops 12320768 | bytes 1311232 | tf_op jit(solution)/shard_map/reduce_sum | solution.py:124
  46.6 0.0 copy-done.4
  46.6 0.0 copy-start.7
  46.6 0.4 multiply_reduce_fusion.2
  47.1 1.6 %collective-permute-start.8 = (f32[128]{0:T(128)S(1)}, f32[128]{0:T(128)S(1)}, u32[]{:S(2)}, u32[]{:S(2)}) collective-permute-start(f32[128]{0:T(128)S(1)} %get-tuple-element.15), channel_id=1, source_target_pairs={{0,1},{1,0},{2,3},{3,2},{4,5},{5,4},{6,7},{7,6},{8,9},{9,8},{10,11... | collective-permute-start | bytes 1544 | tf_op jit(solution)/shard_map/ppermute | solution.py:37
  48.7 2.0 %collective-permute-done.8 = f32[128]{0:T(128)S(1)} collective-permute-done((f32[128]{0:T(128)S(1)}, f32[128]{0:T(128)S(1)}, u32[]{:S(2)}, u32[]{:S(2)}) %collective-permute-start.8) | collective-permute-done | bytes 544 | tf_op jit(solution)/shard_map/ppermute | solution.py:37
  50.7 2.6 %collective-permute-start.9 = (f32[128]{0:T(128)S(1)}, f32[128]{0:T(128)S(1)}, u32[]{:S(2)}, u32[]{:S(2)}) collective-permute-start(f32[128]{0:T(128)S(1)} %add.56), channel_id=1, source_target_pairs={{0,2},{1,3},{2,0},{3,1},{4,6},{5,7},{6,4},{7,5},{8,10},{9,11},{10,... | collective-permute-start | bytes 1544 | tf_op jit(solution)/shard_map/ppermute | solution.py:37
  53.3 1.9 %collective-permute-done.9 = f32[128]{0:T(128)S(1)} collective-permute-done((f32[128]{0:T(128)S(1)}, f32[128]{0:T(128)S(1)}, u32[]{:S(2)}, u32[]{:S(2)}) %collective-permute-start.9) | collective-permute-done | bytes 544 | tf_op jit(solution)/shard_map/ppermute | solution.py:37
  55.2 0.0 copy-done.7
  55.2 1.0 %multiply_convert_fusion = bf16[128,2048]{1,0:T(8,128)(2,1)} fusion(f32[128,2048]{1,0:T(8,128)S(1)} %get-tuple-element.16, f32[2048]{0:T(1024)S(1)} %copy-done.7, f32[128]{0:T(128)S(1)} %add_rsqrt_fusion), kind=kLoop, calls=%fused_computation.10 | loop fusion | flops 786432 | bytes 1581568 | tf_op jit(solution)/shard_map/convert_element_type | solution.py:129
  (6 shorter events, 0.0 us)
Async XLA Ops:
  0.8 5.3 %copy-start = (bf16[128,2048]{1,0:T(8,128)(2,1)S(1)}, bf16[128,2048]{1,0:T(8,128)(2,1)}, u32[]{:S(2)}) copy-start(bf16[128,2048]{1,0:T(8,128)(2,1)} %q_ref.1) | copy-start | bytes 1572868
  0.8 5.3 %copy-start.1 = (bf16[128,2048]{1,0:T(8,128)(2,1)S(1)}, bf16[128,2048]{1,0:T(8,128)(2,1)}, u32[]{:S(2)}) copy-start(bf16[128,2048]{1,0:T(8,128)(2,1)} %k_ref.1) | copy-start | bytes 1572868
  0.8 5.3 %copy-start.2 = (bf16[128,2048]{1,0:T(8,128)(2,1)S(1)}, bf16[128,2048]{1,0:T(8,128)(2,1)}, u32[]{:S(2)}) copy-start(bf16[128,2048]{1,0:T(8,128)(2,1)} %v_ref.1) | copy-start | bytes 1572868
  0.9 5.3 %copy-start.3 = (f32[3,3,2048]{2,1,0:T(4,128)S(1)}, f32[3,3,2048]{2,1,0:T(4,128)}, u32[]{:S(2)}) copy-start(f32[3,3,2048]{2,1,0:T(4,128)} %taps_ref.1) | copy-start | bytes 221188
  0.9 5.3 %collective-permute-start = (bf16[3,2,2048]{2,1,0:T(2,128)(2,1)S(1)}, bf16[3,2,2048]{2,1,0:T(2,128)(2,1)S(1)}, u32[]{:S(2)}, u32[]{:S(2)}) collective-permute-start(bf16[3,2,2048]{2,1,0:T(2,128)(2,1)S(1)} %pad_maximum_fusion), channel_id=1, source_target_pairs={{0,4},{4,8},{8,12},{12,16},{16,20},{20,24},{24,28},{1,5},{5,9},{9,... | collective-permute-start | bytes 73736 | tf_op jit(solution)/shard_map/ppermute | solution.py:14
  5.8 6.1 %copy-start.5 = (f32[2048,16]{0,1:T(8,128)S(1)}, f32[2048,16]{0,1:T(8,128)}, u32[]{:S(2)}) copy-start(f32[2048,16]{0,1:T(8,128)} %param.12) | copy-start | bytes 393220
  5.8 6.1 %copy-start.6 = (f32[2048,16]{0,1:T(8,128)S(1)}, f32[2048,16]{0,1:T(8,128)}, u32[]{:S(2)}) copy-start(f32[2048,16]{0,1:T(8,128)} %param.13) | copy-start | bytes 393220
  20.9 11.1 %collective-permute-start.1 = (f32[16,2048]{1,0:T(8,128)S(1)}, f32[16,2048]{1,0:T(8,128)S(1)}, u32[]{:S(2)}, u32[]{:S(2)}) collective-permute-start(f32[16,2048]{1,0:T(8,128)S(1)} %get-tuple-element.14), channel_id=1, source_target_pairs={{0,4},{4,8},{8,12},{12,16},{16,20},{20,24},{24,28},{1,5},{5,9},{9,... | collective-permute-start | bytes 393224 | tf_op jit(solution)/shard_map/ppermute | solution.py:14
  24.2 8.5 %collective-permute-start.2 = (f32[16,2048]{1,0:T(8,128)S(1)}, f32[16,2048]{1,0:T(8,128)S(1)}, u32[]{:S(2)}, u32[]{:S(2)}) collective-permute-start(f32[16,2048]{1,0:T(8,128)S(1)} %get-tuple-element.14), channel_id=1, source_target_pairs={{0,8},{4,12},{8,16},{12,20},{16,24},{20,28},{1,9},{5,13},{9,17},{1... | collective-permute-start | bytes 393224 | tf_op jit(solution)/shard_map/ppermute | solution.py:14
  27.6 6.0 %collective-permute-start.3 = (f32[16,2048]{1,0:T(8,128)S(1)}, f32[16,2048]{1,0:T(8,128)S(1)}, u32[]{:S(2)}, u32[]{:S(2)}) collective-permute-start(f32[16,2048]{1,0:T(8,128)S(1)} %get-tuple-element.14), channel_id=1, source_target_pairs={{0,12},{4,16},{8,20},{12,24},{16,28},{1,13},{5,17},{9,21},{13,25},... | collective-permute-start | bytes 393224 | tf_op jit(solution)/shard_map/ppermute | solution.py:14
  29.4 10.3 %collective-permute-start.4 = (f32[16,2048]{1,0:T(8,128)S(1)}, f32[16,2048]{1,0:T(8,128)S(1)}, u32[]{:S(2)}, u32[]{:S(2)}) collective-permute-start(f32[16,2048]{1,0:T(8,128)S(1)} %get-tuple-element.14), channel_id=1, source_target_pairs={{0,16},{4,20},{8,24},{12,28},{1,17},{5,21},{9,25},{13,29},{2,18},{... | collective-permute-start | bytes 393224 | tf_op jit(solution)/shard_map/ppermute | solution.py:14
  30.7 10.4 %collective-permute-start.5 = (f32[16,2048]{1,0:T(8,128)S(1)}, f32[16,2048]{1,0:T(8,128)S(1)}, u32[]{:S(2)}, u32[]{:S(2)}) collective-permute-start(f32[16,2048]{1,0:T(8,128)S(1)} %get-tuple-element.14), channel_id=1, source_target_pairs={{0,20},{4,24},{8,28},{1,21},{5,25},{9,29},{2,22},{6,26},{10,30},{3... | collective-permute-start | bytes 393224 | tf_op jit(solution)/shard_map/ppermute | solution.py:14
  32.0 9.1 %collective-permute-start.6 = (f32[16,2048]{1,0:T(8,128)S(1)}, f32[16,2048]{1,0:T(8,128)S(1)}, u32[]{:S(2)}, u32[]{:S(2)}) collective-permute-start(f32[16,2048]{1,0:T(8,128)S(1)} %get-tuple-element.14), channel_id=1, source_target_pairs={{0,24},{4,28},{1,25},{5,29},{2,26},{6,30},{3,27},{7,31}} | collective-permute-start | bytes 393224 | tf_op jit(solution)/shard_map/ppermute | solution.py:14
  32.7 8.4 %collective-permute-start.7 = (f32[16,2048]{1,0:T(8,128)S(1)}, f32[16,2048]{1,0:T(8,128)S(1)}, u32[]{:S(2)}, u32[]{:S(2)}) collective-permute-start(f32[16,2048]{1,0:T(8,128)S(1)} %get-tuple-element.14), channel_id=1, source_target_pairs={{0,28},{1,29},{2,30},{3,31}} | collective-permute-start | bytes 393224 | tf_op jit(solution)/shard_map/ppermute | solution.py:14
  41.3 5.3 %copy-start.4 = (bf16[128,2048]{1,0:T(8,128)(2,1)S(1)}, bf16[128,2048]{1,0:T(8,128)(2,1)}, u32[]{:S(2)}) copy-start(bf16[128,2048]{1,0:T(8,128)(2,1)} %param.14) | copy-start | bytes 1572868
  46.6 8.5 %copy-start.7 = (f32[2048]{0:T(1024)S(1)}, f32[2048]{0:T(1024)}, u32[]{:S(2)}) copy-start(f32[2048]{0:T(1024)} %param.15) | copy-start | bytes 24580
  47.1 3.6 %collective-permute-start.8 = (f32[128]{0:T(128)S(1)}, f32[128]{0:T(128)S(1)}, u32[]{:S(2)}, u32[]{:S(2)}) collective-permute-start(f32[128]{0:T(128)S(1)} %get-tuple-element.15), channel_id=1, source_target_pairs={{0,1},{1,0},{2,3},{3,2},{4,5},{5,4},{6,7},{7,6},{8,9},{9,8},{10,11... | collective-permute-start | bytes 1544 | tf_op jit(solution)/shard_map/ppermute | solution.py:37
  50.7 4.5 %collective-permute-start.9 = (f32[128]{0:T(128)S(1)}, f32[128]{0:T(128)S(1)}, u32[]{:S(2)}, u32[]{:S(2)}) collective-permute-start(f32[128]{0:T(128)S(1)} %add.56), channel_id=1, source_target_pairs={{0,2},{1,3},{2,0},{3,1},{4,6},{5,7},{6,4},{7,5},{8,10},{9,11},{10,... | collective-permute-start | bytes 1544 | tf_op jit(solution)/shard_map/ppermute | solution.py:37

commit v8 on v6

--- a/solution.py
+++ b/solution.py
@@ -121,8 +121,10 @@
     incoming, outputs = scan_in(ending, decay, rows, "ctx", local)
     times = jnp.arange(rows, dtype=jnp.int32).astype(jnp.float32) + 1.0
     weights = weight * incoming
-    mixed_in = jnp.sum(jnp.exp(-decay[:, None, :] * times[None, :, None]) * weights[:, None, :], axis=0)
-    mixed = outputs + mixed_in
+    mixed_in = outputs
+    for m in range(decay.shape[0]):
+        mixed_in = mixed_in + jnp.exp(-decay[m][None, :] * times[:, None]) * weights[m][None, :]
+    mixed = mixed_in
     stream = resid.astype(jnp.float32) + q_feat * mixed
     squares = butterfly_sum(jnp.sum(stream * stream, axis=1), "tp")
     scale = lax.rsqrt(squares / D + 1e-05)

time: 53 us -> 51.1 us (0.964)
  other arithmetic: 19.5 us -> 17.8 us
    reduce_sum x1 -> x0, other arithmetic: 5.31 us -> none  [per_device(): jnp.sum(jnp.exp(-decay[:, None, :] * times[None, :, None]) * weights[:, N...]
    reduce_sum x1, other arithmetic: 0.42 us -> 4.02 us  [per_device(): squares = butterfly_sum(jnp.sum(stream * stream, axis=1), 'tp')]
where the time goes in v8:
time: 51.1 us; the launch traced here: 50.7 us
  starting transfers between devices  22.8 us (45%)
  other arithmetic  17.8 us (35%)
  Pallas kernels  5.73 us (11%)
  waiting for transfers between devices  3.89 us (8%)
    ppermute x8, starting transfers between devices, from_behind(): return lax.ppermute(block, axis, route)  18.5 us
    another operation x1, other arithmetic, local(): running = jnp.cumsum(values[None, :, :] * grow, axis=1) * fade  8.88 us
    pallas_call x1, Pallas kernels, front(): pl.pallas_call(front_kernel, out_shape=(jax.ShapeDtypeStruct((rows, width...  5.73 us
    ppermute x2, starting transfers between devices, butterfly_sum(): lax.ppermute(value, axis, [(i, i ^ step) for i in range(count)])  4.23 us
    reduce_sum x1, other arithmetic, per_device(): squares = butterfly_sum(jnp.sum(stream * stream, axis=1), 'tp')  4.02 us
    ppermute x2, waiting for transfers between devices, butterfly_sum(): lax.ppermute(value, axis, [(i, i ^ step) for i in range(count)])  3.87 us
    exp x1, other arithmetic, front(): jnp.exp(-decay[:, None, :] * (8.0 * (chunks - 1 - jnp.arange(chunks, dtyp...  1.67 us
  transfers between devices with their start and end apart: 10, of which 2 were waited for; matrix products, arithmetic and copies ran while one was open for 23% of the time, Pallas kernels for 0%

profile of v8, /device:TPU:0, one launch (start us, length us, event | category | flops | bytes accessed | tf_op | source)
XLA Modules:
  0.0 50.7 jit_solution(5475709259039009858)
XLA Ops:
  0.0 0.8 %pad_maximum_fusion = bf16[3,2,2048]{2,1,0:T(2,128)(2,1)S(1)} fusion(bf16[1,128,2048]{2,1,0:T(8,128)(2,1)} %bitcast.43, bf16[1,128,2048]{2,1,0:T(8,128)(2,1)} %bitcast.42, bf16[1,128,2048]{2,1,0:T(8,128)(2,1)} %bitcast.41), kind=kLoop, calls=%fused_computation.14 | loop fusion | flops 73728 | bytes 1597440 | tf_op jit(solution)/shard_map/stack | solution.py:96
  0.8 0.0 copy-start.4
  0.8 0.0 copy-start
  0.8 0.0 copy-start.1
  0.9 0.0 copy-start.2
  0.9 0.0 copy-start.3
  0.9 2.5 %collective-permute-start = (bf16[3,2,2048]{2,1,0:T(2,128)(2,1)S(1)}, bf16[3,2,2048]{2,1,0:T(2,128)(2,1)S(1)}, u32[]{:S(2)}, u32[]{:S(2)}) collective-permute-start(bf16[3,2,2048]{2,1,0:T(2,128)(2,1)S(1)} %pad_maximum_fusion), channel_id=1, source_target_pairs={{0,4},{4,8},{8,12},{12,16},{16,20},{20,24},{24,28},{1,5},{5,9},{9,... | collective-permute-start | bytes 73736 | tf_op jit(solution)/shard_map/ppermute | solution.py:14
  3.4 0.9 %bitcast_negate_fusion = f32[16,2048]{1,0:T(8,128)S(1)} fusion(f32[2048,16]{0,1:T(8,128)} %param.12), kind=kLoop, calls=%fused_computation.37 | loop fusion | flops 32768 | bytes 262144 | tf_op jit(solution)/shard_map/neg | solution.py:73
  4.4 1.7 %multiply_exponential_fusion.coarse_ref = f32[16,16,2048]{2,1,0:T(8,128)} fusion(f32[16]{0:T(128)S(1)} %subtract_multiply_fusion, f32[16,2048]{1,0:T(8,128)S(1)} %bitcast_negate_fusion), kind=kLoop, calls=%fused_computation.8 | loop fusion | flops 524288 | bytes 2228288 | tf_op jit(solution)/shard_map/exp | solution.py:73
  6.0 0.2 multiply_exponential_fusion.1.fine_ref
  6.3 0.0 copy-done.4
  6.3 0.1 slice_negate_fusion.15
  6.4 0.0 copy-start.5
  6.4 0.0 collective-permute-done.halo_ref
  6.4 0.0 copy-done
  6.4 0.0 copy-done.1
  6.5 0.0 copy-done.2
  6.5 0.0 copy-done.3
  6.5 5.7 %shard_map.82 = (f32[128,2048]{1,0:T(8,128)S(1)}, f32[128,2048]{1,0:T(8,128)S(1)}, f32[16,2048]{1,0:T(8,128)S(1)}) custom-call(bf16[128,2048]{1,0:T(8,128)(2,1)S(1)} %copy-done, bf16[128,2048]{1,0:T(8,128)(2,1)S(1)} %copy-done.1, bf16[128,2048]{1,0:T(8,128)(2,1)S(1)} %copy-done.2, bf16[3,2,2048]{2,1,0:T(2,128)(2,1)S(1)} %collective-permute-done.halo_ref, ...), custom_call_target="tpu_custom_call" | custom-call | flops 21495808 | bytes 3670016 | tf_op jit(solution)/shard_map/pallas_call | solution.py:76
  12.2 4.5 %collective-permute-start.1 = (f32[16,2048]{1,0:T(8,128)S(1)}, f32[16,2048]{1,0:T(8,128)S(1)}, u32[]{:S(2)}, u32[]{:S(2)}) collective-permute-start(f32[16,2048]{1,0:T(8,128)S(1)} %get-tuple-element.17), channel_id=1, source_target_pairs={{0,4},{4,8},{8,12},{12,16},{16,20},{20,24},{24,28},{1,5},{5,9},{9,... | collective-permute-start | bytes 393224 | tf_op jit(solution)/shard_map/ppermute | solution.py:14
  16.7 3.4 %collective-permute-start.2 = (f32[16,2048]{1,0:T(8,128)S(1)}, f32[16,2048]{1,0:T(8,128)S(1)}, u32[]{:S(2)}, u32[]{:S(2)}) collective-permute-start(f32[16,2048]{1,0:T(8,128)S(1)} %get-tuple-element.17), channel_id=1, source_target_pairs={{0,8},{4,12},{8,16},{12,20},{16,24},{20,28},{1,9},{5,13},{9,17},{1... | collective-permute-start | bytes 393224 | tf_op jit(solution)/shard_map/ppermute | solution.py:14
  20.1 2.9 %collective-permute-start.3 = (f32[16,2048]{1,0:T(8,128)S(1)}, f32[16,2048]{1,0:T(8,128)S(1)}, u32[]{:S(2)}, u32[]{:S(2)}) collective-permute-start(f32[16,2048]{1,0:T(8,128)S(1)} %get-tuple-element.17), channel_id=1, source_target_pairs={{0,12},{4,16},{8,20},{12,24},{16,28},{1,13},{5,17},{9,21},{13,25},... | collective-permute-start | bytes 393224 | tf_op jit(solution)/shard_map/ppermute | solution.py:14
  23.1 1.3 %collective-permute-start.4 = (f32[16,2048]{1,0:T(8,128)S(1)}, f32[16,2048]{1,0:T(8,128)S(1)}, u32[]{:S(2)}, u32[]{:S(2)}) collective-permute-start(f32[16,2048]{1,0:T(8,128)S(1)} %get-tuple-element.17), channel_id=1, source_target_pairs={{0,16},{4,20},{8,24},{12,28},{1,17},{5,21},{9,25},{13,29},{2,18},{... | collective-permute-start | bytes 393224 | tf_op jit(solution)/shard_map/ppermute | solution.py:14
  24.4 1.3 %collective-permute-start.5 = (f32[16,2048]{1,0:T(8,128)S(1)}, f32[16,2048]{1,0:T(8,128)S(1)}, u32[]{:S(2)}, u32[]{:S(2)}) collective-permute-start(f32[16,2048]{1,0:T(8,128)S(1)} %get-tuple-element.17), channel_id=1, source_target_pairs={{0,20},{4,24},{8,28},{1,21},{5,25},{9,29},{2,22},{6,26},{10,30},{3... | collective-permute-start | bytes 393224 | tf_op jit(solution)/shard_map/ppermute | solution.py:14
  25.7 0.0 collective-permute-done.1
  25.7 1.3 %collective-permute-start.6 = (f32[16,2048]{1,0:T(8,128)S(1)}, f32[16,2048]{1,0:T(8,128)S(1)}, u32[]{:S(2)}, u32[]{:S(2)}) collective-permute-start(f32[16,2048]{1,0:T(8,128)S(1)} %get-tuple-element.17), channel_id=1, source_target_pairs={{0,24},{4,28},{1,25},{5,29},{2,26},{6,30},{3,27},{7,31}} | collective-permute-start | bytes 393224 | tf_op jit(solution)/shard_map/ppermute | solution.py:14
  27.0 0.0 collective-permute-done.2
  27.0 1.3 %collective-permute-start.7 = (f32[16,2048]{1,0:T(8,128)S(1)}, f32[16,2048]{1,0:T(8,128)S(1)}, u32[]{:S(2)}, u32[]{:S(2)}) collective-permute-start(f32[16,2048]{1,0:T(8,128)S(1)} %get-tuple-element.17), channel_id=1, source_target_pairs={{0,28},{1,29},{2,30},{3,31}} | collective-permute-start | bytes 393224 | tf_op jit(solution)/shard_map/ppermute | solution.py:14
  28.3 0.0 copy-done.5
  28.3 0.0 copy-start.7
  28.3 8.9 %multiply_reduce_fusion = f32[128,2048]{1,0:T(8,128)S(1)} fusion(f32[16,2048]{1,0:T(8,128)S(1)} %bitcast.46, f32[16,2048]{1,0:T(8,128)S(1)} %bitcast_negate_fusion, f32[128]{0:T(128)S(1)} %iota_convert_fusion, f32[16,2048]{1,0:T(8,128)S(1)} %bitcast.45, f32[128,2048]{1,0:T(8,128)S(1)} %get-tuple-element.18), kind=kOutput, calls=%fused_computation | output fusion | flops 557580288 | bytes 2490880 | tf_op jit(solution)/shard_map/jit(cumsum)/reduce_window_sum | solution.py:117
  37.2 0.0 collective-permute-done.3
  37.2 0.0 collective-permute-done.4
  37.2 0.0 collective-permute-done.5
  37.3 0.0 collective-permute-done.6
  37.3 0.0 collective-permute-done.7
  37.3 0.2 add_multiply_fusion
  37.5 0.1 fusion.7
  37.6 0.0 copy-done.7
  37.6 0.0 copy-start.6
  37.6 4.0 %multiply_reduce_fusion.1 = (f32[128]{0:T(128)S(1)}, f32[128,2048]{1,0:T(8,128)S(1)}) fusion(f32[128,2048]{1,0:T(8,128)S(1)} %get-tuple-element.16, f32[2048]{0:T(1024)S(1)} %bitcast.64, f32[2048]{0:T(1024)S(1)} %bitcast.62, f32[2048]{0:T(1024)S(1)} %bitcast.65, f32[2048]{0:T(1024)S(1)} %bitcast.48, f32[2048]{0:T(1024)S(1)} %bitcast.66, ...), kind=kLoop, calls=%fused_computation.10 | loop fusion | flops 13893504 | bytes 3933184 | tf_op jit(solution)/shard_map/reduce_sum | solution.py:129
  41.6 1.6 %collective-permute-start.8 = (f32[128]{0:T(128)S(1)}, f32[128]{0:T(128)S(1)}, u32[]{:S(2)}, u32[]{:S(2)}) collective-permute-start(f32[128]{0:T(128)S(1)} %get-tuple-element.27), channel_id=1, source_target_pairs={{0,1},{1,0},{2,3},{3,2},{4,5},{5,4},{6,7},{7,6},{8,9},{9,8},{10,11... | collective-permute-start | bytes 1544 | tf_op jit(solution)/shard_map/ppermute | solution.py:37
  43.2 2.0 %collective-permute-done.8 = f32[128]{0:T(128)S(1)} collective-permute-done((f32[128]{0:T(128)S(1)}, f32[128]{0:T(128)S(1)}, u32[]{:S(2)}, u32[]{:S(2)}) %collective-permute-start.8) | collective-permute-done | bytes 544 | tf_op jit(solution)/shard_map/ppermute | solution.py:37
  45.2 2.6 %collective-permute-start.9 = (f32[128]{0:T(128)S(1)}, f32[128]{0:T(128)S(1)}, u32[]{:S(2)}, u32[]{:S(2)}) collective-permute-start(f32[128]{0:T(128)S(1)} %add.146), channel_id=1, source_target_pairs={{0,2},{1,3},{2,0},{3,1},{4,6},{5,7},{6,4},{7,5},{8,10},{9,11},{10,... | collective-permute-start | bytes 1544 | tf_op jit(solution)/shard_map/ppermute | solution.py:37
  47.8 1.9 %collective-permute-done.9 = f32[128]{0:T(128)S(1)} collective-permute-done((f32[128]{0:T(128)S(1)}, f32[128]{0:T(128)S(1)}, u32[]{:S(2)}, u32[]{:S(2)}) %collective-permute-start.9) | collective-permute-done | bytes 544 | tf_op jit(solution)/shard_map/ppermute | solution.py:37
  49.7 0.0 copy-done.6
  49.7 1.0 %multiply_convert_fusion = bf16[128,2048]{1,0:T(8,128)(2,1)} fusion(f32[128,2048]{1,0:T(8,128)S(1)} %get-tuple-element.28, f32[2048]{0:T(1024)S(1)} %copy-done.6, f32[128]{0:T(128)S(1)} %add_rsqrt_fusion), kind=kLoop, calls=%fused_computation.9 | loop fusion | flops 786432 | bytes 1581568 | tf_op jit(solution)/shard_map/convert_element_type | solution.py:131
  (6 shorter events, 0.0 us)
Async XLA Ops:
  0.8 5.4 %copy-start.4 = (f32[2048,16]{0,1:T(8,128)S(1)}, f32[2048,16]{0,1:T(8,128)}, u32[]{:S(2)}) copy-start(f32[2048,16]{0,1:T(8,128)} %param.12) | copy-start | bytes 393220
  0.8 5.6 %copy-start = (bf16[128,2048]{1,0:T(8,128)(2,1)S(1)}, bf16[128,2048]{1,0:T(8,128)(2,1)}, u32[]{:S(2)}) copy-start(bf16[128,2048]{1,0:T(8,128)(2,1)} %q_ref.1) | copy-start | bytes 1572868
  0.8 5.6 %copy-start.1 = (bf16[128,2048]{1,0:T(8,128)(2,1)S(1)}, bf16[128,2048]{1,0:T(8,128)(2,1)}, u32[]{:S(2)}) copy-start(bf16[128,2048]{1,0:T(8,128)(2,1)} %k_ref.1) | copy-start | bytes 1572868
  0.9 5.6 %copy-start.2 = (bf16[128,2048]{1,0:T(8,128)(2,1)S(1)}, bf16[128,2048]{1,0:T(8,128)(2,1)}, u32[]{:S(2)}) copy-start(bf16[128,2048]{1,0:T(8,128)(2,1)} %v_ref.1) | copy-start | bytes 1572868
  0.9 5.6 %copy-start.3 = (f32[3,3,2048]{2,1,0:T(4,128)S(1)}, f32[3,3,2048]{2,1,0:T(4,128)}, u32[]{:S(2)}) copy-start(f32[3,3,2048]{2,1,0:T(4,128)} %taps_ref.1) | copy-start | bytes 221188
  0.9 5.5 %collective-permute-start = (bf16[3,2,2048]{2,1,0:T(2,128)(2,1)S(1)}, bf16[3,2,2048]{2,1,0:T(2,128)(2,1)S(1)}, u32[]{:S(2)}, u32[]{:S(2)}) collective-permute-start(bf16[3,2,2048]{2,1,0:T(2,128)(2,1)S(1)} %pad_maximum_fusion), channel_id=1, source_target_pairs={{0,4},{4,8},{8,12},{12,16},{16,20},{20,24},{24,28},{1,5},{5,9},{9,... | collective-permute-start | bytes 73736 | tf_op jit(solution)/shard_map/ppermute | solution.py:14
  6.4 21.9 %copy-start.5 = (f32[2048,16]{0,1:T(8,128)S(1)}, f32[2048,16]{0,1:T(8,128)}, u32[]{:S(2)}) copy-start(f32[2048,16]{0,1:T(8,128)} %param.13) | copy-start | bytes 393220
  12.2 13.5 %collective-permute-start.1 = (f32[16,2048]{1,0:T(8,128)S(1)}, f32[16,2048]{1,0:T(8,128)S(1)}, u32[]{:S(2)}, u32[]{:S(2)}) collective-permute-start(f32[16,2048]{1,0:T(8,128)S(1)} %get-tuple-element.17), channel_id=1, source_target_pairs={{0,4},{4,8},{8,12},{12,16},{16,20},{20,24},{24,28},{1,5},{5,9},{9,... | collective-permute-start | bytes 393224 | tf_op jit(solution)/shard_map/ppermute | solution.py:14
  16.7 10.3 %collective-permute-start.2 = (f32[16,2048]{1,0:T(8,128)S(1)}, f32[16,2048]{1,0:T(8,128)S(1)}, u32[]{:S(2)}, u32[]{:S(2)}) collective-permute-start(f32[16,2048]{1,0:T(8,128)S(1)} %get-tuple-element.17), channel_id=1, source_target_pairs={{0,8},{4,12},{8,16},{12,20},{16,24},{20,28},{1,9},{5,13},{9,17},{1... | collective-permute-start | bytes 393224 | tf_op jit(solution)/shard_map/ppermute | solution.py:14
  20.1 17.1 %collective-permute-start.3 = (f32[16,2048]{1,0:T(8,128)S(1)}, f32[16,2048]{1,0:T(8,128)S(1)}, u32[]{:S(2)}, u32[]{:S(2)}) collective-permute-start(f32[16,2048]{1,0:T(8,128)S(1)} %get-tuple-element.17), channel_id=1, source_target_pairs={{0,12},{4,16},{8,20},{12,24},{16,28},{1,13},{5,17},{9,21},{13,25},... | collective-permute-start | bytes 393224 | tf_op jit(solution)/shard_map/ppermute | solution.py:14
  23.1 14.2 %collective-permute-start.4 = (f32[16,2048]{1,0:T(8,128)S(1)}, f32[16,2048]{1,0:T(8,128)S(1)}, u32[]{:S(2)}, u32[]{:S(2)}) collective-permute-start(f32[16,2048]{1,0:T(8,128)S(1)} %get-tuple-element.17), channel_id=1, source_target_pairs={{0,16},{4,20},{8,24},{12,28},{1,17},{5,21},{9,25},{13,29},{2,18},{... | collective-permute-start | bytes 393224 | tf_op jit(solution)/shard_map/ppermute | solution.py:14
  24.4 12.9 %collective-permute-start.5 = (f32[16,2048]{1,0:T(8,128)S(1)}, f32[16,2048]{1,0:T(8,128)S(1)}, u32[]{:S(2)}, u32[]{:S(2)}) collective-permute-start(f32[16,2048]{1,0:T(8,128)S(1)} %get-tuple-element.17), channel_id=1, source_target_pairs={{0,20},{4,24},{8,28},{1,21},{5,25},{9,29},{2,22},{6,26},{10,30},{3... | collective-permute-start | bytes 393224 | tf_op jit(solution)/shard_map/ppermute | solution.py:14
  25.7 11.6 %collective-permute-start.6 = (f32[16,2048]{1,0:T(8,128)S(1)}, f32[16,2048]{1,0:T(8,128)S(1)}, u32[]{:S(2)}, u32[]{:S(2)}) collective-permute-start(f32[16,2048]{1,0:T(8,128)S(1)} %get-tuple-element.17), channel_id=1, source_target_pairs={{0,24},{4,28},{1,25},{5,29},{2,26},{6,30},{3,27},{7,31}} | collective-permute-start | bytes 393224 | tf_op jit(solution)/shard_map/ppermute | solution.py:14
  27.0 10.3 %collective-permute-start.7 = (f32[16,2048]{1,0:T(8,128)S(1)}, f32[16,2048]{1,0:T(8,128)S(1)}, u32[]{:S(2)}, u32[]{:S(2)}) collective-permute-start(f32[16,2048]{1,0:T(8,128)S(1)} %get-tuple-element.17), channel_id=1, source_target_pairs={{0,28},{1,29},{2,30},{3,31}} | collective-permute-start | bytes 393224 | tf_op jit(solution)/shard_map/ppermute | solution.py:14
  28.3 9.2 %copy-start.7 = (bf16[128,2048]{1,0:T(8,128)(2,1)S(1)}, bf16[128,2048]{1,0:T(8,128)(2,1)}, u32[]{:S(2)}) copy-start(bf16[128,2048]{1,0:T(8,128)(2,1)} %param.14) | copy-start | bytes 1572868
  37.6 12.2 %copy-start.6 = (f32[2048]{0:T(1024)S(1)}, f32[2048]{0:T(1024)}, u32[]{:S(2)}) copy-start(f32[2048]{0:T(1024)} %param.15) | copy-start | bytes 24580
  41.6 3.6 %collective-permute-start.8 = (f32[128]{0:T(128)S(1)}, f32[128]{0:T(128)S(1)}, u32[]{:S(2)}, u32[]{:S(2)}) collective-permute-start(f32[128]{0:T(128)S(1)} %get-tuple-element.27), channel_id=1, source_target_pairs={{0,1},{1,0},{2,3},{3,2},{4,5},{5,4},{6,7},{7,6},{8,9},{9,8},{10,11... | collective-permute-start | bytes 1544 | tf_op jit(solution)/shard_map/ppermute | solution.py:37
  45.2 4.5 %collective-permute-start.9 = (f32[128]{0:T(128)S(1)}, f32[128]{0:T(128)S(1)}, u32[]{:S(2)}, u32[]{:S(2)}) collective-permute-start(f32[128]{0:T(128)S(1)} %add.146), channel_id=1, source_target_pairs={{0,2},{1,3},{2,0},{3,1},{4,6},{5,7},{6,4},{7,5},{8,10},{9,11},{10,... | collective-permute-start | bytes 1544 | tf_op jit(solution)/shard_map/ppermute | solution.py:37

commit v9 on v8

--- a/solution.py
+++ b/solution.py
@@ -14,19 +14,47 @@
     return lax.ppermute(block, axis, route)
 
 
-def scan_in(ending, rate, rows, axis, cover):
+def edge_rows(taps, head, tail):
+    first = taps[0] * head[0] + taps[1] * tail[1] + taps[2] * tail[0]
+    second = taps[0] * head[1] + taps[1] * head[0] + taps[2] * tail[1]
+    return jnp.stack([first, second])
+
+
+def edge_gated(short_filter, head_k, head_v, tail_k, tail_v):
+    keys = edge_rows(short_filter[1], head_k, tail_k)
+    values = edge_rows(short_filter[2], head_v, tail_v)
+    return (keys * values).astype(jnp.bfloat16).astype(jnp.float32)
+
+
+def scan_in(payload, modes, short_filter, decay, rows, axis, cover):
     count = lax.axis_size(axis)
     radix = min(count, 8)
-    arrived = [from_behind(ending, axis, shift) for shift in range(1, radix)]
-    arrived, covered = lax.optimization_barrier((arrived, cover()))
-    incoming = jnp.zeros_like(ending)
+    got = {shift: from_behind(payload, axis, shift) for shift in range(1, radix + 1) if shift < count}
+    got, covered = lax.optimization_barrier((got, cover()))
+    nothing = jnp.zeros_like(payload)
+    first_end = jnp.exp(-decay * (rows - 1))
+    second_end = jnp.exp(-decay * (rows - 2))
+
+    def block_state(shift):
+        piece = got[shift]
+        before = got.get(shift + 1, nothing)
+        start = modes + 2
+        fixed = edge_gated(
+            short_filter, piece[start : start + 2], piece[start + 2 : start + 4],
+            before[start + 6 : start + 8], before[start + 8 : start + 10],
+        )
+        change = fixed - piece[modes : modes + 2]
+        return piece[:modes] + change[0][None, :] * first_end + change[1][None, :] * second_end
+
+    incoming = jnp.zeros((modes, payload.shape[1]), jnp.float32)
     for shift in range(1, radix):
-        incoming = incoming + jnp.exp(-rate * (rows * (shift - 1))) * arrived[shift - 1]
+        incoming = incoming + jnp.exp(-decay * (rows * (shift - 1))) * block_state(shift)
     span = radix - 1
     while span < count - 1:
-        incoming = incoming + jnp.exp(-rate * (rows * span)) * from_behind(incoming, axis, span)
+        incoming = incoming + jnp.exp(-decay * (rows * span)) * from_behind(incoming, axis, span)
         span *= 2
-    return incoming, covered
+    own_tail = got[1][modes + 6 : modes + 12] if 1 in got else nothing[modes + 6 : modes + 12]
+    return incoming, own_tail, covered
 
 
 def butterfly_sum(value, axis):
@@ -93,12 +121,14 @@
 def per_device(q_in, k_in, v_in, short_filter, rate, residue, resid, gain):
     rows, width = q_in.shape
     taps = short_filter.shape[1]
-    stacked = jnp.stack([q_in, k_in, v_in])
-    tail = stacked[:, rows - (taps - 1) :, :]
-    before = from_behind(tail, "ctx", 1)
     decay = rate.T
     weight = residue.T
-    q_feat, values, ending = front(q_in, k_in, v_in, before, short_filter, decay)
+    modes = decay.shape[0]
+    no_halo = jnp.zeros((3, taps - 1, width), q_in.dtype)
+    q_feat, values, ending = front(q_in, k_in, v_in, no_halo, short_filter, decay)
+    heads = jnp.concatenate([k_in[:2], v_in[:2]], axis=0).astype(jnp.float32)
+    tails = jnp.concatenate([q_in[rows - 2 :], k_in[rows - 2 :], v_in[rows - 2 :]], axis=0).astype(jnp.float32)
+    payload = jnp.concatenate([ending, values[:2], heads, tails], axis=0)
     block = min(128, rows)
     blocks = values.reshape(rows // block, block, width)
     offsets = jnp.arange(block, dtype=jnp.int32).astype(jnp.float32)
@@ -118,13 +148,20 @@
             return jnp.sum(running * weight[:, None, :], axis=0)
         return lax.scan(main_step, zeros, blocks)[1].reshape(rows, width)
 
-    incoming, outputs = scan_in(ending, decay, rows, "ctx", local)
+    incoming, own_tail, outputs = scan_in(payload, modes, short_filter, decay, rows, "ctx", local)
+    own_gated = edge_gated(short_filter, heads[0:2], heads[2:4], own_tail[2:4], own_tail[4:6])
+    change = own_gated - values[:2]
+    q_edge = edge_rows(short_filter[0], q_in[:2].astype(jnp.float32), own_tail[0:2])
+    q_feat = jnp.concatenate([q_edge, q_feat[2:]], axis=0)
+    grow_one = jnp.exp(decay)
+    state = incoming + grow_one * change[0][None, :] + grow_one * grow_one * change[1][None, :]
+    spill = change[1] * jnp.sum(weight * grow_one, axis=0)
     times = jnp.arange(rows, dtype=jnp.int32).astype(jnp.float32) + 1.0
-    weights = weight * incoming
+    weights = weight * state
     mixed_in = outputs
     for m in range(decay.shape[0]):
         mixed_in = mixed_in + jnp.exp(-decay[m][None, :] * times[:, None]) * weights[m][None, :]
-    mixed = mixed_in
+    mixed = mixed_in - jnp.concatenate([spill[None, :], jnp.zeros((rows - 1, width), jnp.float32)], axis=0)
     stream = resid.astype(jnp.float32) + q_feat * mixed
     squares = butterfly_sum(jnp.sum(stream * stream, axis=1), "tp")
     scale = lax.rsqrt(squares / D + 1e-05)

time: 51.1 us -> 56.7 us (1.11)
  waiting for transfers between devices: 3.89 us -> 10.2 us
  starting transfers between devices: 22.8 us -> 20.8 us
  other arithmetic: 17.8 us -> 18.9 us
    ppermute x8 -> x7, waiting for transfers between devices: 0.02 us -> 6.29 us  [from_behind(): return lax.ppermute(block, axis, route)]
    ppermute x8 -> x7, starting transfers between devices: 18.5 us -> 16.5 us  [from_behind(): return lax.ppermute(block, axis, route)]
    add x0 -> x11, other arithmetic: none -> 0.87 us  [the longest x9 0.71 us: edge_rows(): first = taps[0] * head[0] + taps[1] * tail[1] + taps[2] * tail[0]]
    another operation x1 -> x0, other arithmetic: 0.82 us -> none  [per_device(): stacked = jnp.stack([q_in, k_in, v_in])]
  transfers between devices with their start and end apart: 10 -> 9, of which waited for: 2 -> 5; matrix products, arithmetic and copies ran while one was open for 23% -> 16% of each run, Pallas kernels for 0% -> 0%
where the time goes in v9:
time: 56.7 us; the launch traced here: 56.4 us
  starting transfers between devices  20.8 us (37%)
  other arithmetic  18.9 us (33%)
  waiting for transfers between devices  10.2 us (18%)
  Pallas kernels  5.77 us (10%)
    ppermute x7, starting transfers between devices, from_behind(): return lax.ppermute(block, axis, route)  16.5 us
    another operation x1, other arithmetic, local(): running = jnp.cumsum(values[None, :, :] * grow, axis=1) * fade  8.85 us
    ppermute x7, waiting for transfers between devices, from_behind(): return lax.ppermute(block, axis, route)  6.29 us
    pallas_call x1, Pallas kernels, front(): pl.pallas_call(front_kernel, out_shape=(jax.ShapeDtypeStruct((rows, width...  5.77 us
    ppermute x2, starting transfers between devices, butterfly_sum(): lax.ppermute(value, axis, [(i, i ^ step) for i in range(count)])  4.23 us
    reduce_sum x1, other arithmetic, per_device(): squares = butterfly_sum(jnp.sum(stream * stream, axis=1), 'tp')  4.2 us
    ppermute x2, waiting for transfers between devices, butterfly_sum(): lax.ppermute(value, axis, [(i, i ^ step) for i in range(count)])  3.87 us
    exp x1, other arithmetic, front(): jnp.exp(-decay[:, None, :] * (8.0 * (chunks - 1 - jnp.arange(chunks, dtyp...  1.69 us
  transfers between devices with their start and end apart: 9, of which 5 were waited for; matrix products, arithmetic and copies ran while one was open for 16% of the time, Pallas kernels for 0%

profile of v9, /device:TPU:0, one launch (start us, length us, event | category | flops | bytes accessed | tf_op | source)
XLA Modules:
  0.0 56.4 jit_solution(2361012137933389790)
XLA Ops:
  0.0 0.0 copy-start.1
  0.0 0.0 copy-start.2
  0.0 0.0 copy-start.3
  0.0 0.0 copy-start
  0.0 1.1 %bitcast_negate_fusion = (f32[16,2048]{1,0:T(8,128)S(1)}, f32[2048]{0:T(1024)S(1)}) fusion(f32[2048,16]{0,1:T(8,128)} %param.12, f32[2048,16]{0,1:T(8,128)} %param.13), kind=kLoop, calls=%fused_computation.233 | loop fusion | flops 96256 | bytes 401408 | tf_op jit(solution)/shard_map/neg | solution.py:101
  1.2 1.7 %multiply_exponential_fusion.coarse_ref = f32[16,16,2048]{2,1,0:T(8,128)} fusion(f32[16]{0:T(128)S(1)} %subtract_multiply_fusion, f32[16,2048]{1,0:T(8,128)S(1)} %get-tuple-element.101), kind=kLoop, calls=%fused_computation.8 | loop fusion | flops 524288 | bytes 2228288 | tf_op jit(solution)/shard_map/exp | solution.py:101
  2.9 0.2 multiply_exponential_fusion.1.fine_ref
  3.1 0.0 copy-done.1
  3.1 0.0 copy-done.2
  3.1 0.0 copy-done.3
  3.2 0.0 copy-done
  3.2 0.0 copy-start.4
  3.2 0.0 copy-start.5
  3.2 5.8 %shard_map.82 = (f32[128,2048]{1,0:T(8,128)S(1)}, f32[128,2048]{1,0:T(8,128)S(1)}, f32[16,2048]{1,0:T(8,128)S(1)}) custom-call(bf16[128,2048]{1,0:T(8,128)(2,1)S(1)} %copy-done.2, bf16[128,2048]{1,0:T(8,128)(2,1)S(1)} %copy-done.3, bf16[128,2048]{1,0:T(8,128)(2,1)S(1)} %copy-done.1, bf16[3,2,2048]{2,1,0:T(2,128)(2,1)S(1)} %broadcast_in_dim.2.halo_ref, ...), custom_call_target="tpu_custom_call" | custom-call | flops 21495808 | bytes 3670016 | tf_op jit(solution)/shard_map/pallas_call | solution.py:104
  9.1 2.4 %collective-permute-start = (f32[28,2048]{1,0:T(8,128)S(1)}, f32[28,2048]{1,0:T(8,128)S(1)}, u32[]{:S(2)}, u32[]{:S(2)}) collective-permute-start(f32[28,2048]{1,0:T(8,128)S(1)} %pad_maximum_fusion), channel_id=1, source_target_pairs={{0,4},{4,8},{8,12},{12,16},{16,20},{20,24},{24,28},{1,5},{5,9},{9,... | collective-permute-start | bytes 688136 | tf_op jit(solution)/shard_map/ppermute | solution.py:14
  11.6 4.4 %collective-permute-start.1 = (f32[28,2048]{1,0:T(8,128)S(1)}, f32[28,2048]{1,0:T(8,128)S(1)}, u32[]{:S(2)}, u32[]{:S(2)}) collective-permute-start(f32[28,2048]{1,0:T(8,128)S(1)} %pad_maximum_fusion), channel_id=1, source_target_pairs={{0,8},{4,12},{8,16},{12,20},{16,24},{20,28},{1,9},{5,13},{9,17},{1... | collective-permute-start | bytes 688136 | tf_op jit(solution)/shard_map/ppermute | solution.py:14
  16.0 4.3 %collective-permute-start.2 = (f32[28,2048]{1,0:T(8,128)S(1)}, f32[28,2048]{1,0:T(8,128)S(1)}, u32[]{:S(2)}, u32[]{:S(2)}) collective-permute-start(f32[28,2048]{1,0:T(8,128)S(1)} %pad_maximum_fusion), channel_id=1, source_target_pairs={{0,12},{4,16},{8,20},{12,24},{16,28},{1,13},{5,17},{9,21},{13,25},... | collective-permute-start | bytes 688136 | tf_op jit(solution)/shard_map/ppermute | solution.py:14
  20.3 1.3 %collective-permute-start.3 = (f32[28,2048]{1,0:T(8,128)S(1)}, f32[28,2048]{1,0:T(8,128)S(1)}, u32[]{:S(2)}, u32[]{:S(2)}) collective-permute-start(f32[28,2048]{1,0:T(8,128)S(1)} %pad_maximum_fusion), channel_id=1, source_target_pairs={{0,16},{4,20},{8,24},{12,28},{1,17},{5,21},{9,25},{13,29},{2,18},{... | collective-permute-start | bytes 688136 | tf_op jit(solution)/shard_map/ppermute | solution.py:14
  21.6 1.3 %collective-permute-start.4 = (f32[28,2048]{1,0:T(8,128)S(1)}, f32[28,2048]{1,0:T(8,128)S(1)}, u32[]{:S(2)}, u32[]{:S(2)}) collective-permute-start(f32[28,2048]{1,0:T(8,128)S(1)} %pad_maximum_fusion), channel_id=1, source_target_pairs={{0,20},{4,24},{8,28},{1,21},{5,25},{9,29},{2,22},{6,26},{10,30},{3... | collective-permute-start | bytes 688136 | tf_op jit(solution)/shard_map/ppermute | solution.py:14
  22.9 0.0 copy-done.4
  22.9 0.0 copy-done.5
  23.0 8.8 %multiply_reduce_fusion = f32[128,2048]{1,0:T(8,128)S(1)} fusion(f32[16,2048]{1,0:T(8,128)S(1)} %bitcast.429, f32[16,2048]{1,0:T(8,128)S(1)} %get-tuple-element.101, f32[128]{0:T(128)S(1)} %iota_convert_fusion, f32[16,2048]{1,0:T(8,128)S(1)} %bitcast.427, f32[128,2048]{1,0:T(8,128)S(1)} %get-tuple-element.17), kind=kOutput, calls=%fused_computation | output fusion | flops 557580288 | bytes 2490880 | tf_op jit(solution)/shard_map/jit(cumsum)/reduce_window_sum | solution.py:147
  31.8 0.0 collective-permute-done
  31.8 1.3 %collective-permute-start.5 = (f32[28,2048]{1,0:T(8,128)S(1)}, f32[28,2048]{1,0:T(8,128)S(1)}, u32[]{:S(2)}, u32[]{:S(2)}) collective-permute-start(f32[28,2048]{1,0:T(8,128)S(1)} %pad_maximum_fusion), channel_id=1, source_target_pairs={{0,24},{4,28},{1,25},{5,29},{2,26},{6,30},{3,27},{7,31}} | collective-permute-start | bytes 688136 | tf_op jit(solution)/shard_map/ppermute | solution.py:14
  33.1 0.0 collective-permute-done.1
  33.1 1.5 %collective-permute-start.6 = (f32[28,2048]{1,0:T(8,128)S(1)}, f32[28,2048]{1,0:T(8,128)S(1)}, u32[]{:S(2)}, u32[]{:S(2)}) collective-permute-start(f32[28,2048]{1,0:T(8,128)S(1)} %pad_maximum_fusion), channel_id=1, source_target_pairs={{0,28},{1,29},{2,30},{3,31}} | collective-permute-start | bytes 688136 | tf_op jit(solution)/shard_map/ppermute | solution.py:14
  34.6 0.1 slice_negate_fusion.15
  34.8 0.1 slice.702
  34.9 0.0 copy-start.7
  34.9 0.0 collective-permute-done.2
  34.9 0.0 collective-permute-done.3
  34.9 3.0 %collective-permute-done.4 = f32[28,2048]{1,0:T(8,128)S(1)} collective-permute-done((f32[28,2048]{1,0:T(8,128)S(1)}, f32[28,2048]{1,0:T(8,128)S(1)}, u32[]{:S(2)}, u32[]{:S(2)}) %collective-permute-start.4) | collective-permute-done | bytes 229408 | tf_op jit(solution)/shard_map/ppermute | solution.py:14
  37.9 0.5 collective-permute-done.5
  38.4 2.8 %collective-permute-done.6 = f32[28,2048]{1,0:T(8,128)S(1)} collective-permute-done((f32[28,2048]{1,0:T(8,128)S(1)}, f32[28,2048]{1,0:T(8,128)S(1)}, u32[]{:S(2)}, u32[]{:S(2)}) %collective-permute-start.6) | collective-permute-done | bytes 229408 | tf_op jit(solution)/shard_map/ppermute | solution.py:14
  41.2 0.1 fusion.52
  41.3 0.1 fusion.54
  41.4 0.1 fusion.53
  41.5 0.1 fusion.56
  41.5 0.1 fusion.58
  41.6 0.1 fusion.60
  41.7 0.1 fusion.59
  41.8 0.1 fusion.62
  41.9 0.1 fusion.78
  42.0 0.1 fusion.64
  42.5 0.1 fusion.82
  42.7 0.4 add_multiply_fusion
  43.0 0.1 fusion.87
  43.1 0.0 copy-done.7
  43.1 0.0 copy-start.6
  43.2 4.2 %multiply_reduce_fusion.1 = (f32[128]{0:T(128)S(1)}, f32[128,2048]{1,0:T(8,128)S(1)}) fusion(f32[1,2048]{1,0:T(1,128)S(1)} %get-tuple-element.118, f32[2048]{0:T(1024)S(1)} %bitcast.464, f32[2048]{0:T(1024)S(1)} %bitcast.461, f32[2048]{0:T(1024)S(1)} %bitcast.465, f32[2048]{0:T(1024)S(1)} %bitcast.462, f32[2048]{0:T(1024)S(1)} %bitcast.466, ...), kind=kLoop, calls=%fused_computation.12 | loop fusion | flops 14679936 | bytes 3941376 | tf_op jit(solution)/shard_map/reduce_sum | solution.py:166
  47.4 1.6 %collective-permute-start.7 = (f32[128]{0:T(128)S(1)}, f32[128]{0:T(128)S(1)}, u32[]{:S(2)}, u32[]{:S(2)}) collective-permute-start(f32[128]{0:T(128)S(1)} %get-tuple-element.27), channel_id=1, source_target_pairs={{0,1},{1,0},{2,3},{3,2},{4,5},{5,4},{6,7},{7,6},{8,9},{9,8},{10,11... | collective-permute-start | bytes 1544 | tf_op jit(solution)/shard_map/ppermute | solution.py:65
  49.0 2.0 %collective-permute-done.7 = f32[128]{0:T(128)S(1)} collective-permute-done((f32[128]{0:T(128)S(1)}, f32[128]{0:T(128)S(1)}, u32[]{:S(2)}, u32[]{:S(2)}) %collective-permute-start.7) | collective-permute-done | bytes 544 | tf_op jit(solution)/shard_map/ppermute | solution.py:65
  51.0 2.6 %collective-permute-start.8 = (f32[128]{0:T(128)S(1)}, f32[128]{0:T(128)S(1)}, u32[]{:S(2)}, u32[]{:S(2)}) collective-permute-start(f32[128]{0:T(128)S(1)} %add.552), channel_id=1, source_target_pairs={{0,2},{1,3},{2,0},{3,1},{4,6},{5,7},{6,4},{7,5},{8,10},{9,11},{10,... | collective-permute-start | bytes 1544 | tf_op jit(solution)/shard_map/ppermute | solution.py:65
  53.6 1.9 %collective-permute-done.8 = f32[128]{0:T(128)S(1)} collective-permute-done((f32[128]{0:T(128)S(1)}, f32[128]{0:T(128)S(1)}, u32[]{:S(2)}, u32[]{:S(2)}) %collective-permute-start.8) | collective-permute-done | bytes 544 | tf_op jit(solution)/shard_map/ppermute | solution.py:65
  55.5 0.0 copy-done.6
  55.5 1.0 %multiply_convert_fusion = bf16[128,2048]{1,0:T(8,128)(2,1)} fusion(f32[128,2048]{1,0:T(8,128)S(1)} %get-tuple-element.28, f32[2048]{0:T(1024)S(1)} %copy-done.6, f32[128]{0:T(128)S(1)} %add_rsqrt_fusion), kind=kLoop, calls=%fused_computation.11 | loop fusion | flops 786432 | bytes 1581568 | tf_op jit(solution)/shard_map/convert_element_type | solution.py:168
  (29 shorter events, 0.6 us)
Async XLA Ops:
  0.0 3.1 %copy-start.1 = (bf16[128,2048]{1,0:T(8,128)(2,1)S(1)}, bf16[128,2048]{1,0:T(8,128)(2,1)}, u32[]{:S(2)}) copy-start(bf16[128,2048]{1,0:T(8,128)(2,1)} %v_ref.1) | copy-start | bytes 1572868
  0.0 3.1 %copy-start.2 = (bf16[128,2048]{1,0:T(8,128)(2,1)S(1)}, bf16[128,2048]{1,0:T(8,128)(2,1)}, u32[]{:S(2)}) copy-start(bf16[128,2048]{1,0:T(8,128)(2,1)} %q_ref.1) | copy-start | bytes 1572868
  0.0 3.1 %copy-start.3 = (bf16[128,2048]{1,0:T(8,128)(2,1)S(1)}, bf16[128,2048]{1,0:T(8,128)(2,1)}, u32[]{:S(2)}) copy-start(bf16[128,2048]{1,0:T(8,128)(2,1)} %k_ref.1) | copy-start | bytes 1572868
  0.0 3.2 %copy-start = (f32[3,3,2048]{2,1,0:T(4,128)S(1)}, f32[3,3,2048]{2,1,0:T(4,128)}, u32[]{:S(2)}) copy-start(f32[3,3,2048]{2,1,0:T(4,128)} %taps_ref.1) | copy-start | bytes 221188
  3.2 19.7 %copy-start.4 = (f32[2048,16]{0,1:T(8,128)S(1)}, f32[2048,16]{0,1:T(8,128)}, u32[]{:S(2)}) copy-start(f32[2048,16]{0,1:T(8,128)} %param.12) | copy-start | bytes 393220
  3.2 19.7 %copy-start.5 = (f32[2048,16]{0,1:T(8,128)S(1)}, f32[2048,16]{0,1:T(8,128)}, u32[]{:S(2)}) copy-start(f32[2048,16]{0,1:T(8,128)} %param.13) | copy-start | bytes 393220
  9.1 22.7 %collective-permute-start = (f32[28,2048]{1,0:T(8,128)S(1)}, f32[28,2048]{1,0:T(8,128)S(1)}, u32[]{:S(2)}, u32[]{:S(2)}) collective-permute-start(f32[28,2048]{1,0:T(8,128)S(1)} %pad_maximum_fusion), channel_id=1, source_target_pairs={{0,4},{4,8},{8,12},{12,16},{16,20},{20,24},{24,28},{1,5},{5,9},{9,... | collective-permute-start | bytes 688136 | tf_op jit(solution)/shard_map/ppermute | solution.py:14
  11.6 21.6 %collective-permute-start.1 = (f32[28,2048]{1,0:T(8,128)S(1)}, f32[28,2048]{1,0:T(8,128)S(1)}, u32[]{:S(2)}, u32[]{:S(2)}) collective-permute-start(f32[28,2048]{1,0:T(8,128)S(1)} %pad_maximum_fusion), channel_id=1, source_target_pairs={{0,8},{4,12},{8,16},{12,20},{16,24},{20,28},{1,9},{5,13},{9,17},{1... | collective-permute-start | bytes 688136 | tf_op jit(solution)/shard_map/ppermute | solution.py:14
  16.0 18.9 %collective-permute-start.2 = (f32[28,2048]{1,0:T(8,128)S(1)}, f32[28,2048]{1,0:T(8,128)S(1)}, u32[]{:S(2)}, u32[]{:S(2)}) collective-permute-start(f32[28,2048]{1,0:T(8,128)S(1)} %pad_maximum_fusion), channel_id=1, source_target_pairs={{0,12},{4,16},{8,20},{12,24},{16,28},{1,13},{5,17},{9,21},{13,25},... | collective-permute-start | bytes 688136 | tf_op jit(solution)/shard_map/ppermute | solution.py:14
  20.3 14.6 %collective-permute-start.3 = (f32[28,2048]{1,0:T(8,128)S(1)}, f32[28,2048]{1,0:T(8,128)S(1)}, u32[]{:S(2)}, u32[]{:S(2)}) collective-permute-start(f32[28,2048]{1,0:T(8,128)S(1)} %pad_maximum_fusion), channel_id=1, source_target_pairs={{0,16},{4,20},{8,24},{12,28},{1,17},{5,21},{9,25},{13,29},{2,18},{... | collective-permute-start | bytes 688136 | tf_op jit(solution)/shard_map/ppermute | solution.py:14
  21.6 16.3 %collective-permute-start.4 = (f32[28,2048]{1,0:T(8,128)S(1)}, f32[28,2048]{1,0:T(8,128)S(1)}, u32[]{:S(2)}, u32[]{:S(2)}) collective-permute-start(f32[28,2048]{1,0:T(8,128)S(1)} %pad_maximum_fusion), channel_id=1, source_target_pairs={{0,20},{4,24},{8,28},{1,21},{5,25},{9,29},{2,22},{6,26},{10,30},{3... | collective-permute-start | bytes 688136 | tf_op jit(solution)/shard_map/ppermute | solution.py:14
  31.8 6.6 %collective-permute-start.5 = (f32[28,2048]{1,0:T(8,128)S(1)}, f32[28,2048]{1,0:T(8,128)S(1)}, u32[]{:S(2)}, u32[]{:S(2)}) collective-permute-start(f32[28,2048]{1,0:T(8,128)S(1)} %pad_maximum_fusion), channel_id=1, source_target_pairs={{0,24},{4,28},{1,25},{5,29},{2,26},{6,30},{3,27},{7,31}} | collective-permute-start | bytes 688136 | tf_op jit(solution)/shard_map/ppermute | solution.py:14
  33.1 8.0 %collective-permute-start.6 = (f32[28,2048]{1,0:T(8,128)S(1)}, f32[28,2048]{1,0:T(8,128)S(1)}, u32[]{:S(2)}, u32[]{:S(2)}) collective-permute-start(f32[28,2048]{1,0:T(8,128)S(1)} %pad_maximum_fusion), channel_id=1, source_target_pairs={{0,28},{1,29},{2,30},{3,31}} | collective-permute-start | bytes 688136 | tf_op jit(solution)/shard_map/ppermute | solution.py:14
  34.9 8.3 %copy-start.7 = (bf16[128,2048]{1,0:T(8,128)(2,1)S(1)}, bf16[128,2048]{1,0:T(8,128)(2,1)}, u32[]{:S(2)}) copy-start(bf16[128,2048]{1,0:T(8,128)(2,1)} %param.14) | copy-start | bytes 1572868
  43.1 12.3 %copy-start.6 = (f32[2048]{0:T(1024)S(1)}, f32[2048]{0:T(1024)}, u32[]{:S(2)}) copy-start(f32[2048]{0:T(1024)} %param.15) | copy-start | bytes 24580
  47.4 3.6 %collective-permute-start.7 = (f32[128]{0:T(128)S(1)}, f32[128]{0:T(128)S(1)}, u32[]{:S(2)}, u32[]{:S(2)}) collective-permute-start(f32[128]{0:T(128)S(1)} %get-tuple-element.27), channel_id=1, source_target_pairs={{0,1},{1,0},{2,3},{3,2},{4,5},{5,4},{6,7},{7,6},{8,9},{9,8},{10,11... | collective-permute-start | bytes 1544 | tf_op jit(solution)/shard_map/ppermute | solution.py:65
  51.0 4.5 %collective-permute-start.8 = (f32[128]{0:T(128)S(1)}, f32[128]{0:T(128)S(1)}, u32[]{:S(2)}, u32[]{:S(2)}) collective-permute-start(f32[128]{0:T(128)S(1)} %add.552), channel_id=1, source_target_pairs={{0,2},{1,3},{2,0},{3,1},{4,6},{5,7},{6,4},{7,5},{8,10},{9,11},{10,... | collective-permute-start | bytes 1544 | tf_op jit(solution)/shard_map/ppermute | solution.py:65

commit v10 on v9

--- a/solution.py
+++ b/solution.py
@@ -30,7 +30,8 @@
     count = lax.axis_size(axis)
     radix = min(count, 8)
     got = {shift: from_behind(payload, axis, shift) for shift in range(1, radix + 1) if shift < count}
-    got, covered = lax.optimization_barrier((got, cover()))
+    covered = cover()
+    got, covered = lax.optimization_barrier((got, covered))
     nothing = jnp.zeros_like(payload)
     first_end = jnp.exp(-decay * (rows - 1))
     second_end = jnp.exp(-decay * (rows - 2))
@@ -118,7 +119,7 @@
     )(q_in, k_in, v_in, before, short_filter, coarse, fine)
 
 
-def per_device(q_in, k_in, v_in, short_filter, rate, residue, resid, gain):
+def mixer(q_in, k_in, v_in, short_filter, rate, residue, resid, gain):
     rows, width = q_in.shape
     taps = short_filter.shape[1]
     decay = rate.T
@@ -180,7 +181,4 @@
         P("tp"),
     )
     out_specs = P("ctx", "tp")
-    step = jax.shard_map(
-        per_device, mesh=mesh, in_specs=in_specs, out_specs=out_specs, check_vma=False
-    )
-    return step
+    return jax.shard_map(mixer, mesh=mesh, in_specs=in_specs, out_specs=out_specs, check_vma=False)

time: 56.7 us -> 56.7 us (level)
  no operation moved by 1% of the time
where the time goes in v10:
time: 56.7 us; the launch traced here: 56.4 us
  starting transfers between devices  20.8 us (37%)
  other arithmetic  18.9 us (33%)
  waiting for transfers between devices  10.2 us (18%)
  Pallas kernels  5.77 us (10%)
    ppermute x7, starting transfers between devices, from_behind(): return lax.ppermute(block, axis, route)  16.5 us
    another operation x1, other arithmetic, local(): running = jnp.cumsum(values[None, :, :] * grow, axis=1) * fade  8.85 us
    ppermute x7, waiting for transfers between devices, from_behind(): return lax.ppermute(block, axis, route)  6.29 us
    pallas_call x1, Pallas kernels, front(): pl.pallas_call(front_kernel, out_shape=(jax.ShapeDtypeStruct((rows, width...  5.77 us
    ppermute x2, starting transfers between devices, butterfly_sum(): lax.ppermute(value, axis, [(i, i ^ step) for i in range(count)])  4.23 us
    reduce_sum x1, other arithmetic, mixer(): squares = butterfly_sum(jnp.sum(stream * stream, axis=1), 'tp')  4.2 us
    ppermute x2, waiting for transfers between devices, butterfly_sum(): lax.ppermute(value, axis, [(i, i ^ step) for i in range(count)])  3.87 us
    exp x1, other arithmetic, front(): jnp.exp(-decay[:, None, :] * (8.0 * (chunks - 1 - jnp.arange(chunks, dtyp...  1.69 us
  transfers between devices with their start and end apart: 9, of which 5 were waited for; matrix products, arithmetic and copies ran while one was open for 16% of the time, Pallas kernels for 0%

profile of v10, /device:TPU:0, one launch (start us, length us, event | category | flops | bytes accessed | tf_op | source)
XLA Modules:
  0.0 56.4 jit_solution(2361012137933389790)
XLA Ops:
  0.0 0.0 copy-start.1
  0.0 0.0 copy-start.2
  0.0 0.0 copy-start.3
  0.0 0.0 copy-start
  0.0 1.1 %bitcast_negate_fusion = (f32[16,2048]{1,0:T(8,128)S(1)}, f32[2048]{0:T(1024)S(1)}) fusion(f32[2048,16]{0,1:T(8,128)} %param.12, f32[2048,16]{0,1:T(8,128)} %param.13), kind=kLoop, calls=%fused_computation.233 | loop fusion | flops 96256 | bytes 401408 | tf_op jit(solution)/shard_map/neg | solution.py:102
  1.2 1.7 %multiply_exponential_fusion.coarse_ref = f32[16,16,2048]{2,1,0:T(8,128)} fusion(f32[16]{0:T(128)S(1)} %subtract_multiply_fusion, f32[16,2048]{1,0:T(8,128)S(1)} %get-tuple-element.101), kind=kLoop, calls=%fused_computation.8 | loop fusion | flops 524288 | bytes 2228288 | tf_op jit(solution)/shard_map/exp | solution.py:102
  2.9 0.2 multiply_exponential_fusion.1.fine_ref
  3.1 0.0 copy-done.1
  3.1 0.0 copy-done.2
  3.1 0.0 copy-done.3
  3.2 0.0 copy-done
  3.2 0.0 copy-start.4
  3.2 0.0 copy-start.5
  3.2 5.8 %shard_map.82 = (f32[128,2048]{1,0:T(8,128)S(1)}, f32[128,2048]{1,0:T(8,128)S(1)}, f32[16,2048]{1,0:T(8,128)S(1)}) custom-call(bf16[128,2048]{1,0:T(8,128)(2,1)S(1)} %copy-done.2, bf16[128,2048]{1,0:T(8,128)(2,1)S(1)} %copy-done.3, bf16[128,2048]{1,0:T(8,128)(2,1)S(1)} %copy-done.1, bf16[3,2,2048]{2,1,0:T(2,128)(2,1)S(1)} %broadcast_in_dim.2.halo_ref, ...), custom_call_target="tpu_custom_call" | custom-call | flops 21495808 | bytes 3670016 | tf_op jit(solution)/shard_map/pallas_call | solution.py:105
  9.1 2.4 %collective-permute-start = (f32[28,2048]{1,0:T(8,128)S(1)}, f32[28,2048]{1,0:T(8,128)S(1)}, u32[]{:S(2)}, u32[]{:S(2)}) collective-permute-start(f32[28,2048]{1,0:T(8,128)S(1)} %pad_maximum_fusion), channel_id=1, source_target_pairs={{0,4},{4,8},{8,12},{12,16},{16,20},{20,24},{24,28},{1,5},{5,9},{9,... | collective-permute-start | bytes 688136 | tf_op jit(solution)/shard_map/ppermute | solution.py:14
  11.6 4.4 %collective-permute-start.1 = (f32[28,2048]{1,0:T(8,128)S(1)}, f32[28,2048]{1,0:T(8,128)S(1)}, u32[]{:S(2)}, u32[]{:S(2)}) collective-permute-start(f32[28,2048]{1,0:T(8,128)S(1)} %pad_maximum_fusion), channel_id=1, source_target_pairs={{0,8},{4,12},{8,16},{12,20},{16,24},{20,28},{1,9},{5,13},{9,17},{1... | collective-permute-start | bytes 688136 | tf_op jit(solution)/shard_map/ppermute | solution.py:14
  16.0 4.3 %collective-permute-start.2 = (f32[28,2048]{1,0:T(8,128)S(1)}, f32[28,2048]{1,0:T(8,128)S(1)}, u32[]{:S(2)}, u32[]{:S(2)}) collective-permute-start(f32[28,2048]{1,0:T(8,128)S(1)} %pad_maximum_fusion), channel_id=1, source_target_pairs={{0,12},{4,16},{8,20},{12,24},{16,28},{1,13},{5,17},{9,21},{13,25},... | collective-permute-start | bytes 688136 | tf_op jit(solution)/shard_map/ppermute | solution.py:14
  20.3 1.3 %collective-permute-start.3 = (f32[28,2048]{1,0:T(8,128)S(1)}, f32[28,2048]{1,0:T(8,128)S(1)}, u32[]{:S(2)}, u32[]{:S(2)}) collective-permute-start(f32[28,2048]{1,0:T(8,128)S(1)} %pad_maximum_fusion), channel_id=1, source_target_pairs={{0,16},{4,20},{8,24},{12,28},{1,17},{5,21},{9,25},{13,29},{2,18},{... | collective-permute-start | bytes 688136 | tf_op jit(solution)/shard_map/ppermute | solution.py:14
  21.6 1.3 %collective-permute-start.4 = (f32[28,2048]{1,0:T(8,128)S(1)}, f32[28,2048]{1,0:T(8,128)S(1)}, u32[]{:S(2)}, u32[]{:S(2)}) collective-permute-start(f32[28,2048]{1,0:T(8,128)S(1)} %pad_maximum_fusion), channel_id=1, source_target_pairs={{0,20},{4,24},{8,28},{1,21},{5,25},{9,29},{2,22},{6,26},{10,30},{3... | collective-permute-start | bytes 688136 | tf_op jit(solution)/shard_map/ppermute | solution.py:14
  22.9 0.0 copy-done.4
  22.9 0.0 copy-done.5
  23.0 8.8 %multiply_reduce_fusion = f32[128,2048]{1,0:T(8,128)S(1)} fusion(f32[16,2048]{1,0:T(8,128)S(1)} %bitcast.429, f32[16,2048]{1,0:T(8,128)S(1)} %get-tuple-element.101, f32[128]{0:T(128)S(1)} %iota_convert_fusion, f32[16,2048]{1,0:T(8,128)S(1)} %bitcast.427, f32[128,2048]{1,0:T(8,128)S(1)} %get-tuple-element.17), kind=kOutput, calls=%fused_computation | output fusion | flops 557580288 | bytes 2490880 | tf_op jit(solution)/shard_map/jit(cumsum)/reduce_window_sum | solution.py:148
  31.8 0.0 collective-permute-done
  31.8 1.3 %collective-permute-start.5 = (f32[28,2048]{1,0:T(8,128)S(1)}, f32[28,2048]{1,0:T(8,128)S(1)}, u32[]{:S(2)}, u32[]{:S(2)}) collective-permute-start(f32[28,2048]{1,0:T(8,128)S(1)} %pad_maximum_fusion), channel_id=1, source_target_pairs={{0,24},{4,28},{1,25},{5,29},{2,26},{6,30},{3,27},{7,31}} | collective-permute-start | bytes 688136 | tf_op jit(solution)/shard_map/ppermute | solution.py:14
  33.1 0.0 collective-permute-done.1
  33.1 1.5 %collective-permute-start.6 = (f32[28,2048]{1,0:T(8,128)S(1)}, f32[28,2048]{1,0:T(8,128)S(1)}, u32[]{:S(2)}, u32[]{:S(2)}) collective-permute-start(f32[28,2048]{1,0:T(8,128)S(1)} %pad_maximum_fusion), channel_id=1, source_target_pairs={{0,28},{1,29},{2,30},{3,31}} | collective-permute-start | bytes 688136 | tf_op jit(solution)/shard_map/ppermute | solution.py:14
  34.6 0.1 slice_negate_fusion.15
  34.8 0.1 slice.702
  34.9 0.0 copy-start.7
  34.9 0.0 collective-permute-done.2
  34.9 0.0 collective-permute-done.3
  34.9 3.0 %collective-permute-done.4 = f32[28,2048]{1,0:T(8,128)S(1)} collective-permute-done((f32[28,2048]{1,0:T(8,128)S(1)}, f32[28,2048]{1,0:T(8,128)S(1)}, u32[]{:S(2)}, u32[]{:S(2)}) %collective-permute-start.4) | collective-permute-done | bytes 229408 | tf_op jit(solution)/shard_map/ppermute | solution.py:14
  37.9 0.5 collective-permute-done.5
  38.4 2.8 %collective-permute-done.6 = f32[28,2048]{1,0:T(8,128)S(1)} collective-permute-done((f32[28,2048]{1,0:T(8,128)S(1)}, f32[28,2048]{1,0:T(8,128)S(1)}, u32[]{:S(2)}, u32[]{:S(2)}) %collective-permute-start.6) | collective-permute-done | bytes 229408 | tf_op jit(solution)/shard_map/ppermute | solution.py:14
  41.2 0.1 fusion.52
  41.3 0.1 fusion.54
  41.4 0.1 fusion.53
  41.5 0.1 fusion.56
  41.5 0.1 fusion.58
  41.6 0.1 fusion.60
  41.7 0.1 fusion.59
  41.8 0.1 fusion.62
  41.9 0.1 fusion.78
  42.0 0.1 fusion.64
  42.5 0.1 fusion.82
  42.7 0.4 add_multiply_fusion
  43.0 0.1 fusion.87
  43.1 0.0 copy-done.7
  43.1 0.0 copy-start.6
  43.2 4.2 %multiply_reduce_fusion.1 = (f32[128]{0:T(128)S(1)}, f32[128,2048]{1,0:T(8,128)S(1)}) fusion(f32[1,2048]{1,0:T(1,128)S(1)} %get-tuple-element.118, f32[2048]{0:T(1024)S(1)} %bitcast.464, f32[2048]{0:T(1024)S(1)} %bitcast.461, f32[2048]{0:T(1024)S(1)} %bitcast.465, f32[2048]{0:T(1024)S(1)} %bitcast.462, f32[2048]{0:T(1024)S(1)} %bitcast.466, ...), kind=kLoop, calls=%fused_computation.12 | loop fusion | flops 14679936 | bytes 3941376 | tf_op jit(solution)/shard_map/reduce_sum | solution.py:167
  47.4 1.6 %collective-permute-start.7 = (f32[128]{0:T(128)S(1)}, f32[128]{0:T(128)S(1)}, u32[]{:S(2)}, u32[]{:S(2)}) collective-permute-start(f32[128]{0:T(128)S(1)} %get-tuple-element.27), channel_id=1, source_target_pairs={{0,1},{1,0},{2,3},{3,2},{4,5},{5,4},{6,7},{7,6},{8,9},{9,8},{10,11... | collective-permute-start | bytes 1544 | tf_op jit(solution)/shard_map/ppermute | solution.py:66
  49.0 2.0 %collective-permute-done.7 = f32[128]{0:T(128)S(1)} collective-permute-done((f32[128]{0:T(128)S(1)}, f32[128]{0:T(128)S(1)}, u32[]{:S(2)}, u32[]{:S(2)}) %collective-permute-start.7) | collective-permute-done | bytes 544 | tf_op jit(solution)/shard_map/ppermute | solution.py:66
  51.0 2.6 %collective-permute-start.8 = (f32[128]{0:T(128)S(1)}, f32[128]{0:T(128)S(1)}, u32[]{:S(2)}, u32[]{:S(2)}) collective-permute-start(f32[128]{0:T(128)S(1)} %add.552), channel_id=1, source_target_pairs={{0,2},{1,3},{2,0},{3,1},{4,6},{5,7},{6,4},{7,5},{8,10},{9,11},{10,... | collective-permute-start | bytes 1544 | tf_op jit(solution)/shard_map/ppermute | solution.py:66
  53.6 1.9 %collective-permute-done.8 = f32[128]{0:T(128)S(1)} collective-permute-done((f32[128]{0:T(128)S(1)}, f32[128]{0:T(128)S(1)}, u32[]{:S(2)}, u32[]{:S(2)}) %collective-permute-start.8) | collective-permute-done | bytes 544 | tf_op jit(solution)/shard_map/ppermute | solution.py:66
  55.5 0.0 copy-done.6
  55.5 1.0 %multiply_convert_fusion = bf16[128,2048]{1,0:T(8,128)(2,1)} fusion(f32[128,2048]{1,0:T(8,128)S(1)} %get-tuple-element.28, f32[2048]{0:T(1024)S(1)} %copy-done.6, f32[128]{0:T(128)S(1)} %add_rsqrt_fusion), kind=kLoop, calls=%fused_computation.11 | loop fusion | flops 786432 | bytes 1581568 | tf_op jit(solution)/shard_map/convert_element_type | solution.py:169
  (29 shorter events, 0.6 us)
Async XLA Ops:
  0.0 3.1 %copy-start.1 = (bf16[128,2048]{1,0:T(8,128)(2,1)S(1)}, bf16[128,2048]{1,0:T(8,128)(2,1)}, u32[]{:S(2)}) copy-start(bf16[128,2048]{1,0:T(8,128)(2,1)} %v_ref.1) | copy-start | bytes 1572868
  0.0 3.1 %copy-start.2 = (bf16[128,2048]{1,0:T(8,128)(2,1)S(1)}, bf16[128,2048]{1,0:T(8,128)(2,1)}, u32[]{:S(2)}) copy-start(bf16[128,2048]{1,0:T(8,128)(2,1)} %q_ref.1) | copy-start | bytes 1572868
  0.0 3.1 %copy-start.3 = (bf16[128,2048]{1,0:T(8,128)(2,1)S(1)}, bf16[128,2048]{1,0:T(8,128)(2,1)}, u32[]{:S(2)}) copy-start(bf16[128,2048]{1,0:T(8,128)(2,1)} %k_ref.1) | copy-start | bytes 1572868
  0.0 3.2 %copy-start = (f32[3,3,2048]{2,1,0:T(4,128)S(1)}, f32[3,3,2048]{2,1,0:T(4,128)}, u32[]{:S(2)}) copy-start(f32[3,3,2048]{2,1,0:T(4,128)} %taps_ref.1) | copy-start | bytes 221188
  3.2 19.7 %copy-start.4 = (f32[2048,16]{0,1:T(8,128)S(1)}, f32[2048,16]{0,1:T(8,128)}, u32[]{:S(2)}) copy-start(f32[2048,16]{0,1:T(8,128)} %param.12) | copy-start | bytes 393220
  3.2 19.7 %copy-start.5 = (f32[2048,16]{0,1:T(8,128)S(1)}, f32[2048,16]{0,1:T(8,128)}, u32[]{:S(2)}) copy-start(f32[2048,16]{0,1:T(8,128)} %param.13) | copy-start | bytes 393220
  9.1 22.7 %collective-permute-start = (f32[28,2048]{1,0:T(8,128)S(1)}, f32[28,2048]{1,0:T(8,128)S(1)}, u32[]{:S(2)}, u32[]{:S(2)}) collective-permute-start(f32[28,2048]{1,0:T(8,128)S(1)} %pad_maximum_fusion), channel_id=1, source_target_pairs={{0,4},{4,8},{8,12},{12,16},{16,20},{20,24},{24,28},{1,5},{5,9},{9,... | collective-permute-start | bytes 688136 | tf_op jit(solution)/shard_map/ppermute | solution.py:14
  11.6 21.6 %collective-permute-start.1 = (f32[28,2048]{1,0:T(8,128)S(1)}, f32[28,2048]{1,0:T(8,128)S(1)}, u32[]{:S(2)}, u32[]{:S(2)}) collective-permute-start(f32[28,2048]{1,0:T(8,128)S(1)} %pad_maximum_fusion), channel_id=1, source_target_pairs={{0,8},{4,12},{8,16},{12,20},{16,24},{20,28},{1,9},{5,13},{9,17},{1... | collective-permute-start | bytes 688136 | tf_op jit(solution)/shard_map/ppermute | solution.py:14
  16.0 18.9 %collective-permute-start.2 = (f32[28,2048]{1,0:T(8,128)S(1)}, f32[28,2048]{1,0:T(8,128)S(1)}, u32[]{:S(2)}, u32[]{:S(2)}) collective-permute-start(f32[28,2048]{1,0:T(8,128)S(1)} %pad_maximum_fusion), channel_id=1, source_target_pairs={{0,12},{4,16},{8,20},{12,24},{16,28},{1,13},{5,17},{9,21},{13,25},... | collective-permute-start | bytes 688136 | tf_op jit(solution)/shard_map/ppermute | solution.py:14
  20.3 14.6 %collective-permute-start.3 = (f32[28,2048]{1,0:T(8,128)S(1)}, f32[28,2048]{1,0:T(8,128)S(1)}, u32[]{:S(2)}, u32[]{:S(2)}) collective-permute-start(f32[28,2048]{1,0:T(8,128)S(1)} %pad_maximum_fusion), channel_id=1, source_target_pairs={{0,16},{4,20},{8,24},{12,28},{1,17},{5,21},{9,25},{13,29},{2,18},{... | collective-permute-start | bytes 688136 | tf_op jit(solution)/shard_map/ppermute | solution.py:14
  21.6 16.3 %collective-permute-start.4 = (f32[28,2048]{1,0:T(8,128)S(1)}, f32[28,2048]{1,0:T(8,128)S(1)}, u32[]{:S(2)}, u32[]{:S(2)}) collective-permute-start(f32[28,2048]{1,0:T(8,128)S(1)} %pad_maximum_fusion), channel_id=1, source_target_pairs={{0,20},{4,24},{8,28},{1,21},{5,25},{9,29},{2,22},{6,26},{10,30},{3... | collective-permute-start | bytes 688136 | tf_op jit(solution)/shard_map/ppermute | solution.py:14
  31.8 6.6 %collective-permute-start.5 = (f32[28,2048]{1,0:T(8,128)S(1)}, f32[28,2048]{1,0:T(8,128)S(1)}, u32[]{:S(2)}, u32[]{:S(2)}) collective-permute-start(f32[28,2048]{1,0:T(8,128)S(1)} %pad_maximum_fusion), channel_id=1, source_target_pairs={{0,24},{4,28},{1,25},{5,29},{2,26},{6,30},{3,27},{7,31}} | collective-permute-start | bytes 688136 | tf_op jit(solution)/shard_map/ppermute | solution.py:14
  33.1 8.0 %collective-permute-start.6 = (f32[28,2048]{1,0:T(8,128)S(1)}, f32[28,2048]{1,0:T(8,128)S(1)}, u32[]{:S(2)}, u32[]{:S(2)}) collective-permute-start(f32[28,2048]{1,0:T(8,128)S(1)} %pad_maximum_fusion), channel_id=1, source_target_pairs={{0,28},{1,29},{2,30},{3,31}} | collective-permute-start | bytes 688136 | tf_op jit(solution)/shard_map/ppermute | solution.py:14
  34.9 8.3 %copy-start.7 = (bf16[128,2048]{1,0:T(8,128)(2,1)S(1)}, bf16[128,2048]{1,0:T(8,128)(2,1)}, u32[]{:S(2)}) copy-start(bf16[128,2048]{1,0:T(8,128)(2,1)} %param.14) | copy-start | bytes 1572868
  43.1 12.3 %copy-start.6 = (f32[2048]{0:T(1024)S(1)}, f32[2048]{0:T(1024)}, u32[]{:S(2)}) copy-start(f32[2048]{0:T(1024)} %param.15) | copy-start | bytes 24580
  47.4 3.6 %collective-permute-start.7 = (f32[128]{0:T(128)S(1)}, f32[128]{0:T(128)S(1)}, u32[]{:S(2)}, u32[]{:S(2)}) collective-permute-start(f32[128]{0:T(128)S(1)} %get-tuple-element.27), channel_id=1, source_target_pairs={{0,1},{1,0},{2,3},{3,2},{4,5},{5,4},{6,7},{7,6},{8,9},{9,8},{10,11... | collective-permute-start | bytes 1544 | tf_op jit(solution)/shard_map/ppermute | solution.py:66
  51.0 4.5 %collective-permute-start.8 = (f32[128]{0:T(128)S(1)}, f32[128]{0:T(128)S(1)}, u32[]{:S(2)}, u32[]{:S(2)}) collective-permute-start(f32[128]{0:T(128)S(1)} %add.552), channel_id=1, source_target_pairs={{0,2},{1,3},{2,0},{3,1},{4,6},{5,7},{6,4},{7,5},{8,10},{9,11},{10,... | collective-permute-start | bytes 1544 | tf_op jit(solution)/shard_map/ppermute | solution.py:66

commit v11 on v8

--- a/solution.py
+++ b/solution.py
@@ -122,8 +122,16 @@
     times = jnp.arange(rows, dtype=jnp.int32).astype(jnp.float32) + 1.0
     weights = weight * incoming
     mixed_in = outputs
-    for m in range(decay.shape[0]):
-        mixed_in = mixed_in + jnp.exp(-decay[m][None, :] * times[:, None]) * weights[m][None, :]
+    if rows % 8 == 0:
+        coarse_t = jnp.arange(0, rows, 8, dtype=jnp.int32).astype(jnp.float32)
+        fine_t = jnp.arange(8, dtype=jnp.int32).astype(jnp.float32) + 1.0
+        far = jnp.exp(-decay[:, None, :] * coarse_t[None, :, None]) * weights[:, None, :]
+        near = jnp.exp(-decay[:, None, :] * fine_t[None, :, None])
+        for m in range(decay.shape[0]):
+            mixed_in = mixed_in + (far[m][:, None, :] * near[m][None, :, :]).reshape(rows, width)
+    else:
+        for m in range(decay.shape[0]):
+            mixed_in = mixed_in + jnp.exp(-decay[m][None, :] * times[:, None]) * weights[m][None, :]
     mixed = mixed_in
     stream = resid.astype(jnp.float32) + q_feat * mixed
     squares = butterfly_sum(jnp.sum(stream * stream, axis=1), "tp")

time: 51.1 us -> 49.1 us (0.961)
  starting transfers between devices: 22.8 us -> 20.9 us
  other arithmetic: 17.8 us -> 15.9 us
  local copies, waits for them, and re-layouts: 0.14 us -> 2 us
    reduce_sum x1, other arithmetic: 4.02 us -> 1.58 us  [per_device(): squares = butterfly_sum(jnp.sum(stream * stream, axis=1), 'tp')]
    ppermute x8, starting transfers between devices: 18.5 us -> 16.6 us  [from_behind(): return lax.ppermute(block, axis, route)]
    unnamed x16, local copies, waits for them, and re-layouts: 0.05 us -> 1.78 us
  transfers between devices with their start and end apart: 10 -> 10, of which waited for: 2 -> 2; matrix products, arithmetic and copies ran while one was open for 23% -> 25% of each run, Pallas kernels for 0% -> 0%
where the time goes in v11:
time: 49.1 us; the launch traced here: 48.6 us
  starting transfers between devices  20.9 us (43%)
  other arithmetic  15.9 us (32%)
  Pallas kernels  5.77 us (12%)
  waiting for transfers between devices  3.89 us (8%)
  local copies, waits for them, and re-layouts  2 us (4%)
    ppermute x8, starting transfers between devices, from_behind(): return lax.ppermute(block, axis, route)  16.6 us
    another operation x1, other arithmetic, local(): running = jnp.cumsum(values[None, :, :] * grow, axis=1) * fade  9.02 us
    pallas_call x1, Pallas kernels, front(): pl.pallas_call(front_kernel, out_shape=(jax.ShapeDtypeStruct((rows, width...  5.77 us
    ppermute x2, starting transfers between devices, butterfly_sum(): lax.ppermute(value, axis, [(i, i ^ step) for i in range(count)])  4.23 us
    ppermute x2, waiting for transfers between devices, butterfly_sum(): lax.ppermute(value, axis, [(i, i ^ step) for i in range(count)])  3.87 us
    unnamed x16, local copies, waits for them, and re-layouts  1.78 us
    exp x1, other arithmetic, front(): jnp.exp(-decay[:, None, :] * (8.0 * (chunks - 1 - jnp.arange(chunks, dtyp...  1.68 us
    reduce_sum x1, other arithmetic, per_device(): squares = butterfly_sum(jnp.sum(stream * stream, axis=1), 'tp')  1.58 us
  transfers between devices with their start and end apart: 10, of which 2 were waited for; matrix products, arithmetic and copies ran while one was open for 25% of the time, Pallas kernels for 0%

profile of v11, /device:TPU:0, one launch (start us, length us, event | category | flops | bytes accessed | tf_op | source)
XLA Modules:
  0.0 48.6 jit_solution(12486964210313866666)
XLA Ops:
  0.0 0.8 %pad_maximum_fusion = bf16[3,2,2048]{2,1,0:T(2,128)(2,1)S(1)} fusion(bf16[1,128,2048]{2,1,0:T(8,128)(2,1)} %bitcast.157, bf16[1,128,2048]{2,1,0:T(8,128)(2,1)} %bitcast.156, bf16[1,128,2048]{2,1,0:T(8,128)(2,1)} %bitcast.155), kind=kLoop, calls=%fused_computation.65 | loop fusion | flops 73728 | bytes 1597440 | tf_op jit(solution)/shard_map/stack | solution.py:96
  0.8 2.4 %collective-permute-start = (bf16[3,2,2048]{2,1,0:T(2,128)(2,1)S(1)}, bf16[3,2,2048]{2,1,0:T(2,128)(2,1)S(1)}, u32[]{:S(2)}, u32[]{:S(2)}) collective-permute-start(bf16[3,2,2048]{2,1,0:T(2,128)(2,1)S(1)} %pad_maximum_fusion), channel_id=1, source_target_pairs={{0,4},{4,8},{8,12},{12,16},{16,20},{20,24},{24,28},{1,5},{5,9},{9,... | collective-permute-start | bytes 73736 | tf_op jit(solution)/shard_map/ppermute | solution.py:14
  3.3 0.9 %bitcast_negate_fusion = f32[16,2048]{1,0:T(8,128)S(1)} fusion(f32[2048,16]{0,1:T(8,128)} %param.12), kind=kLoop, calls=%fused_computation.73 | loop fusion | flops 32768 | bytes 262144 | tf_op jit(solution)/shard_map/neg | solution.py:73
  4.2 1.7 %multiply_exponential_fusion.coarse_ref = f32[16,16,2048]{2,1,0:T(8,128)} fusion(f32[16]{0:T(128)S(1)} %subtract_multiply_fusion, f32[16,2048]{1,0:T(8,128)S(1)} %bitcast_negate_fusion), kind=kLoop, calls=%fused_computation.9 | loop fusion | flops 524288 | bytes 2228288 | tf_op jit(solution)/shard_map/exp | solution.py:73
  5.9 0.0 copy-start
  5.9 0.0 copy-start.1
  5.9 0.0 copy-start.2
  5.9 0.0 copy-start.3
  5.9 0.4 multiply_exponential_fusion.1
  6.2 0.1 slice_bitcast_fusion.31
  6.3 0.0 collective-permute-done.halo_ref
  6.3 0.6 %copy-done = bf16[128,2048]{1,0:T(8,128)(2,1)S(1)} copy-done((bf16[128,2048]{1,0:T(8,128)(2,1)S(1)}, bf16[128,2048]{1,0:T(8,128)(2,1)}, u32[]{:S(2)}) %copy-start) | copy-done | bytes 524312
  6.9 0.2 copy-done.1
  7.1 0.2 copy-done.2
  7.2 0.0 copy-done.3
  7.2 0.0 copy-start.4
  7.2 0.0 copy-start.6
  7.2 5.8 %shard_map.82 = (f32[128,2048]{1,0:T(8,128)S(1)}, f32[128,2048]{1,0:T(8,128)S(1)}, f32[16,2048]{1,0:T(8,128)S(1)}) custom-call(bf16[128,2048]{1,0:T(8,128)(2,1)S(1)} %copy-done, bf16[128,2048]{1,0:T(8,128)(2,1)S(1)} %copy-done.1, bf16[128,2048]{1,0:T(8,128)(2,1)S(1)} %copy-done.2, bf16[3,2,2048]{2,1,0:T(2,128)(2,1)S(1)} %collective-permute-done.halo_ref, ...), custom_call_target="tpu_custom_call" | custom-call | flops 21495808 | bytes 3670016 | tf_op jit(solution)/shard_map/pallas_call | solution.py:76
  13.0 4.2 %collective-permute-start.7 = (f32[16,2048]{1,0:T(8,128)S(1)}, f32[16,2048]{1,0:T(8,128)S(1)}, u32[]{:S(2)}, u32[]{:S(2)}) collective-permute-start(f32[16,2048]{1,0:T(8,128)S(1)} %get-tuple-element.17), channel_id=1, source_target_pairs={{0,28},{1,29},{2,30},{3,31}} | collective-permute-start | bytes 393224 | tf_op jit(solution)/shard_map/ppermute | solution.py:14
  17.2 1.9 %collective-permute-start.6 = (f32[16,2048]{1,0:T(8,128)S(1)}, f32[16,2048]{1,0:T(8,128)S(1)}, u32[]{:S(2)}, u32[]{:S(2)}) collective-permute-start(f32[16,2048]{1,0:T(8,128)S(1)} %get-tuple-element.17), channel_id=1, source_target_pairs={{0,24},{4,28},{1,25},{5,29},{2,26},{6,30},{3,27},{7,31}} | collective-permute-start | bytes 393224 | tf_op jit(solution)/shard_map/ppermute | solution.py:14
  19.1 1.3 %collective-permute-start.5 = (f32[16,2048]{1,0:T(8,128)S(1)}, f32[16,2048]{1,0:T(8,128)S(1)}, u32[]{:S(2)}, u32[]{:S(2)}) collective-permute-start(f32[16,2048]{1,0:T(8,128)S(1)} %get-tuple-element.17), channel_id=1, source_target_pairs={{0,20},{4,24},{8,28},{1,21},{5,25},{9,29},{2,22},{6,26},{10,30},{3... | collective-permute-start | bytes 393224 | tf_op jit(solution)/shard_map/ppermute | solution.py:14
  20.4 1.3 %collective-permute-start.4 = (f32[16,2048]{1,0:T(8,128)S(1)}, f32[16,2048]{1,0:T(8,128)S(1)}, u32[]{:S(2)}, u32[]{:S(2)}) collective-permute-start(f32[16,2048]{1,0:T(8,128)S(1)} %get-tuple-element.17), channel_id=1, source_target_pairs={{0,16},{4,20},{8,24},{12,28},{1,17},{5,21},{9,25},{13,29},{2,18},{... | collective-permute-start | bytes 393224 | tf_op jit(solution)/shard_map/ppermute | solution.py:14
  21.7 1.6 %collective-permute-start.3 = (f32[16,2048]{1,0:T(8,128)S(1)}, f32[16,2048]{1,0:T(8,128)S(1)}, u32[]{:S(2)}, u32[]{:S(2)}) collective-permute-start(f32[16,2048]{1,0:T(8,128)S(1)} %get-tuple-element.17), channel_id=1, source_target_pairs={{0,12},{4,16},{8,20},{12,24},{16,28},{1,13},{5,17},{9,21},{13,25},... | collective-permute-start | bytes 393224 | tf_op jit(solution)/shard_map/ppermute | solution.py:14
  23.3 0.0 collective-permute-done.7
  23.3 2.7 %collective-permute-start.2 = (f32[16,2048]{1,0:T(8,128)S(1)}, f32[16,2048]{1,0:T(8,128)S(1)}, u32[]{:S(2)}, u32[]{:S(2)}) collective-permute-start(f32[16,2048]{1,0:T(8,128)S(1)} %get-tuple-element.17), channel_id=1, source_target_pairs={{0,8},{4,12},{8,16},{12,20},{16,24},{20,28},{1,9},{5,13},{9,17},{1... | collective-permute-start | bytes 393224 | tf_op jit(solution)/shard_map/ppermute | solution.py:14
  26.0 0.0 collective-permute-done.6
  26.0 1.3 %collective-permute-start.1 = (f32[16,2048]{1,0:T(8,128)S(1)}, f32[16,2048]{1,0:T(8,128)S(1)}, u32[]{:S(2)}, u32[]{:S(2)}) collective-permute-start(f32[16,2048]{1,0:T(8,128)S(1)} %get-tuple-element.17), channel_id=1, source_target_pairs={{0,4},{4,8},{8,12},{12,16},{16,20},{20,24},{24,28},{1,5},{5,9},{9,... | collective-permute-start | bytes 393224 | tf_op jit(solution)/shard_map/ppermute | solution.py:14
  27.3 0.0 copy-done.4
  27.3 0.0 copy-done.6
  27.3 9.0 %multiply_reduce_fusion = f32[128,2048]{1,0:T(8,128)S(1)} fusion(f32[16,2048]{1,0:T(8,128)S(1)} %bitcast.159, f32[16,2048]{1,0:T(8,128)S(1)} %bitcast_negate_fusion, f32[128]{0:T(128)S(1)} %iota_convert_fusion, f32[16,2048]{1,0:T(8,128)S(1)} %bitcast.158, f32[128,2048]{1,0:T(8,128)S(1)} %get-tuple-element.18), kind=kOutput, calls=%fused_computation | output fusion | flops 557580288 | bytes 2490880 | tf_op jit(solution)/shard_map/jit(cumsum)/reduce_window_sum | solution.py:117
  36.4 0.0 collective-permute-done.5
  36.4 0.0 collective-permute-done.4
  36.4 0.0 collective-permute-done.3
  36.4 0.0 collective-permute-done.2
  36.4 0.0 collective-permute-done.1
  36.4 0.2 add_multiply_fusion
  36.6 0.3 exponential_multiply_fusion
  36.9 0.0 copy-start.5
  36.9 0.1 slice_bitcast_fusion.15
  37.1 0.9 %copy-done.5 = bf16[128,2048]{1,0:T(8,128)(2,1)S(1)} copy-done((bf16[128,2048]{1,0:T(8,128)(2,1)S(1)}, bf16[128,2048]{1,0:T(8,128)(2,1)}, u32[]{:S(2)}) %copy-start.5) | copy-done | bytes 524312
  38.0 0.0 copy-start.7
  38.0 1.6 %multiply_reduce_fusion.1 = (f32[128]{0:T(128)S(1)}, f32[128,2048]{1,0:T(8,128)S(1)}) fusion(f32[128,2048]{1,0:T(8,128)S(1)} %get-tuple-element.16, f32[8,2048]{1,0:T(8,128)S(1)} %get-tuple-element.46, f32[16,2048]{1,0:T(8,128)S(1)} %get-tuple-element.30, f32[8,2048]{1,0:T(8,128)S(1)} %get-tuple-element.47, f32[16,2048]{1,0:T(8,128)S(1)} %get-tuple-element.31, ...), kind=kLoop, calls=%fused_computation.29 | loop fusion | flops 9699200 | bytes 6816256 | tf_op jit(solution)/shard_map/reduce_sum | solution.py:137
  39.6 1.6 %collective-permute-start.8 = (f32[128]{0:T(128)S(1)}, f32[128]{0:T(128)S(1)}, u32[]{:S(2)}, u32[]{:S(2)}) collective-permute-start(f32[128]{0:T(128)S(1)} %get-tuple-element.27), channel_id=1, source_target_pairs={{0,1},{1,0},{2,3},{3,2},{4,5},{5,4},{6,7},{7,6},{8,9},{9,8},{10,11... | collective-permute-start | bytes 1544 | tf_op jit(solution)/shard_map/ppermute | solution.py:37
  41.2 2.0 %collective-permute-done.8 = f32[128]{0:T(128)S(1)} collective-permute-done((f32[128]{0:T(128)S(1)}, f32[128]{0:T(128)S(1)}, u32[]{:S(2)}, u32[]{:S(2)}) %collective-permute-start.8) | collective-permute-done | bytes 544 | tf_op jit(solution)/shard_map/ppermute | solution.py:37
  43.2 2.6 %collective-permute-start.9 = (f32[128]{0:T(128)S(1)}, f32[128]{0:T(128)S(1)}, u32[]{:S(2)}, u32[]{:S(2)}) collective-permute-start(f32[128]{0:T(128)S(1)} %add.112), channel_id=1, source_target_pairs={{0,2},{1,3},{2,0},{3,1},{4,6},{5,7},{6,4},{7,5},{8,10},{9,11},{10,... | collective-permute-start | bytes 1544 | tf_op jit(solution)/shard_map/ppermute | solution.py:37
  45.8 1.9 %collective-permute-done.9 = f32[128]{0:T(128)S(1)} collective-permute-done((f32[128]{0:T(128)S(1)}, f32[128]{0:T(128)S(1)}, u32[]{:S(2)}, u32[]{:S(2)}) %collective-permute-start.9) | collective-permute-done | bytes 544 | tf_op jit(solution)/shard_map/ppermute | solution.py:37
  47.7 0.0 copy-done.7
  47.7 1.0 %multiply_convert_fusion = bf16[128,2048]{1,0:T(8,128)(2,1)} fusion(f32[128,2048]{1,0:T(8,128)S(1)} %get-tuple-element.28, f32[2048]{0:T(1024)S(1)} %copy-done.7, f32[128]{0:T(128)S(1)} %add_rsqrt_fusion), kind=kLoop, calls=%fused_computation.28 | loop fusion | flops 786432 | bytes 1581568 | tf_op jit(solution)/shard_map/convert_element_type | solution.py:139
  (6 shorter events, 0.0 us)
Async XLA Ops:
  0.8 5.5 %collective-permute-start = (bf16[3,2,2048]{2,1,0:T(2,128)(2,1)S(1)}, bf16[3,2,2048]{2,1,0:T(2,128)(2,1)S(1)}, u32[]{:S(2)}, u32[]{:S(2)}) collective-permute-start(bf16[3,2,2048]{2,1,0:T(2,128)(2,1)S(1)} %pad_maximum_fusion), channel_id=1, source_target_pairs={{0,4},{4,8},{8,12},{12,16},{16,20},{20,24},{24,28},{1,5},{5,9},{9,... | collective-permute-start | bytes 73736 | tf_op jit(solution)/shard_map/ppermute | solution.py:14
  5.9 1.0 %copy-start = (bf16[128,2048]{1,0:T(8,128)(2,1)S(1)}, bf16[128,2048]{1,0:T(8,128)(2,1)}, u32[]{:S(2)}) copy-start(bf16[128,2048]{1,0:T(8,128)(2,1)} %q_ref.1) | copy-start | bytes 1572868
  5.9 1.2 %copy-start.1 = (bf16[128,2048]{1,0:T(8,128)(2,1)S(1)}, bf16[128,2048]{1,0:T(8,128)(2,1)}, u32[]{:S(2)}) copy-start(bf16[128,2048]{1,0:T(8,128)(2,1)} %k_ref.1) | copy-start | bytes 1572868
  5.9 1.4 %copy-start.2 = (bf16[128,2048]{1,0:T(8,128)(2,1)S(1)}, bf16[128,2048]{1,0:T(8,128)(2,1)}, u32[]{:S(2)}) copy-start(bf16[128,2048]{1,0:T(8,128)(2,1)} %v_ref.1) | copy-start | bytes 1572868
  5.9 1.4 %copy-start.3 = (f32[3,3,2048]{2,1,0:T(4,128)S(1)}, f32[3,3,2048]{2,1,0:T(4,128)}, u32[]{:S(2)}) copy-start(f32[3,3,2048]{2,1,0:T(4,128)} %taps_ref.1) | copy-start | bytes 221188
  7.2 20.1 %copy-start.4 = (f32[2048,16]{0,1:T(8,128)S(1)}, f32[2048,16]{0,1:T(8,128)}, u32[]{:S(2)}) copy-start(f32[2048,16]{0,1:T(8,128)} %param.12) | copy-start | bytes 393220
  7.2 20.1 %copy-start.6 = (f32[2048,16]{0,1:T(8,128)S(1)}, f32[2048,16]{0,1:T(8,128)}, u32[]{:S(2)}) copy-start(f32[2048,16]{0,1:T(8,128)} %param.13) | copy-start | bytes 393220
  13.0 10.3 %collective-permute-start.7 = (f32[16,2048]{1,0:T(8,128)S(1)}, f32[16,2048]{1,0:T(8,128)S(1)}, u32[]{:S(2)}, u32[]{:S(2)}) collective-permute-start(f32[16,2048]{1,0:T(8,128)S(1)} %get-tuple-element.17), channel_id=1, source_target_pairs={{0,28},{1,29},{2,30},{3,31}} | collective-permute-start | bytes 393224 | tf_op jit(solution)/shard_map/ppermute | solution.py:14
  17.2 8.8 %collective-permute-start.6 = (f32[16,2048]{1,0:T(8,128)S(1)}, f32[16,2048]{1,0:T(8,128)S(1)}, u32[]{:S(2)}, u32[]{:S(2)}) collective-permute-start(f32[16,2048]{1,0:T(8,128)S(1)} %get-tuple-element.17), channel_id=1, source_target_pairs={{0,24},{4,28},{1,25},{5,29},{2,26},{6,30},{3,27},{7,31}} | collective-permute-start | bytes 393224 | tf_op jit(solution)/shard_map/ppermute | solution.py:14
  19.1 17.3 %collective-permute-start.5 = (f32[16,2048]{1,0:T(8,128)S(1)}, f32[16,2048]{1,0:T(8,128)S(1)}, u32[]{:S(2)}, u32[]{:S(2)}) collective-permute-start(f32[16,2048]{1,0:T(8,128)S(1)} %get-tuple-element.17), channel_id=1, source_target_pairs={{0,20},{4,24},{8,28},{1,21},{5,25},{9,29},{2,22},{6,26},{10,30},{3... | collective-permute-start | bytes 393224 | tf_op jit(solution)/shard_map/ppermute | solution.py:14
  20.4 16.0 %collective-permute-start.4 = (f32[16,2048]{1,0:T(8,128)S(1)}, f32[16,2048]{1,0:T(8,128)S(1)}, u32[]{:S(2)}, u32[]{:S(2)}) collective-permute-start(f32[16,2048]{1,0:T(8,128)S(1)} %get-tuple-element.17), channel_id=1, source_target_pairs={{0,16},{4,20},{8,24},{12,28},{1,17},{5,21},{9,25},{13,29},{2,18},{... | collective-permute-start | bytes 393224 | tf_op jit(solution)/shard_map/ppermute | solution.py:14
  21.7 14.7 %collective-permute-start.3 = (f32[16,2048]{1,0:T(8,128)S(1)}, f32[16,2048]{1,0:T(8,128)S(1)}, u32[]{:S(2)}, u32[]{:S(2)}) collective-permute-start(f32[16,2048]{1,0:T(8,128)S(1)} %get-tuple-element.17), channel_id=1, source_target_pairs={{0,12},{4,16},{8,20},{12,24},{16,28},{1,13},{5,17},{9,21},{13,25},... | collective-permute-start | bytes 393224 | tf_op jit(solution)/shard_map/ppermute | solution.py:14
  23.3 13.1 %collective-permute-start.2 = (f32[16,2048]{1,0:T(8,128)S(1)}, f32[16,2048]{1,0:T(8,128)S(1)}, u32[]{:S(2)}, u32[]{:S(2)}) collective-permute-start(f32[16,2048]{1,0:T(8,128)S(1)} %get-tuple-element.17), channel_id=1, source_target_pairs={{0,8},{4,12},{8,16},{12,20},{16,24},{20,28},{1,9},{5,13},{9,17},{1... | collective-permute-start | bytes 393224 | tf_op jit(solution)/shard_map/ppermute | solution.py:14
  26.0 10.4 %collective-permute-start.1 = (f32[16,2048]{1,0:T(8,128)S(1)}, f32[16,2048]{1,0:T(8,128)S(1)}, u32[]{:S(2)}, u32[]{:S(2)}) collective-permute-start(f32[16,2048]{1,0:T(8,128)S(1)} %get-tuple-element.17), channel_id=1, source_target_pairs={{0,4},{4,8},{8,12},{12,16},{16,20},{20,24},{24,28},{1,5},{5,9},{9,... | collective-permute-start | bytes 393224 | tf_op jit(solution)/shard_map/ppermute | solution.py:14
  36.9 1.0 %copy-start.5 = (bf16[128,2048]{1,0:T(8,128)(2,1)S(1)}, bf16[128,2048]{1,0:T(8,128)(2,1)}, u32[]{:S(2)}) copy-start(bf16[128,2048]{1,0:T(8,128)(2,1)} %param.14) | copy-start | bytes 1572868
  38.0 9.7 %copy-start.7 = (f32[2048]{0:T(1024)S(1)}, f32[2048]{0:T(1024)}, u32[]{:S(2)}) copy-start(f32[2048]{0:T(1024)} %param.15) | copy-start | bytes 24580
  39.6 3.6 %collective-permute-start.8 = (f32[128]{0:T(128)S(1)}, f32[128]{0:T(128)S(1)}, u32[]{:S(2)}, u32[]{:S(2)}) collective-permute-start(f32[128]{0:T(128)S(1)} %get-tuple-element.27), channel_id=1, source_target_pairs={{0,1},{1,0},{2,3},{3,2},{4,5},{5,4},{6,7},{7,6},{8,9},{9,8},{10,11... | collective-permute-start | bytes 1544 | tf_op jit(solution)/shard_map/ppermute | solution.py:37
  43.2 4.5 %collective-permute-start.9 = (f32[128]{0:T(128)S(1)}, f32[128]{0:T(128)S(1)}, u32[]{:S(2)}, u32[]{:S(2)}) collective-permute-start(f32[128]{0:T(128)S(1)} %add.112), channel_id=1, source_target_pairs={{0,2},{1,3},{2,0},{3,1},{4,6},{5,7},{6,4},{7,5},{8,10},{9,11},{10,... | collective-permute-start | bytes 1544 | tf_op jit(solution)/shard_map/ppermute | solution.py:37

commit v12 on v11

--- a/solution.py
+++ b/solution.py
@@ -113,12 +113,15 @@
         return (states[:, -1, :], jnp.sum(states * weight[:, None, :], axis=0))
 
     def local():
+        return local_part(), resid.astype(jnp.float32)
+
+    def local_part():
         if rows == block:
             running = jnp.cumsum(values[None, :, :] * grow, axis=1) * fade
             return jnp.sum(running * weight[:, None, :], axis=0)
         return lax.scan(main_step, zeros, blocks)[1].reshape(rows, width)
 
-    incoming, outputs = scan_in(ending, decay, rows, "ctx", local)
+    incoming, (outputs, resid_f32) = scan_in(ending, decay, rows, "ctx", local)
     times = jnp.arange(rows, dtype=jnp.int32).astype(jnp.float32) + 1.0
     weights = weight * incoming
     mixed_in = outputs
@@ -133,7 +136,7 @@
         for m in range(decay.shape[0]):
             mixed_in = mixed_in + jnp.exp(-decay[m][None, :] * times[:, None]) * weights[m][None, :]
     mixed = mixed_in
-    stream = resid.astype(jnp.float32) + q_feat * mixed
+    stream = resid_f32 + q_feat * mixed
     squares = butterfly_sum(jnp.sum(stream * stream, axis=1), "tp")
     scale = lax.rsqrt(squares / D + 1e-05)
     return (stream * scale[:, None] * gain[None, :]).astype(jnp.bfloat16)

time: 49.1 us -> 48.4 us (0.986)
  local copies, waits for them, and re-layouts: 2 us -> 1.2 us
    unnamed x16, local copies, waits for them, and re-layouts: 1.78 us -> 0.9 us
where the time goes in v12:
time: 48.4 us; the launch traced here: 48 us
  starting transfers between devices  20.9 us (43%)
  other arithmetic  16 us (33%)
  Pallas kernels  5.8 us (12%)
  waiting for transfers between devices  3.89 us (8%)
  local copies, waits for them, and re-layouts  1.2 us (2%)
    ppermute x8, starting transfers between devices, from_behind(): return lax.ppermute(block, axis, route)  16.6 us
    another operation x1, other arithmetic, local_part(): running = jnp.cumsum(values[None, :, :] * grow, axis=1) * fade  9.02 us
    pallas_call x1, Pallas kernels, front(): pl.pallas_call(front_kernel, out_shape=(jax.ShapeDtypeStruct((rows, width...  5.8 us
    ppermute x2, starting transfers between devices, butterfly_sum(): lax.ppermute(value, axis, [(i, i ^ step) for i in range(count)])  4.23 us
    ppermute x2, waiting for transfers between devices, butterfly_sum(): lax.ppermute(value, axis, [(i, i ^ step) for i in range(count)])  3.87 us
    exp x1, other arithmetic, front(): jnp.exp(-decay[:, None, :] * (8.0 * (chunks - 1 - jnp.arange(chunks, dtyp...  1.68 us
    reduce_sum x1, other arithmetic, per_device(): squares = butterfly_sum(jnp.sum(stream * stream, axis=1), 'tp')  1.63 us
  transfers between devices with their start and end apart: 10, of which 2 were waited for; matrix products, arithmetic and copies ran while one was open for 25% of the time, Pallas kernels for 0%

profile of v12, /device:TPU:0, one launch (start us, length us, event | category | flops | bytes accessed | tf_op | source)
XLA Modules:
  0.0 48.0 jit_solution(18338398753184838470)
XLA Ops:
  0.0 0.8 %pad_maximum_fusion = bf16[3,2,2048]{2,1,0:T(2,128)(2,1)S(1)} fusion(bf16[1,128,2048]{2,1,0:T(8,128)(2,1)} %bitcast.157, bf16[1,128,2048]{2,1,0:T(8,128)(2,1)} %bitcast.156, bf16[1,128,2048]{2,1,0:T(8,128)(2,1)} %bitcast.155), kind=kLoop, calls=%fused_computation.65 | loop fusion | flops 73728 | bytes 1597440 | tf_op jit(solution)/shard_map/stack | solution.py:96
  0.8 2.4 %collective-permute-start = (bf16[3,2,2048]{2,1,0:T(2,128)(2,1)S(1)}, bf16[3,2,2048]{2,1,0:T(2,128)(2,1)S(1)}, u32[]{:S(2)}, u32[]{:S(2)}) collective-permute-start(bf16[3,2,2048]{2,1,0:T(2,128)(2,1)S(1)} %pad_maximum_fusion), channel_id=1, source_target_pairs={{0,4},{4,8},{8,12},{12,16},{16,20},{20,24},{24,28},{1,5},{5,9},{9,... | collective-permute-start | bytes 73736 | tf_op jit(solution)/shard_map/ppermute | solution.py:14
  3.3 0.9 %bitcast_negate_fusion = f32[16,2048]{1,0:T(8,128)S(1)} fusion(f32[2048,16]{0,1:T(8,128)} %param.12), kind=kLoop, calls=%fused_computation.73 | loop fusion | flops 32768 | bytes 262144 | tf_op jit(solution)/shard_map/neg | solution.py:73
  4.2 1.7 %multiply_exponential_fusion.coarse_ref = f32[16,16,2048]{2,1,0:T(8,128)} fusion(f32[16]{0:T(128)S(1)} %subtract_multiply_fusion, f32[16,2048]{1,0:T(8,128)S(1)} %bitcast_negate_fusion), kind=kLoop, calls=%fused_computation.9 | loop fusion | flops 524288 | bytes 2228288 | tf_op jit(solution)/shard_map/exp | solution.py:73
  5.9 0.0 copy-start
  5.9 0.0 copy-start.1
  5.9 0.0 copy-start.2
  5.9 0.0 copy-start.3
  5.9 0.4 multiply_exponential_fusion.1
  6.2 0.1 slice_bitcast_fusion.31
  6.3 0.0 collective-permute-done.halo_ref
  6.3 0.6 %copy-done = bf16[128,2048]{1,0:T(8,128)(2,1)S(1)} copy-done((bf16[128,2048]{1,0:T(8,128)(2,1)S(1)}, bf16[128,2048]{1,0:T(8,128)(2,1)}, u32[]{:S(2)}) %copy-start) | copy-done | bytes 524312
  6.9 0.2 copy-done.1
  7.1 0.2 copy-done.2
  7.2 0.0 copy-done.3
  7.2 0.0 copy-start.4
  7.2 0.0 copy-start.5
  7.2 0.0 copy-start.6
  7.2 5.8 %shard_map.82 = (f32[128,2048]{1,0:T(8,128)S(1)}, f32[128,2048]{1,0:T(8,128)S(1)}, f32[16,2048]{1,0:T(8,128)S(1)}) custom-call(bf16[128,2048]{1,0:T(8,128)(2,1)S(1)} %copy-done, bf16[128,2048]{1,0:T(8,128)(2,1)S(1)} %copy-done.1, bf16[128,2048]{1,0:T(8,128)(2,1)S(1)} %copy-done.2, bf16[3,2,2048]{2,1,0:T(2,128)(2,1)S(1)} %collective-permute-done.halo_ref, ...), custom_call_target="tpu_custom_call" | custom-call | flops 21495808 | bytes 3670016 | tf_op jit(solution)/shard_map/pallas_call | solution.py:76
  13.0 4.2 %collective-permute-start.7 = (f32[16,2048]{1,0:T(8,128)S(1)}, f32[16,2048]{1,0:T(8,128)S(1)}, u32[]{:S(2)}, u32[]{:S(2)}) collective-permute-start(f32[16,2048]{1,0:T(8,128)S(1)} %get-tuple-element.17), channel_id=1, source_target_pairs={{0,28},{1,29},{2,30},{3,31}} | collective-permute-start | bytes 393224 | tf_op jit(solution)/shard_map/ppermute | solution.py:14
  17.2 1.9 %collective-permute-start.6 = (f32[16,2048]{1,0:T(8,128)S(1)}, f32[16,2048]{1,0:T(8,128)S(1)}, u32[]{:S(2)}, u32[]{:S(2)}) collective-permute-start(f32[16,2048]{1,0:T(8,128)S(1)} %get-tuple-element.17), channel_id=1, source_target_pairs={{0,24},{4,28},{1,25},{5,29},{2,26},{6,30},{3,27},{7,31}} | collective-permute-start | bytes 393224 | tf_op jit(solution)/shard_map/ppermute | solution.py:14
  19.1 0.0 copy-done.4
  19.1 0.1 convert_element_type.30
  19.2 1.3 %collective-permute-start.5 = (f32[16,2048]{1,0:T(8,128)S(1)}, f32[16,2048]{1,0:T(8,128)S(1)}, u32[]{:S(2)}, u32[]{:S(2)}) collective-permute-start(f32[16,2048]{1,0:T(8,128)S(1)} %get-tuple-element.17), channel_id=1, source_target_pairs={{0,20},{4,24},{8,28},{1,21},{5,25},{9,29},{2,22},{6,26},{10,30},{3... | collective-permute-start | bytes 393224 | tf_op jit(solution)/shard_map/ppermute | solution.py:14
  20.5 1.3 %collective-permute-start.4 = (f32[16,2048]{1,0:T(8,128)S(1)}, f32[16,2048]{1,0:T(8,128)S(1)}, u32[]{:S(2)}, u32[]{:S(2)}) collective-permute-start(f32[16,2048]{1,0:T(8,128)S(1)} %get-tuple-element.17), channel_id=1, source_target_pairs={{0,16},{4,20},{8,24},{12,28},{1,17},{5,21},{9,25},{13,29},{2,18},{... | collective-permute-start | bytes 393224 | tf_op jit(solution)/shard_map/ppermute | solution.py:14
  21.8 1.6 %collective-permute-start.3 = (f32[16,2048]{1,0:T(8,128)S(1)}, f32[16,2048]{1,0:T(8,128)S(1)}, u32[]{:S(2)}, u32[]{:S(2)}) collective-permute-start(f32[16,2048]{1,0:T(8,128)S(1)} %get-tuple-element.17), channel_id=1, source_target_pairs={{0,12},{4,16},{8,20},{12,24},{16,28},{1,13},{5,17},{9,21},{13,25},... | collective-permute-start | bytes 393224 | tf_op jit(solution)/shard_map/ppermute | solution.py:14
  23.4 0.0 collective-permute-done.7
  23.5 2.7 %collective-permute-start.2 = (f32[16,2048]{1,0:T(8,128)S(1)}, f32[16,2048]{1,0:T(8,128)S(1)}, u32[]{:S(2)}, u32[]{:S(2)}) collective-permute-start(f32[16,2048]{1,0:T(8,128)S(1)} %get-tuple-element.17), channel_id=1, source_target_pairs={{0,8},{4,12},{8,16},{12,20},{16,24},{20,28},{1,9},{5,13},{9,17},{1... | collective-permute-start | bytes 393224 | tf_op jit(solution)/shard_map/ppermute | solution.py:14
  26.1 0.0 collective-permute-done.6
  26.2 1.3 %collective-permute-start.1 = (f32[16,2048]{1,0:T(8,128)S(1)}, f32[16,2048]{1,0:T(8,128)S(1)}, u32[]{:S(2)}, u32[]{:S(2)}) collective-permute-start(f32[16,2048]{1,0:T(8,128)S(1)} %get-tuple-element.17), channel_id=1, source_target_pairs={{0,4},{4,8},{8,12},{12,16},{16,20},{20,24},{24,28},{1,5},{5,9},{9,... | collective-permute-start | bytes 393224 | tf_op jit(solution)/shard_map/ppermute | solution.py:14
  27.5 0.0 copy-done.5
  27.5 0.0 copy-done.6
  27.5 9.0 %multiply_reduce_fusion = f32[128,2048]{1,0:T(8,128)S(1)} fusion(f32[16,2048]{1,0:T(8,128)S(1)} %bitcast.159, f32[16,2048]{1,0:T(8,128)S(1)} %bitcast_negate_fusion, f32[128]{0:T(128)S(1)} %iota_convert_fusion, f32[16,2048]{1,0:T(8,128)S(1)} %bitcast.158, f32[128,2048]{1,0:T(8,128)S(1)} %get-tuple-element.18), kind=kOutput, calls=%fused_computation | output fusion | flops 557580288 | bytes 2490880 | tf_op jit(solution)/shard_map/jit(cumsum)/reduce_window_sum | solution.py:120
  36.5 0.0 collective-permute-done.5
  36.5 0.0 collective-permute-done.4
  36.5 0.0 collective-permute-done.3
  36.5 0.0 collective-permute-done.2
  36.5 0.0 collective-permute-done.1
  36.6 0.2 add_multiply_fusion
  36.7 0.3 exponential_multiply_fusion
  37.1 0.2 slice_bitcast_fusion.15
  37.3 0.0 copy-start.7
  37.3 1.6 %multiply_reduce_fusion.1 = (f32[128]{0:T(128)S(1)}, f32[128,2048]{1,0:T(8,128)S(1)}) fusion(f32[128,2048]{1,0:T(8,128)S(1)} %convert_element_type.30, f32[128,2048]{1,0:T(8,128)S(1)} %get-tuple-element.20, f32[8,2048]{1,0:T(8,128)S(1)} %get-tuple-element.48, f32[16,2048]{1,0:T(8,128)S(1)} %get-tuple-element.32, f32[8,2048]{1,0:T(8,128)S(1)} %get-tuple-element.49, ...), kind=kLoop, calls=%fused_computation.29 | loop fusion | flops 9437056 | bytes 7340544 | tf_op jit(solution)/shard_map/reduce_sum | solution.py:140
  39.0 1.6 %collective-permute-start.8 = (f32[128]{0:T(128)S(1)}, f32[128]{0:T(128)S(1)}, u32[]{:S(2)}, u32[]{:S(2)}) collective-permute-start(f32[128]{0:T(128)S(1)} %get-tuple-element.29), channel_id=1, source_target_pairs={{0,1},{1,0},{2,3},{3,2},{4,5},{5,4},{6,7},{7,6},{8,9},{9,8},{10,11... | collective-permute-start | bytes 1544 | tf_op jit(solution)/shard_map/ppermute | solution.py:37
  40.6 2.0 %collective-permute-done.8 = f32[128]{0:T(128)S(1)} collective-permute-done((f32[128]{0:T(128)S(1)}, f32[128]{0:T(128)S(1)}, u32[]{:S(2)}, u32[]{:S(2)}) %collective-permute-start.8) | collective-permute-done | bytes 544 | tf_op jit(solution)/shard_map/ppermute | solution.py:37
  42.6 2.6 %collective-permute-start.9 = (f32[128]{0:T(128)S(1)}, f32[128]{0:T(128)S(1)}, u32[]{:S(2)}, u32[]{:S(2)}) collective-permute-start(f32[128]{0:T(128)S(1)} %add.112), channel_id=1, source_target_pairs={{0,2},{1,3},{2,0},{3,1},{4,6},{5,7},{6,4},{7,5},{8,10},{9,11},{10,... | collective-permute-start | bytes 1544 | tf_op jit(solution)/shard_map/ppermute | solution.py:37
  45.2 1.9 %collective-permute-done.9 = f32[128]{0:T(128)S(1)} collective-permute-done((f32[128]{0:T(128)S(1)}, f32[128]{0:T(128)S(1)}, u32[]{:S(2)}, u32[]{:S(2)}) %collective-permute-start.9) | collective-permute-done | bytes 544 | tf_op jit(solution)/shard_map/ppermute | solution.py:37
  47.1 0.0 copy-done.7
  47.1 1.0 %multiply_convert_fusion = bf16[128,2048]{1,0:T(8,128)(2,1)} fusion(f32[128,2048]{1,0:T(8,128)S(1)} %get-tuple-element.30, f32[2048]{0:T(1024)S(1)} %copy-done.7, f32[128]{0:T(128)S(1)} %add_rsqrt_fusion), kind=kLoop, calls=%fused_computation.28 | loop fusion | flops 786432 | bytes 1581568 | tf_op jit(solution)/shard_map/convert_element_type | solution.py:142
  (6 shorter events, 0.0 us)
Async XLA Ops:
  0.8 5.5 %collective-permute-start = (bf16[3,2,2048]{2,1,0:T(2,128)(2,1)S(1)}, bf16[3,2,2048]{2,1,0:T(2,128)(2,1)S(1)}, u32[]{:S(2)}, u32[]{:S(2)}) collective-permute-start(bf16[3,2,2048]{2,1,0:T(2,128)(2,1)S(1)} %pad_maximum_fusion), channel_id=1, source_target_pairs={{0,4},{4,8},{8,12},{12,16},{16,20},{20,24},{24,28},{1,5},{5,9},{9,... | collective-permute-start | bytes 73736 | tf_op jit(solution)/shard_map/ppermute | solution.py:14
  5.9 1.0 %copy-start = (bf16[128,2048]{1,0:T(8,128)(2,1)S(1)}, bf16[128,2048]{1,0:T(8,128)(2,1)}, u32[]{:S(2)}) copy-start(bf16[128,2048]{1,0:T(8,128)(2,1)} %q_ref.1) | copy-start | bytes 1572868
  5.9 1.2 %copy-start.1 = (bf16[128,2048]{1,0:T(8,128)(2,1)S(1)}, bf16[128,2048]{1,0:T(8,128)(2,1)}, u32[]{:S(2)}) copy-start(bf16[128,2048]{1,0:T(8,128)(2,1)} %k_ref.1) | copy-start | bytes 1572868
  5.9 1.4 %copy-start.2 = (bf16[128,2048]{1,0:T(8,128)(2,1)S(1)}, bf16[128,2048]{1,0:T(8,128)(2,1)}, u32[]{:S(2)}) copy-start(bf16[128,2048]{1,0:T(8,128)(2,1)} %v_ref.1) | copy-start | bytes 1572868
  5.9 1.4 %copy-start.3 = (f32[3,3,2048]{2,1,0:T(4,128)S(1)}, f32[3,3,2048]{2,1,0:T(4,128)}, u32[]{:S(2)}) copy-start(f32[3,3,2048]{2,1,0:T(4,128)} %taps_ref.1) | copy-start | bytes 221188
  7.2 11.9 %copy-start.4 = (bf16[128,2048]{1,0:T(8,128)(2,1)S(1)}, bf16[128,2048]{1,0:T(8,128)(2,1)}, u32[]{:S(2)}) copy-start(bf16[128,2048]{1,0:T(8,128)(2,1)} %param.14) | copy-start | bytes 1572868
  7.2 20.2 %copy-start.5 = (f32[2048,16]{0,1:T(8,128)S(1)}, f32[2048,16]{0,1:T(8,128)}, u32[]{:S(2)}) copy-start(f32[2048,16]{0,1:T(8,128)} %param.12) | copy-start | bytes 393220
  7.2 20.2 %copy-start.6 = (f32[2048,16]{0,1:T(8,128)S(1)}, f32[2048,16]{0,1:T(8,128)}, u32[]{:S(2)}) copy-start(f32[2048,16]{0,1:T(8,128)} %param.13) | copy-start | bytes 393220
  13.0 10.4 %collective-permute-start.7 = (f32[16,2048]{1,0:T(8,128)S(1)}, f32[16,2048]{1,0:T(8,128)S(1)}, u32[]{:S(2)}, u32[]{:S(2)}) collective-permute-start(f32[16,2048]{1,0:T(8,128)S(1)} %get-tuple-element.17), channel_id=1, source_target_pairs={{0,28},{1,29},{2,30},{3,31}} | collective-permute-start | bytes 393224 | tf_op jit(solution)/shard_map/ppermute | solution.py:14
  17.2 8.9 %collective-permute-start.6 = (f32[16,2048]{1,0:T(8,128)S(1)}, f32[16,2048]{1,0:T(8,128)S(1)}, u32[]{:S(2)}, u32[]{:S(2)}) collective-permute-start(f32[16,2048]{1,0:T(8,128)S(1)} %get-tuple-element.17), channel_id=1, source_target_pairs={{0,24},{4,28},{1,25},{5,29},{2,26},{6,30},{3,27},{7,31}} | collective-permute-start | bytes 393224 | tf_op jit(solution)/shard_map/ppermute | solution.py:14
  19.2 17.3 %collective-permute-start.5 = (f32[16,2048]{1,0:T(8,128)S(1)}, f32[16,2048]{1,0:T(8,128)S(1)}, u32[]{:S(2)}, u32[]{:S(2)}) collective-permute-start(f32[16,2048]{1,0:T(8,128)S(1)} %get-tuple-element.17), channel_id=1, source_target_pairs={{0,20},{4,24},{8,28},{1,21},{5,25},{9,29},{2,22},{6,26},{10,30},{3... | collective-permute-start | bytes 393224 | tf_op jit(solution)/shard_map/ppermute | solution.py:14
  20.5 16.0 %collective-permute-start.4 = (f32[16,2048]{1,0:T(8,128)S(1)}, f32[16,2048]{1,0:T(8,128)S(1)}, u32[]{:S(2)}, u32[]{:S(2)}) collective-permute-start(f32[16,2048]{1,0:T(8,128)S(1)} %get-tuple-element.17), channel_id=1, source_target_pairs={{0,16},{4,20},{8,24},{12,28},{1,17},{5,21},{9,25},{13,29},{2,18},{... | collective-permute-start | bytes 393224 | tf_op jit(solution)/shard_map/ppermute | solution.py:14
  21.8 14.7 %collective-permute-start.3 = (f32[16,2048]{1,0:T(8,128)S(1)}, f32[16,2048]{1,0:T(8,128)S(1)}, u32[]{:S(2)}, u32[]{:S(2)}) collective-permute-start(f32[16,2048]{1,0:T(8,128)S(1)} %get-tuple-element.17), channel_id=1, source_target_pairs={{0,12},{4,16},{8,20},{12,24},{16,28},{1,13},{5,17},{9,21},{13,25},... | collective-permute-start | bytes 393224 | tf_op jit(solution)/shard_map/ppermute | solution.py:14
  23.5 13.1 %collective-permute-start.2 = (f32[16,2048]{1,0:T(8,128)S(1)}, f32[16,2048]{1,0:T(8,128)S(1)}, u32[]{:S(2)}, u32[]{:S(2)}) collective-permute-start(f32[16,2048]{1,0:T(8,128)S(1)} %get-tuple-element.17), channel_id=1, source_target_pairs={{0,8},{4,12},{8,16},{12,20},{16,24},{20,28},{1,9},{5,13},{9,17},{1... | collective-permute-start | bytes 393224 | tf_op jit(solution)/shard_map/ppermute | solution.py:14
  26.2 10.4 %collective-permute-start.1 = (f32[16,2048]{1,0:T(8,128)S(1)}, f32[16,2048]{1,0:T(8,128)S(1)}, u32[]{:S(2)}, u32[]{:S(2)}) collective-permute-start(f32[16,2048]{1,0:T(8,128)S(1)} %get-tuple-element.17), channel_id=1, source_target_pairs={{0,4},{4,8},{8,12},{12,16},{16,20},{20,24},{24,28},{1,5},{5,9},{9,... | collective-permute-start | bytes 393224 | tf_op jit(solution)/shard_map/ppermute | solution.py:14
  37.3 9.8 %copy-start.7 = (f32[2048]{0:T(1024)S(1)}, f32[2048]{0:T(1024)}, u32[]{:S(2)}) copy-start(f32[2048]{0:T(1024)} %param.15) | copy-start | bytes 24580
  39.0 3.6 %collective-permute-start.8 = (f32[128]{0:T(128)S(1)}, f32[128]{0:T(128)S(1)}, u32[]{:S(2)}, u32[]{:S(2)}) collective-permute-start(f32[128]{0:T(128)S(1)} %get-tuple-element.29), channel_id=1, source_target_pairs={{0,1},{1,0},{2,3},{3,2},{4,5},{5,4},{6,7},{7,6},{8,9},{9,8},{10,11... | collective-permute-start | bytes 1544 | tf_op jit(solution)/shard_map/ppermute | solution.py:37
  42.6 4.5 %collective-permute-start.9 = (f32[128]{0:T(128)S(1)}, f32[128]{0:T(128)S(1)}, u32[]{:S(2)}, u32[]{:S(2)}) collective-permute-start(f32[128]{0:T(128)S(1)} %add.112), channel_id=1, source_target_pairs={{0,2},{1,3},{2,0},{3,1},{4,6},{5,7},{6,4},{7,5},{8,10},{9,11},{10,... | collective-permute-start | bytes 1544 | tf_op jit(solution)/shard_map/ppermute | solution.py:37

commit v13 on v12

--- a/solution.py
+++ b/solution.py
@@ -39,7 +39,7 @@
     return value
 
 
-def front_kernel(q_ref, k_ref, v_ref, halo_ref, taps_ref, coarse_ref, fine_ref, qf_ref, g_ref, end_ref, pad_ref):
+def front_kernel(q_ref, k_ref, v_ref, halo_ref, taps_ref, decay_ref, qf_ref, g_ref, end_ref, pad_ref):
     rows = q_ref.shape[0]
     lead = pad_ref.shape[1] - rows
     feats = []
@@ -55,23 +55,26 @@
     g_ref[...] = gated
     chunks = rows // 8
 
+    far = (8.0 * (chunks - 1) - 8.0 * lax.broadcasted_iota(jnp.int32, (chunks, 1), 0).astype(jnp.float32))
+    near = 7.0 - lax.broadcasted_iota(jnp.int32, (8, 1), 0).astype(jnp.float32)
+
     def mode(m, carry):
-        weights = coarse_ref[m]
+        rate_row = decay_ref[pl.ds(m, 1), :]
+        weights = jnp.exp(-rate_row * far)
+        fine = jnp.exp(-rate_row * near)
         inner = weights[0:1, :] * gated[0:8, :]
         for u in range(1, chunks):
             inner = inner + weights[u : u + 1, :] * gated[8 * u : 8 * u + 8, :]
-        end_ref[pl.ds(m, 1), :] = jnp.sum(inner * fine_ref[m], axis=0, keepdims=True)
+        end_ref[pl.ds(m, 1), :] = jnp.sum(inner * fine, axis=0, keepdims=True)
         return carry
 
-    lax.fori_loop(0, coarse_ref.shape[0], mode, 0)
+    lax.fori_loop(0, decay_ref.shape[0], mode, 0)
 
 
 def front(q_in, k_in, v_in, before, short_filter, decay):
     rows, width = q_in.shape
     modes = decay.shape[0]
     chunks = rows // 8
-    coarse = jnp.exp(-decay[:, None, :] * (8.0 * (chunks - 1 - jnp.arange(chunks, dtype=jnp.float32)))[None, :, None])
-    fine = jnp.exp(-decay[:, None, :] * (7.0 - jnp.arange(8, dtype=jnp.float32))[None, :, None])
     vmem = pl.BlockSpec(memory_space=pltpu.VMEM)
     return pl.pallas_call(
         front_kernel,
@@ -80,14 +83,14 @@
             jax.ShapeDtypeStruct((rows, width), jnp.float32),
             jax.ShapeDtypeStruct((modes, width), jnp.float32),
         ),
-        in_specs=[vmem] * 7,
+        in_specs=[vmem] * 6,
         out_specs=(vmem, vmem, vmem),
         scratch_shapes=[pltpu.VMEM((3, rows + 8, width), jnp.float32)],
         compiler_params=pltpu.CompilerParams(vmem_limit_bytes=48 * 1024 * 1024),
         cost_estimate=pl.CostEstimate(
             flops=2 * rows * width * (9 + 2 * modes), transcendentals=0, bytes_accessed=rows * width * 14
         ),
-    )(q_in, k_in, v_in, before, short_filter, coarse, fine)
+    )(q_in, k_in, v_in, before, short_filter, decay)
 
 
 def per_device(q_in, k_in, v_in, short_filter, rate, residue, resid, gain):

time: 48.4 us -> 48.7 us (level)
  starting transfers between devices: 20.9 us -> 24.5 us
  other arithmetic: 16 us -> 14.2 us
  local copies, waits for them, and re-layouts: 1.2 us -> 0.35 us
  Pallas kernels: 5.8 us -> 5.08 us
    ppermute x8, starting transfers between devices: 16.6 us -> 20.3 us  [from_behind(): return lax.ppermute(block, axis, route)]
    exp x1 -> x0, other arithmetic: 1.68 us -> none  [front(): jnp.exp(-decay[:, None, :] * (8.0 * (chunks - 1 - jnp.arange(chunks, dtyp...]
    unnamed x16, local copies, waits for them, and re-layouts: 0.9 us -> 0.05 us
    pallas_call x1, Pallas kernels: 5.8 us -> 5.08 us  [front(): pl.pallas_call(front_kernel, out_shape=(jax.ShapeDtypeStruct((rows, width...]
  transfers between devices with their start and end apart: 10 -> 10, of which waited for: 2 -> 2; matrix products, arithmetic and copies ran while one was open for 25% -> 21% of each run, Pallas kernels for 0% -> 0%
where the time goes in v13:
time: 48.7 us; the launch traced here: 48.4 us
  starting transfers between devices  24.5 us (50%)
  other arithmetic  14.2 us (29%)
  Pallas kernels  5.08 us (10%)
  waiting for transfers between devices  3.89 us (8%)
    ppermute x8, starting transfers between devices, from_behind(): return lax.ppermute(block, axis, route)  20.3 us
    another operation x1, other arithmetic, local_part(): running = jnp.cumsum(values[None, :, :] * grow, axis=1) * fade  9.06 us
    pallas_call x1, Pallas kernels, front(): pl.pallas_call(front_kernel, out_shape=(jax.ShapeDtypeStruct((rows, width...  5.08 us
    ppermute x2, starting transfers between devices, butterfly_sum(): lax.ppermute(value, axis, [(i, i ^ step) for i in range(count)])  4.23 us
    ppermute x2, waiting for transfers between devices, butterfly_sum(): lax.ppermute(value, axis, [(i, i ^ step) for i in range(count)])  3.87 us
    reduce_sum x1, other arithmetic, per_device(): squares = butterfly_sum(jnp.sum(stream * stream, axis=1), 'tp')  1.63 us
  transfers between devices with their start and end apart: 10, of which 2 were waited for; matrix products, arithmetic and copies ran while one was open for 21% of the time, Pallas kernels for 0%

profile of v13, /device:TPU:0, one launch (start us, length us, event | category | flops | bytes accessed | tf_op | source)
XLA Modules:
  0.0 48.4 jit_solution(9955239808501501391)
XLA Ops:
  0.0 0.8 %pad_maximum_fusion = bf16[3,2,2048]{2,1,0:T(2,128)(2,1)S(1)} fusion(bf16[1,128,2048]{2,1,0:T(8,128)(2,1)} %bitcast.157, bf16[1,128,2048]{2,1,0:T(8,128)(2,1)} %bitcast.156, bf16[1,128,2048]{2,1,0:T(8,128)(2,1)} %bitcast.155), kind=kLoop, calls=%fused_computation.63 | loop fusion | flops 73728 | bytes 1597440 | tf_op jit(solution)/shard_map/stack | solution.py:99
  0.8 0.0 copy-start
  0.8 0.0 copy-start.1
  0.8 0.0 copy-start.2
  0.9 0.0 copy-start.3
  0.9 0.0 copy-start.4
  0.9 2.5 %collective-permute-start = (bf16[3,2,2048]{2,1,0:T(2,128)(2,1)S(1)}, bf16[3,2,2048]{2,1,0:T(2,128)(2,1)S(1)}, u32[]{:S(2)}, u32[]{:S(2)}) collective-permute-start(bf16[3,2,2048]{2,1,0:T(2,128)(2,1)S(1)} %pad_maximum_fusion), channel_id=1, source_target_pairs={{0,4},{4,8},{8,12},{12,16},{16,20},{20,24},{24,28},{1,5},{5,9},{9,... | collective-permute-start | bytes 73736 | tf_op jit(solution)/shard_map/ppermute | solution.py:14
  3.4 0.9 %bitcast_negate_fusion = f32[16,2048]{1,0:T(8,128)S(1)} fusion(f32[2048,16]{0,1:T(8,128)} %param.12), kind=kLoop, calls=%fused_computation.69 | loop fusion | flops 32768 | bytes 262144 | tf_op jit(solution)/shard_map/neg | solution.py:109
  4.4 0.2 multiply_exponential_fusion
  4.6 0.0 copy-start.5
  4.6 0.1 slice_bitcast_fusion.31
  4.7 0.0 copy-start.6
  4.7 0.0 collective-permute-done.halo_ref
  4.7 0.0 copy-done
  4.7 0.0 copy-done.1
  4.7 0.0 copy-done.2
  4.7 0.0 copy-done.3
  4.7 0.0 copy-done.4
  4.7 5.1 %shard_map.82 = (f32[128,2048]{1,0:T(8,128)S(1)}, f32[128,2048]{1,0:T(8,128)S(1)}, f32[16,2048]{1,0:T(8,128)S(1)}) custom-call(bf16[128,2048]{1,0:T(8,128)(2,1)S(1)} %copy-done, bf16[128,2048]{1,0:T(8,128)(2,1)S(1)} %copy-done.1, bf16[128,2048]{1,0:T(8,128)(2,1)S(1)} %copy-done.2, bf16[3,2,2048]{2,1,0:T(2,128)(2,1)S(1)} %collective-permute-done.halo_ref, ...), custom_call_target="tpu_custom_call" | custom-call | flops 21495808 | bytes 3670016 | tf_op jit(solution)/shard_map/pallas_call | solution.py:79
  9.8 4.5 %collective-permute-start.1 = (f32[16,2048]{1,0:T(8,128)S(1)}, f32[16,2048]{1,0:T(8,128)S(1)}, u32[]{:S(2)}, u32[]{:S(2)}) collective-permute-start(f32[16,2048]{1,0:T(8,128)S(1)} %get-tuple-element.17), channel_id=1, source_target_pairs={{0,4},{4,8},{8,12},{12,16},{16,20},{20,24},{24,28},{1,5},{5,9},{9,... | collective-permute-start | bytes 393224 | tf_op jit(solution)/shard_map/ppermute | solution.py:14
  14.3 3.7 %collective-permute-start.2 = (f32[16,2048]{1,0:T(8,128)S(1)}, f32[16,2048]{1,0:T(8,128)S(1)}, u32[]{:S(2)}, u32[]{:S(2)}) collective-permute-start(f32[16,2048]{1,0:T(8,128)S(1)} %get-tuple-element.17), channel_id=1, source_target_pairs={{0,8},{4,12},{8,16},{12,20},{16,24},{20,28},{1,9},{5,13},{9,17},{1... | collective-permute-start | bytes 393224 | tf_op jit(solution)/shard_map/ppermute | solution.py:14
  18.1 0.0 copy-done.5
  18.1 0.1 convert_element_type.30
  18.2 4.3 %collective-permute-start.3 = (f32[16,2048]{1,0:T(8,128)S(1)}, f32[16,2048]{1,0:T(8,128)S(1)}, u32[]{:S(2)}, u32[]{:S(2)}) collective-permute-start(f32[16,2048]{1,0:T(8,128)S(1)} %get-tuple-element.17), channel_id=1, source_target_pairs={{0,12},{4,16},{8,20},{12,24},{16,28},{1,13},{5,17},{9,21},{13,25},... | collective-permute-start | bytes 393224 | tf_op jit(solution)/shard_map/ppermute | solution.py:14
  22.6 1.3 %collective-permute-start.4 = (f32[16,2048]{1,0:T(8,128)S(1)}, f32[16,2048]{1,0:T(8,128)S(1)}, u32[]{:S(2)}, u32[]{:S(2)}) collective-permute-start(f32[16,2048]{1,0:T(8,128)S(1)} %get-tuple-element.17), channel_id=1, source_target_pairs={{0,16},{4,20},{8,24},{12,28},{1,17},{5,21},{9,25},{13,29},{2,18},{... | collective-permute-start | bytes 393224 | tf_op jit(solution)/shard_map/ppermute | solution.py:14
  23.9 1.3 %collective-permute-start.5 = (f32[16,2048]{1,0:T(8,128)S(1)}, f32[16,2048]{1,0:T(8,128)S(1)}, u32[]{:S(2)}, u32[]{:S(2)}) collective-permute-start(f32[16,2048]{1,0:T(8,128)S(1)} %get-tuple-element.17), channel_id=1, source_target_pairs={{0,20},{4,24},{8,28},{1,21},{5,25},{9,29},{2,22},{6,26},{10,30},{3... | collective-permute-start | bytes 393224 | tf_op jit(solution)/shard_map/ppermute | solution.py:14
  25.2 0.0 collective-permute-done.1
  25.2 1.3 %collective-permute-start.6 = (f32[16,2048]{1,0:T(8,128)S(1)}, f32[16,2048]{1,0:T(8,128)S(1)}, u32[]{:S(2)}, u32[]{:S(2)}) collective-permute-start(f32[16,2048]{1,0:T(8,128)S(1)} %get-tuple-element.17), channel_id=1, source_target_pairs={{0,24},{4,28},{1,25},{5,29},{2,26},{6,30},{3,27},{7,31}} | collective-permute-start | bytes 393224 | tf_op jit(solution)/shard_map/ppermute | solution.py:14
  26.5 0.0 collective-permute-done.2
  26.5 1.3 %collective-permute-start.7 = (f32[16,2048]{1,0:T(8,128)S(1)}, f32[16,2048]{1,0:T(8,128)S(1)}, u32[]{:S(2)}, u32[]{:S(2)}) collective-permute-start(f32[16,2048]{1,0:T(8,128)S(1)} %get-tuple-element.17), channel_id=1, source_target_pairs={{0,28},{1,29},{2,30},{3,31}} | collective-permute-start | bytes 393224 | tf_op jit(solution)/shard_map/ppermute | solution.py:14
  27.8 0.0 copy-done.6
  27.8 9.1 %multiply_reduce_fusion = f32[128,2048]{1,0:T(8,128)S(1)} fusion(f32[16,2048]{1,0:T(8,128)S(1)} %bitcast.160, f32[16,2048]{1,0:T(8,128)S(1)} %bitcast_negate_fusion, f32[128]{0:T(128)S(1)} %iota_convert_fusion, f32[16,2048]{1,0:T(8,128)S(1)} %bitcast.159, f32[128,2048]{1,0:T(8,128)S(1)} %get-tuple-element.18), kind=kOutput, calls=%fused_computation | output fusion | flops 557580288 | bytes 2490880 | tf_op jit(solution)/shard_map/jit(cumsum)/reduce_window_sum | solution.py:123
  36.9 0.0 collective-permute-done.3
  36.9 0.0 collective-permute-done.4
  36.9 0.0 collective-permute-done.5
  36.9 0.0 collective-permute-done.6
  36.9 0.0 collective-permute-done.7
  36.9 0.2 add_multiply_fusion
  37.1 0.3 exponential_multiply_fusion
  37.4 0.2 slice_bitcast_fusion.15
  37.7 0.0 copy-start.7
  37.7 1.6 %multiply_reduce_fusion.1 = (f32[128]{0:T(128)S(1)}, f32[128,2048]{1,0:T(8,128)S(1)}) fusion(f32[128,2048]{1,0:T(8,128)S(1)} %convert_element_type.30, f32[128,2048]{1,0:T(8,128)S(1)} %get-tuple-element.20, f32[8,2048]{1,0:T(8,128)S(1)} %get-tuple-element.48, f32[16,2048]{1,0:T(8,128)S(1)} %get-tuple-element.32, f32[8,2048]{1,0:T(8,128)S(1)} %get-tuple-element.49, ...), kind=kLoop, calls=%fused_computation.28 | loop fusion | flops 9437056 | bytes 7340544 | tf_op jit(solution)/shard_map/reduce_sum | solution.py:143
  39.3 1.6 %collective-permute-start.8 = (f32[128]{0:T(128)S(1)}, f32[128]{0:T(128)S(1)}, u32[]{:S(2)}, u32[]{:S(2)}) collective-permute-start(f32[128]{0:T(128)S(1)} %get-tuple-element.29), channel_id=1, source_target_pairs={{0,1},{1,0},{2,3},{3,2},{4,5},{5,4},{6,7},{7,6},{8,9},{9,8},{10,11... | collective-permute-start | bytes 1544 | tf_op jit(solution)/shard_map/ppermute | solution.py:37
  41.0 2.0 %collective-permute-done.8 = f32[128]{0:T(128)S(1)} collective-permute-done((f32[128]{0:T(128)S(1)}, f32[128]{0:T(128)S(1)}, u32[]{:S(2)}, u32[]{:S(2)}) %collective-permute-start.8) | collective-permute-done | bytes 544 | tf_op jit(solution)/shard_map/ppermute | solution.py:37
  43.0 2.6 %collective-permute-start.9 = (f32[128]{0:T(128)S(1)}, f32[128]{0:T(128)S(1)}, u32[]{:S(2)}, u32[]{:S(2)}) collective-permute-start(f32[128]{0:T(128)S(1)} %add.112), channel_id=1, source_target_pairs={{0,2},{1,3},{2,0},{3,1},{4,6},{5,7},{6,4},{7,5},{8,10},{9,11},{10,... | collective-permute-start | bytes 1544 | tf_op jit(solution)/shard_map/ppermute | solution.py:37
  45.6 1.9 %collective-permute-done.9 = f32[128]{0:T(128)S(1)} collective-permute-done((f32[128]{0:T(128)S(1)}, f32[128]{0:T(128)S(1)}, u32[]{:S(2)}, u32[]{:S(2)}) %collective-permute-start.9) | collective-permute-done | bytes 544 | tf_op jit(solution)/shard_map/ppermute | solution.py:37
  47.4 0.0 copy-done.7
  47.4 1.0 %multiply_convert_fusion = bf16[128,2048]{1,0:T(8,128)(2,1)} fusion(f32[128,2048]{1,0:T(8,128)S(1)} %get-tuple-element.30, f32[2048]{0:T(1024)S(1)} %copy-done.7, f32[128]{0:T(128)S(1)} %add_rsqrt_fusion), kind=kLoop, calls=%fused_computation.27 | loop fusion | flops 786432 | bytes 1581568 | tf_op jit(solution)/shard_map/convert_element_type | solution.py:145
  (5 shorter events, 0.0 us)
Async XLA Ops:
  0.8 3.9 %copy-start = (bf16[128,2048]{1,0:T(8,128)(2,1)S(1)}, bf16[128,2048]{1,0:T(8,128)(2,1)}, u32[]{:S(2)}) copy-start(bf16[128,2048]{1,0:T(8,128)(2,1)} %q_ref.1) | copy-start | bytes 1572868
  0.8 3.9 %copy-start.1 = (bf16[128,2048]{1,0:T(8,128)(2,1)S(1)}, bf16[128,2048]{1,0:T(8,128)(2,1)}, u32[]{:S(2)}) copy-start(bf16[128,2048]{1,0:T(8,128)(2,1)} %k_ref.1) | copy-start | bytes 1572868
  0.8 3.9 %copy-start.2 = (bf16[128,2048]{1,0:T(8,128)(2,1)S(1)}, bf16[128,2048]{1,0:T(8,128)(2,1)}, u32[]{:S(2)}) copy-start(bf16[128,2048]{1,0:T(8,128)(2,1)} %v_ref.1) | copy-start | bytes 1572868
  0.9 3.9 %copy-start.3 = (f32[2048,16]{0,1:T(8,128)S(1)}, f32[2048,16]{0,1:T(8,128)}, u32[]{:S(2)}) copy-start(f32[2048,16]{0,1:T(8,128)} %param.12) | copy-start | bytes 393220
  0.9 3.9 %copy-start.4 = (f32[3,3,2048]{2,1,0:T(4,128)S(1)}, f32[3,3,2048]{2,1,0:T(4,128)}, u32[]{:S(2)}) copy-start(f32[3,3,2048]{2,1,0:T(4,128)} %taps_ref.1) | copy-start | bytes 221188
  0.9 3.8 %collective-permute-start = (bf16[3,2,2048]{2,1,0:T(2,128)(2,1)S(1)}, bf16[3,2,2048]{2,1,0:T(2,128)(2,1)S(1)}, u32[]{:S(2)}, u32[]{:S(2)}) collective-permute-start(bf16[3,2,2048]{2,1,0:T(2,128)(2,1)S(1)} %pad_maximum_fusion), channel_id=1, source_target_pairs={{0,4},{4,8},{8,12},{12,16},{16,20},{20,24},{24,28},{1,5},{5,9},{9,... | collective-permute-start | bytes 73736 | tf_op jit(solution)/shard_map/ppermute | solution.py:14
  4.6 13.5 %copy-start.5 = (bf16[128,2048]{1,0:T(8,128)(2,1)S(1)}, bf16[128,2048]{1,0:T(8,128)(2,1)}, u32[]{:S(2)}) copy-start(bf16[128,2048]{1,0:T(8,128)(2,1)} %param.14) | copy-start | bytes 1572868
  4.7 23.1 %copy-start.6 = (f32[2048,16]{0,1:T(8,128)S(1)}, f32[2048,16]{0,1:T(8,128)}, u32[]{:S(2)}) copy-start(f32[2048,16]{0,1:T(8,128)} %param.13) | copy-start | bytes 393220
  9.8 15.3 %collective-permute-start.1 = (f32[16,2048]{1,0:T(8,128)S(1)}, f32[16,2048]{1,0:T(8,128)S(1)}, u32[]{:S(2)}, u32[]{:S(2)}) collective-permute-start(f32[16,2048]{1,0:T(8,128)S(1)} %get-tuple-element.17), channel_id=1, source_target_pairs={{0,4},{4,8},{8,12},{12,16},{16,20},{20,24},{24,28},{1,5},{5,9},{9,... | collective-permute-start | bytes 393224 | tf_op jit(solution)/shard_map/ppermute | solution.py:14
  14.3 12.1 %collective-permute-start.2 = (f32[16,2048]{1,0:T(8,128)S(1)}, f32[16,2048]{1,0:T(8,128)S(1)}, u32[]{:S(2)}, u32[]{:S(2)}) collective-permute-start(f32[16,2048]{1,0:T(8,128)S(1)} %get-tuple-element.17), channel_id=1, source_target_pairs={{0,8},{4,12},{8,16},{12,20},{16,24},{20,28},{1,9},{5,13},{9,17},{1... | collective-permute-start | bytes 393224 | tf_op jit(solution)/shard_map/ppermute | solution.py:14
  18.2 18.6 %collective-permute-start.3 = (f32[16,2048]{1,0:T(8,128)S(1)}, f32[16,2048]{1,0:T(8,128)S(1)}, u32[]{:S(2)}, u32[]{:S(2)}) collective-permute-start(f32[16,2048]{1,0:T(8,128)S(1)} %get-tuple-element.17), channel_id=1, source_target_pairs={{0,12},{4,16},{8,20},{12,24},{16,28},{1,13},{5,17},{9,21},{13,25},... | collective-permute-start | bytes 393224 | tf_op jit(solution)/shard_map/ppermute | solution.py:14
  22.6 14.3 %collective-permute-start.4 = (f32[16,2048]{1,0:T(8,128)S(1)}, f32[16,2048]{1,0:T(8,128)S(1)}, u32[]{:S(2)}, u32[]{:S(2)}) collective-permute-start(f32[16,2048]{1,0:T(8,128)S(1)} %get-tuple-element.17), channel_id=1, source_target_pairs={{0,16},{4,20},{8,24},{12,28},{1,17},{5,21},{9,25},{13,29},{2,18},{... | collective-permute-start | bytes 393224 | tf_op jit(solution)/shard_map/ppermute | solution.py:14
  23.9 13.0 %collective-permute-start.5 = (f32[16,2048]{1,0:T(8,128)S(1)}, f32[16,2048]{1,0:T(8,128)S(1)}, u32[]{:S(2)}, u32[]{:S(2)}) collective-permute-start(f32[16,2048]{1,0:T(8,128)S(1)} %get-tuple-element.17), channel_id=1, source_target_pairs={{0,20},{4,24},{8,28},{1,21},{5,25},{9,29},{2,22},{6,26},{10,30},{3... | collective-permute-start | bytes 393224 | tf_op jit(solution)/shard_map/ppermute | solution.py:14
  25.2 11.7 %collective-permute-start.6 = (f32[16,2048]{1,0:T(8,128)S(1)}, f32[16,2048]{1,0:T(8,128)S(1)}, u32[]{:S(2)}, u32[]{:S(2)}) collective-permute-start(f32[16,2048]{1,0:T(8,128)S(1)} %get-tuple-element.17), channel_id=1, source_target_pairs={{0,24},{4,28},{1,25},{5,29},{2,26},{6,30},{3,27},{7,31}} | collective-permute-start | bytes 393224 | tf_op jit(solution)/shard_map/ppermute | solution.py:14
  26.5 10.4 %collective-permute-start.7 = (f32[16,2048]{1,0:T(8,128)S(1)}, f32[16,2048]{1,0:T(8,128)S(1)}, u32[]{:S(2)}, u32[]{:S(2)}) collective-permute-start(f32[16,2048]{1,0:T(8,128)S(1)} %get-tuple-element.17), channel_id=1, source_target_pairs={{0,28},{1,29},{2,30},{3,31}} | collective-permute-start | bytes 393224 | tf_op jit(solution)/shard_map/ppermute | solution.py:14
  37.7 9.8 %copy-start.7 = (f32[2048]{0:T(1024)S(1)}, f32[2048]{0:T(1024)}, u32[]{:S(2)}) copy-start(f32[2048]{0:T(1024)} %param.15) | copy-start | bytes 24580
  39.3 3.6 %collective-permute-start.8 = (f32[128]{0:T(128)S(1)}, f32[128]{0:T(128)S(1)}, u32[]{:S(2)}, u32[]{:S(2)}) collective-permute-start(f32[128]{0:T(128)S(1)} %get-tuple-element.29), channel_id=1, source_target_pairs={{0,1},{1,0},{2,3},{3,2},{4,5},{5,4},{6,7},{7,6},{8,9},{9,8},{10,11... | collective-permute-start | bytes 1544 | tf_op jit(solution)/shard_map/ppermute | solution.py:37
  43.0 4.5 %collective-permute-start.9 = (f32[128]{0:T(128)S(1)}, f32[128]{0:T(128)S(1)}, u32[]{:S(2)}, u32[]{:S(2)}) collective-permute-start(f32[128]{0:T(128)S(1)} %add.112), channel_id=1, source_target_pairs={{0,2},{1,3},{2,0},{3,1},{4,6},{5,7},{6,4},{7,5},{8,10},{9,11},{10,... | collective-permute-start | bytes 1544 | tf_op jit(solution)/shard_map/ppermute | solution.py:37
